TPU v7x, 512 devices: a whole 4x4x16 slice. The times are simulated.
512 devices in a mesh: fsdp: 64 (over z, x), sp: 8 (over y, core).
Axes of the slice: x: 4, y: 4, z: 16, core: 2. Of those that a mesh axis runs over, the one named last changes fastest.
Arguments:
- queries: bfloat16 [65536, 2048], P(('fsdp', 'sp')), may hold values from -6.5 to 6.5
- key_rows: bfloat16 [65536, 512], P(('fsdp', 'sp')), may hold values from -6.5 to 6.5
- value_rows: bfloat16 [65536, 512], P(('fsdp', 'sp')), may hold values from -6 to 6
- out_grad: bfloat16 [65536, 2048], P(('fsdp', 'sp')), may hold values from -6 to 6
- doc_lengths: int32 [128], replicated, may hold values from 1 to 16, 512 in all
Outputs:
- attn_out: bfloat16 [65536, 2048], P(('fsdp', 'sp'))
- grad_queries: bfloat16 [65536, 2048], P(('fsdp', 'sp'))
- grad_keys: bfloat16 [65536, 512], P(('fsdp', 'sp'))
- grad_values: bfloat16 [65536, 512], P(('fsdp', 'sp'))
Inputs may be any that keep to these rules, and one draw needn't show every extreme that they name: Document d covers doc_lengths[d] blocks of 128 tokens right after documents 0 to d - 1; the lengths sum to 512 blocks.
All inputs are finite; a program needn't handle non-finite values.
Results may differ from a plain program's by a relative error of at most 0.012.
The roundings to bfloat16 on the way count: a program that leaves them out, or rounds other values in their place, can miss the bound.
Values may be sent and summed in bfloat16 or wider, within the bound.
No kernel may reach another device: no remote copies, remote signals or barrier semaphores. Data moves between devices by JAX's collectives and lax.ppermute only.
A program may use at most 64 MiB of HBM per device.

v0:
```python
import math

import jax
import jax.numpy as jnp
from jax import lax
from jax.sharding import PartitionSpec as P

HD = 128
BLK = 128
MOST_BLK = 16


MASK_FILL = -1e30


def passed_along(value, axis, steps):
    count = lax.axis_size(axis)
    first, last = (max(0, -steps), min(count, count - steps))
    return lax.ppermute(value, axis, [(source, source + steps) for source in range(first, last)])


def for_sending(value):
    return jax.tree.map(lambda a: a.astype(jnp.bfloat16) if a.dtype == jnp.float32 else a, value)


def lifted(row_data):
    return lax.optimization_barrier(row_data).astype(jnp.float32)


def doc_index(doc_lengths, first_place, row_count):
    doc_ends = jnp.cumsum(doc_lengths) * BLK
    places = first_place + jnp.arange(row_count, dtype=jnp.int32)
    labels = jnp.sum((places[:, None] >= doc_ends[None, :]).astype(jnp.int32), axis=1)
    return jnp.where(places < 0, -1, labels)


def widen_heads(row_data, copies):
    tokens_here = row_data.shape[0]
    head_count = row_data.shape[1] // HD
    shaped = row_data.reshape(tokens_here, head_count, 1, HD)
    shaped = jnp.broadcast_to(shaped, (tokens_here, head_count, copies, HD))
    return shaped.reshape(tokens_here, head_count * copies * HD)


def pair_mask(q_label, q_place, k_label, k_place):
    return (q_label[:, None] == k_label[None, :]) & (k_place[None, :] <= q_place[:, None])


def pair_live(q_label, q_place, k_label, k_place):
    return (k_label[-1] >= q_label[0]) & (k_place[0] <= q_place[-1])


def tally(stats_state, q_block, k_block, allowed, score_scale):
    highest, row_total = stats_state
    scores = (
        jnp.einsum("qkgd,skd->kgqs", q_block, k_block, preferred_element_type=jnp.float32)
        * score_scale
    )
    scores = jnp.where(allowed, scores, MASK_FILL)
    new_high = jnp.maximum(highest, jnp.max(scores, axis=-1))
    fading = jnp.exp(highest - new_high)
    weights = jnp.where(allowed, jnp.exp(scores - new_high[..., None]), 0.0)
    row_total = row_total * fading + jnp.sum(weights, axis=-1)
    return (new_high, row_total)


def spread(summed, q_block, k_block, v_block, allowed, log_total, score_scale):
    scores = (
        jnp.einsum("qkgd,skd->kgqs", q_block, k_block, preferred_element_type=jnp.float32)
        * score_scale
    )
    weights = jnp.exp(jnp.where(allowed, scores - log_total[..., None], MASK_FILL))
    update = jnp.einsum(
        "kgqs,skd->qkgd", weights.astype(jnp.bfloat16), v_block, preferred_element_type=jnp.float32
    )
    return summed + update


def backward_pair(
    grad_q, q_block, g_block, k_block, v_block, allowed, log_total, row_delta, score_scale
):
    scores = (
        jnp.einsum("qkgd,skd->kgqs", q_block, k_block, preferred_element_type=jnp.float32)
        * score_scale
    )
    weights = jnp.exp(jnp.where(allowed, scores - log_total[..., None], MASK_FILL))
    dprobs = jnp.einsum("qkgd,skd->kgqs", g_block, v_block, preferred_element_type=jnp.float32)
    dscores = (weights * (dprobs - row_delta[..., None])).astype(jnp.bfloat16)
    grad_q = grad_q + jnp.einsum(
        "kgqs,skd->qkgd", dscores, k_block, preferred_element_type=jnp.float32
    )
    grad_k = jnp.einsum("kgqs,qkgd->skd", dscores, q_block, preferred_element_type=jnp.float32)
    grad_v = jnp.einsum(
        "kgqs,qkgd->skd", weights.astype(jnp.bfloat16), g_block, preferred_element_type=jnp.float32
    )
    return (grad_q, grad_k, grad_v)


def local(queries, key_rows, value_rows, out_grad, doc_lengths):
    seq_width = lax.axis_size("sp")
    tok_dev = queries.shape[0]
    span_rows = tok_dev * seq_width
    heads_q = queries.shape[1] // HD
    heads_k = key_rows.shape[1] // HD
    copies = heads_q // heads_k
    q_seq, k_seq, v_seq, g_seq = (
        lax.all_to_all(queries, "sp", split_axis=1, concat_axis=0, tiled=True),
        lax.all_to_all(
            widen_heads(key_rows, copies), "sp", split_axis=1, concat_axis=0, tiled=True
        ),
        lax.all_to_all(
            widen_heads(value_rows, copies), "sp", split_axis=1, concat_axis=0, tiled=True
        ),
        lax.all_to_all(out_grad, "sp", split_axis=1, concat_axis=0, tiled=True),
    )
    local_q = heads_q // seq_width
    local_k = heads_k * copies // seq_width
    group_size = local_q // local_k
    score_scale = 1.0 / math.sqrt(HD)
    reach_groups = (MOST_BLK * BLK - 1) // span_rows + 1
    block_rows = math.gcd(512, span_rows)
    blocks = span_rows // block_rows
    first_place = lax.axis_index("fsdp") * span_rows
    pieces = [(k_seq, v_seq)]
    for distance in range(1, reach_groups + 1):
        pieces.append(passed_along((k_seq, v_seq), "fsdp", distance))
    piece_blocks = []
    for distance in range(reach_groups + 1):
        k_piece, v_piece = pieces[distance]
        start_place = first_place - distance * span_rows
        labels = doc_index(doc_lengths, start_place, span_rows).reshape(blocks, block_rows)
        places = (start_place + jnp.arange(span_rows, dtype=jnp.int32)).reshape(blocks, block_rows)
        piece_blocks.append(
            (
                k_piece.reshape(blocks, block_rows, local_k, HD),
                v_piece.reshape(blocks, block_rows, local_k, HD),
                labels,
                places,
            )
        )
    q_blocks = q_seq.reshape(blocks, block_rows, local_k, group_size, HD)
    g_blocks = g_seq.reshape(blocks, block_rows, local_k, group_size, HD)
    q_labels = piece_blocks[0][2]
    q_places = piece_blocks[0][3]
    zero_grads = tuple(
        (
            (
                jnp.zeros((blocks, block_rows, local_k, HD), jnp.float32),
                jnp.zeros((blocks, block_rows, local_k, HD), jnp.float32),
            )
            for _ in piece_blocks
        )
    )

    def per_block(grads_acc, q_entry):
        q_block, g_block, q_label, q_place = q_entry
        stats_state = (
            jnp.full((local_k, group_size, block_rows), MASK_FILL, jnp.float32),
            jnp.zeros((local_k, group_size, block_rows), jnp.float32),
        )
        for k_all, v_all, k_labels, k_places in piece_blocks:

            def stats_visit(carried, key_entry):
                k_block, v_block, k_label, k_place = key_entry
                allowed = pair_mask(q_label, q_place, k_label, k_place)
                is_live = pair_live(q_label, q_place, k_label, k_place)
                carried = lax.cond(
                    is_live,
                    lambda held_state: tally(held_state, q_block, k_block, allowed, score_scale),
                    lambda held_state: held_state,
                    carried,
                )
                return (carried, None)

            stats_state, _ = lax.scan(stats_visit, stats_state, (k_all, v_all, k_labels, k_places))
        highest, row_total = stats_state
        log_total = highest + jnp.log(row_total)
        summed = jnp.zeros((block_rows, local_k, group_size, HD), jnp.float32)
        for k_all, v_all, k_labels, k_places in piece_blocks:

            def value_visit(carried, key_entry):
                k_block, v_block, k_label, k_place = key_entry
                allowed = pair_mask(q_label, q_place, k_label, k_place)
                is_live = pair_live(q_label, q_place, k_label, k_place)
                carried = lax.cond(
                    is_live,
                    lambda held_state: spread(
                        held_state, q_block, k_block, v_block, allowed, log_total, score_scale
                    ),
                    lambda held_state: held_state,
                    carried,
                )
                return (carried, None)

            summed, _ = lax.scan(value_visit, summed, (k_all, v_all, k_labels, k_places))
        attn_block = summed.astype(jnp.bfloat16)
        row_delta = jnp.transpose(jnp.sum(lifted(g_block) * lifted(attn_block), axis=-1), (1, 2, 0))
        grad_q = jnp.zeros((block_rows, local_k, group_size, HD), jnp.float32)
        new_acc = []
        for piece_number, (k_all, v_all, k_labels, k_places) in enumerate(piece_blocks):

            def back_visit(carried, key_entry):
                k_block, v_block, k_label, k_place = key_entry
                allowed = pair_mask(q_label, q_place, k_label, k_place)
                is_live = pair_live(q_label, q_place, k_label, k_place)

                def compute_pair(held_state):
                    return backward_pair(
                        held_state,
                        q_block,
                        g_block,
                        k_block,
                        v_block,
                        allowed,
                        log_total,
                        row_delta,
                        score_scale,
                    )

                def skip_pair(held_state):
                    zero_block = jnp.zeros((block_rows, local_k, HD), jnp.float32)
                    return (held_state, zero_block, zero_block)

                carried, grad_k, grad_v = lax.cond(is_live, compute_pair, skip_pair, carried)
                return (carried, (grad_k, grad_v))

            grad_q, (part_k, part_v) = lax.scan(
                back_visit, grad_q, (k_all, v_all, k_labels, k_places)
            )
            new_acc.append(
                (grads_acc[piece_number][0] + part_k, grads_acc[piece_number][1] + part_v)
            )
        dq_block = (grad_q * score_scale).astype(jnp.bfloat16)
        return (tuple(new_acc), (attn_block, dq_block))

    grads_acc, (attn_blocks, dq_blocks) = lax.scan(
        per_block, zero_grads, (q_blocks, g_blocks, q_labels, q_places)
    )
    partials = [
        (grad_k.reshape(span_rows, local_k * HD), grad_v.reshape(span_rows, local_k * HD))
        for grad_k, grad_v in grads_acc
    ]
    key_sum, value_sum = partials[0]
    for distance in range(1, reach_groups + 1):
        back_k, back_v = passed_along(for_sending(partials[distance]), "fsdp", -distance)
        key_sum = key_sum + back_k
        value_sum = value_sum + back_v
    key_back, value_back = (
        lax.all_to_all(
            for_sending(key_sum * score_scale), "sp", split_axis=0, concat_axis=1, tiled=True
        ),
        lax.all_to_all(
            for_sending(value_sum), "sp", split_axis=0, concat_axis=1, tiled=True
        ).astype(value_sum.dtype),
    )
    grad_keys = jnp.sum(key_back.reshape(tok_dev, heads_k, copies, HD), axis=2).reshape(
        tok_dev, heads_k * HD
    )
    grad_values = jnp.sum(value_back.reshape(tok_dev, heads_k, copies, HD), axis=2).reshape(
        tok_dev, heads_k * HD
    )
    attn_seq = attn_blocks.reshape(span_rows, local_q * HD)
    dq_seq = dq_blocks.reshape(span_rows, local_q * HD)
    attn_out, grad_queries = (
        lax.all_to_all(attn_seq, "sp", split_axis=0, concat_axis=1, tiled=True),
        lax.all_to_all(dq_seq, "sp", split_axis=0, concat_axis=1, tiled=True),
    )
    return (
        attn_out,
        grad_queries,
        grad_keys.astype(jnp.bfloat16),
        grad_values.astype(jnp.bfloat16),
    )


def solution(mesh):
    in_specs = (
        P(("fsdp", "sp"), None),
        P(("fsdp", "sp"), None),
        P(("fsdp", "sp"), None),
        P(("fsdp", "sp"), None),
        P(),
    )
    out_specs = (
        P(("fsdp", "sp"), None),
        P(("fsdp", "sp"), None),
        P(("fsdp", "sp"), None),
        P(("fsdp", "sp"), None),
    )
    return jax.shard_map(local, mesh=mesh, in_specs=in_specs, out_specs=out_specs, check_vma=False)
```

profile of v0, /device:TPU:166, one launch (start us, length us, event | category | flops | bytes accessed | tf_op | source)
XLA Modules:
  0.0 480.5 jit_solution(12669491160464902838)
XLA Ops:
  8.2 9.2 %all-to-all-done.1 = bf16[128,8,256]{0,2,1:T(8,128)(2,1)S(1)} async-done(((bf16[128,8,256]{0,2,1:T(8,128)(2,1)}), bf16[128,8,256]{0,2,1:T(8,128)(2,1)S(1)}, u32[]{:S(2)}, u32[]{:S(2)}) %all-to-all-start.1) | async-done | bytes 524320 | tf_op jit(solution)/shard_map/all_to_all | solution.py:108
  22.7 9.4 %all-to-all-done.3 = bf16[128,8,256]{0,2,1:T(8,128)(2,1)S(1)} async-done(((bf16[128,8,256]{0,2,1:T(8,128)(2,1)}), bf16[128,8,256]{0,2,1:T(8,128)(2,1)S(1)}, u32[]{:S(2)}, u32[]{:S(2)}) %all-to-all-start.3) | async-done | bytes 524320 | tf_op jit(solution)/shard_map/all_to_all | solution.py:111
  77.7 9.3 %collective-permute-done.2 = bf16[1024,256]{1,0:T(8,128)(2,1)} collective-permute-done((bf16[1024,256]{1,0:T(8,128)(2,1)S(1)}, bf16[1024,256]{1,0:T(8,128)(2,1)}, u32[]{:S(2)}, u32[]{:S(2)}) %collective-permute-start.2) | collective-permute-done | bytes 524320 | tf_op jit(solution)/shard_map/ppermute | solution.py:19
  99.5 270.2 %while.169 = (s32[]{:T(128)}, f32[2,512,2,128]{3,1,2,0:T(8,128)}, f32[2,512,2,128]{3,1,2,0:T(8,128)}, f32[2,512,2,128]{3,1,2,0:T(8,128)}, f32[2,512,2,128]{3,1,2...) while((s32[]{:T(128)}, f32[2,512,2,128]{3,1,2,0:T(8,128)}, ...), condition=%wide.region_48.49_spmd.clone, body=%wide.region_4.48_spmd.clone.sunk | while | flops 3262918656 | bytes 115478656 | solution.py:236
  100.9 11.4 %while.170 = (s32[]{:T(128)}, f32[2,1,512]{2,0,1:T(2,128)S(1)}, f32[2,1,512]{2,0,1:T(2,128)S(1)}, s32[2,512]{1,0:T(2,128)S(1)}, s32[512]{0:T(512)S(1)}, /*index=...) while((s32[]{:T(128)}, f32[2,1,512]{2,0,1:T(2,128)S(1)}, ...), condition=%wide.region_10.10_spmd, body=%wide.region_5.9_spmd.sunk | while | flops 139200512 | bytes 5574979 | solution.py:175
  112.3 11.4 %while.171 = (s32[]{:T(128)}, f32[2,1,512]{2,0,1:T(2,128)S(1)}, f32[2,1,512]{2,0,1:T(2,128)S(1)}, s32[2,512]{1,0:T(2,128)S(1)}, s32[512]{0:T(512)S(1)}, /*index=...) while((s32[]{:T(128)}, f32[2,1,512]{2,0,1:T(2,128)S(1)}, ...), condition=%wide.region_16.16_spmd, body=%wide.region_11.15_spmd.sunk | while | flops 139200512 | bytes 5574979 | solution.py:175
  123.8 9.4 %while.172 = (s32[]{:T(128)}, f32[2,1,512]{2,0,1:T(2,128)S(1)}, f32[2,1,512]{2,0,1:T(2,128)S(1)}, s32[2,512]{1,0:T(2,128)S(1)}, s32[512]{0:T(512)S(1)}, /*index=...) while((s32[]{:T(128)}, f32[2,1,512]{2,0,1:T(2,128)S(1)}, ...), condition=%wide.region_22.22_spmd, body=%wide.region_17.21_spmd.sunk | while | flops 139200512 | bytes 5575487 | solution.py:175
  134.8 11.2 %while.173 = (s32[]{:T(128)}, f32[512,2,1,128]{0,3,1,2:T(8,128)S(1)}, s32[2,512]{1,0:T(2,128)S(1)}, s32[512]{0:T(512)S(1)}, s32[2,512]{1,0:T(2,128)S(1)}, /*inde...) while((s32[]{:T(128)}, ...), condition=%wide.region_26.26_spmd, body=%wide.region_23.25_spmd.sunk | while | flops 271450112 | bytes 2381103 | solution.py:195
  147.2 11.2 %while.174 = (s32[]{:T(128)}, f32[512,2,1,128]{0,3,1,2:T(8,128)S(1)}, s32[2,512]{1,0:T(2,128)S(1)}, s32[512]{0:T(512)S(1)}, s32[2,512]{1,0:T(2,128)S(1)}, /*inde...) while((s32[]{:T(128)}, ...), condition=%wide.region_30.30_spmd, body=%wide.region_27.29_spmd.sunk | while | flops 271450112 | bytes 2381103 | solution.py:195
  159.7 9.4 %while.175 = (s32[]{:T(128)}, f32[512,2,1,128]{0,3,1,2:T(8,128)S(1)}, s32[2,512]{1,0:T(2,128)S(1)}, s32[512]{0:T(512)S(1)}, s32[2,512]{1,0:T(2,128)S(1)}, /*inde...) while((s32[]{:T(128)}, ...), condition=%wide.region_34.34_spmd, body=%wide.region_31.33_spmd.sunk | while | flops 271450112 | bytes 2381103 | solution.py:195
  171.7 15.7 %while.176 = (s32[]{:T(128)}, f32[512,2,1,128]{0,3,1,2:T(8,128)S(1)}, f32[2,512,2,128]{3,1,2,0:T(8,128)}, f32[2,512,2,128]{3,1,2,0:T(8,128)}, s32[2,512]{1,0:T(2...) while((s32[]{:T(128)}, ...), condition=%wide.region_39.39_spmd, body=%wide.region_36.38_spmd.sunk | while | flops 675676160 | bytes 16016763 | solution.py:227
  192.6 15.7 %while.177 = (s32[]{:T(128)}, f32[512,2,1,128]{0,3,1,2:T(8,128)S(1)}, f32[2,512,2,128]{3,1,2,0:T(8,128)}, f32[2,512,2,128]{3,1,2,0:T(8,128)}, s32[2,512]{1,0:T(2...) while((s32[]{:T(128)}, ...), condition=%wide.region_43.43_spmd, body=%wide.region_40.42_spmd.sunk | while | flops 675676160 | bytes 16016763 | solution.py:227
  213.6 11.6 %while.178 = (s32[]{:T(128)}, f32[512,2,1,128]{0,3,1,2:T(8,128)S(1)}, f32[2,512,2,128]{3,1,2,0:T(8,128)}, f32[2,512,2,128]{3,1,2,0:T(8,128)}, s32[2,512]{1,0:T(2...) while((s32[]{:T(128)}, ...), condition=%wide.region_47.47_spmd, body=%wide.region_44.46_spmd.sunk | while | flops 675676160 | bytes 16017779 | solution.py:227
  231.9 12.9 %while.170 = (s32[]{:T(128)}, f32[2,1,512]{2,0,1:T(2,128)S(1)}, f32[2,1,512]{2,0,1:T(2,128)S(1)}, s32[2,512]{1,0:T(2,128)S(1)}, s32[512]{0:T(512)S(1)}, /*index=...) while((s32[]{:T(128)}, f32[2,1,512]{2,0,1:T(2,128)S(1)}, ...), condition=%wide.region_10.10_spmd, body=%wide.region_5.9_spmd.sunk | while | flops 139200512 | bytes 5574979 | solution.py:175
  244.8 11.4 %while.171 = (s32[]{:T(128)}, f32[2,1,512]{2,0,1:T(2,128)S(1)}, f32[2,1,512]{2,0,1:T(2,128)S(1)}, s32[2,512]{1,0:T(2,128)S(1)}, s32[512]{0:T(512)S(1)}, /*index=...) while((s32[]{:T(128)}, f32[2,1,512]{2,0,1:T(2,128)S(1)}, ...), condition=%wide.region_16.16_spmd, body=%wide.region_11.15_spmd.sunk | while | flops 139200512 | bytes 5574979 | solution.py:175
  256.2 9.4 %while.172 = (s32[]{:T(128)}, f32[2,1,512]{2,0,1:T(2,128)S(1)}, f32[2,1,512]{2,0,1:T(2,128)S(1)}, s32[2,512]{1,0:T(2,128)S(1)}, s32[512]{0:T(512)S(1)}, /*index=...) while((s32[]{:T(128)}, f32[2,1,512]{2,0,1:T(2,128)S(1)}, ...), condition=%wide.region_22.22_spmd, body=%wide.region_17.21_spmd.sunk | while | flops 139200512 | bytes 5575487 | solution.py:175
  267.2 12.4 %while.173 = (s32[]{:T(128)}, f32[512,2,1,128]{0,3,1,2:T(8,128)S(1)}, s32[2,512]{1,0:T(2,128)S(1)}, s32[512]{0:T(512)S(1)}, s32[2,512]{1,0:T(2,128)S(1)}, /*inde...) while((s32[]{:T(128)}, ...), condition=%wide.region_26.26_spmd, body=%wide.region_23.25_spmd.sunk | while | flops 271450112 | bytes 2381103 | solution.py:195
  280.9 11.2 %while.174 = (s32[]{:T(128)}, f32[512,2,1,128]{0,3,1,2:T(8,128)S(1)}, s32[2,512]{1,0:T(2,128)S(1)}, s32[512]{0:T(512)S(1)}, s32[2,512]{1,0:T(2,128)S(1)}, /*inde...) while((s32[]{:T(128)}, ...), condition=%wide.region_30.30_spmd, body=%wide.region_27.29_spmd.sunk | while | flops 271450112 | bytes 2381103 | solution.py:195
  293.4 9.4 %while.175 = (s32[]{:T(128)}, f32[512,2,1,128]{0,3,1,2:T(8,128)S(1)}, s32[2,512]{1,0:T(2,128)S(1)}, s32[512]{0:T(512)S(1)}, s32[2,512]{1,0:T(2,128)S(1)}, /*inde...) while((s32[]{:T(128)}, ...), condition=%wide.region_34.34_spmd, body=%wide.region_31.33_spmd.sunk | while | flops 271450112 | bytes 2381103 | solution.py:195
  305.4 19.3 %while.176 = (s32[]{:T(128)}, f32[512,2,1,128]{0,3,1,2:T(8,128)S(1)}, f32[2,512,2,128]{3,1,2,0:T(8,128)}, f32[2,512,2,128]{3,1,2,0:T(8,128)}, s32[2,512]{1,0:T(2...) while((s32[]{:T(128)}, ...), condition=%wide.region_39.39_spmd, body=%wide.region_36.38_spmd.sunk | while | flops 675676160 | bytes 16016763 | solution.py:227
  330.6 15.7 %while.177 = (s32[]{:T(128)}, f32[512,2,1,128]{0,3,1,2:T(8,128)S(1)}, f32[2,512,2,128]{3,1,2,0:T(8,128)}, f32[2,512,2,128]{3,1,2,0:T(8,128)}, s32[2,512]{1,0:T(2...) while((s32[]{:T(128)}, ...), condition=%wide.region_43.43_spmd, body=%wide.region_40.42_spmd.sunk | while | flops 675676160 | bytes 16016763 | solution.py:227
  352.1 11.6 %while.178 = (s32[]{:T(128)}, f32[512,2,1,128]{0,3,1,2:T(8,128)S(1)}, f32[2,512,2,128]{3,1,2,0:T(8,128)}, f32[2,512,2,128]{3,1,2,0:T(8,128)}, s32[2,512]{1,0:T(2...) while((s32[]{:T(128)}, ...), condition=%wide.region_47.47_spmd, body=%wide.region_44.46_spmd.sunk | while | flops 675676160 | bytes 16017779 | solution.py:227
  402.4 39.3 %collective-permute-done.4 = bf16[1024,256]{1,0:T(8,128)(2,1)} collective-permute-done((bf16[1024,256]{1,0:T(8,128)(2,1)}, bf16[1024,256]{1,0:T(8,128)(2,1)}, u32[]{:S(2)}, u32[]{:S(2)}) %collective-permute-start.4) | collective-permute-done | bytes 524320 | tf_op jit(solution)/shard_map/ppermute | solution.py:19
  449.5 13.3 %collective-permute-done.6 = bf16[1024,256]{1,0:T(8,128)(2,1)} collective-permute-done((bf16[1024,256]{1,0:T(8,128)(2,1)}, bf16[1024,256]{1,0:T(8,128)(2,1)}, u32[]{:S(2)}, u32[]{:S(2)}) %collective-permute-start.6) | collective-permute-done | bytes 524320 | tf_op jit(solution)/shard_map/ppermute | solution.py:19
  (517 shorter events, 340.5 us)
Async XLA Ops:
  0.6 21.2 %copy-start.9 = (bf16[128,2048]{1,0:T(8,128)(2,1)S(1)}, bf16[128,2048]{1,0:T(8,128)(2,1)}, u32[]{:S(2)}) copy-start(bf16[128,2048]{1,0:T(8,128)(2,1)} %param.43) | copy-start | bytes 1572868
  2.6 14.8 %all-to-all-start.1 = ((bf16[128,8,256]{0,2,1:T(8,128)(2,1)}), bf16[128,8,256]{0,2,1:T(8,128)(2,1)S(1)}, u32[]{:S(2)}, u32[]{:S(2)}) async-start(bf16[128,8,256]{0,2,1:T(8,128)(2,1)} %bitcast.159), calls=%async_computation.1 | async-start | bytes 1048576 | tf_op jit(solution)/shard_map/all_to_all | solution.py:108
  7.1 28.5 %copy-start.13 = (s32[128]{0:T(128)S(1)}, s32[128]{0:T(128)}, u32[]{:S(2)}) copy-start(s32[128]{0:T(128)} %param.47) | copy-start | bytes 1540
  7.1 28.6 %copy-start.10 = (bf16[128,2048]{1,0:T(8,128)(2,1)S(1)}, bf16[128,2048]{1,0:T(8,128)(2,1)}, u32[]{:S(2)}) copy-start(bf16[128,2048]{1,0:T(8,128)(2,1)} %param.46) | copy-start | bytes 1572868
  18.3 13.8 %all-to-all-start.3 = ((bf16[128,8,256]{0,2,1:T(8,128)(2,1)}), bf16[128,8,256]{0,2,1:T(8,128)(2,1)S(1)}, u32[]{:S(2)}, u32[]{:S(2)}) async-start(bf16[128,8,256]{0,2,1:T(8,128)(2,1)} %bitcast.164), calls=%async_computation.3 | async-start | bytes 1048576 | tf_op jit(solution)/shard_map/all_to_all | solution.py:111
  32.1 20.5 %all-to-all-start = ((bf16[128,8,256]{2,0,1:T(8,128)(2,1)}), bf16[128,8,256]{2,0,1:T(8,128)(2,1)S(1)}, u32[]{:S(2)}, u32[]{:S(2)}) async-start(bf16[128,8,256]{2,0,1:T(8,128)(2,1)} %bitcast.514), calls=%async_computation | async-start | bytes 1048576 | tf_op jit(solution)/shard_map/all_to_all | solution.py:107
  37.1 37.3 %collective-permute-start = (bf16[1024,256]{1,0:T(8,128)(2,1)S(1)}, bf16[1024,256]{1,0:T(8,128)(2,1)}, u32[]{:S(2)}, u32[]{:S(2)}) collective-permute-start(bf16[1024,256]{1,0:T(8,128)(2,1)S(1)} %bitcast.640), channel_id=1, source_target_pairs={{0,8},{8,16},{16,24},{24,32},{32,40},{40,48},{48,56},{56,64},{64,7... | collective-permute-start | bytes 1572872 | tf_op jit(solution)/shard_map/ppermute | solution.py:19
  40.9 34.8 %collective-permute-start.1 = (bf16[1024,256]{1,0:T(8,128)(2,1)S(1)}, bf16[1024,256]{1,0:T(8,128)(2,1)}, u32[]{:S(2)}, u32[]{:S(2)}) collective-permute-start(bf16[1024,256]{1,0:T(8,128)(2,1)S(1)} %bitcast.641), channel_id=1, source_target_pairs={{0,16},{8,24},{16,32},{24,40},{32,48},{40,56},{48,64},{56,72},{64,... | collective-permute-start | bytes 1572872 | tf_op jit(solution)/shard_map/ppermute | solution.py:19
  45.5 41.6 %collective-permute-start.2 = (bf16[1024,256]{1,0:T(8,128)(2,1)S(1)}, bf16[1024,256]{1,0:T(8,128)(2,1)}, u32[]{:S(2)}, u32[]{:S(2)}) collective-permute-start(bf16[1024,256]{1,0:T(8,128)(2,1)S(1)} %bitcast.638), channel_id=1, source_target_pairs={{0,8},{8,16},{16,24},{24,32},{32,40},{40,48},{48,56},{56,64},{64,7... | collective-permute-start | bytes 1572872 | tf_op jit(solution)/shard_map/ppermute | solution.py:19
  49.2 48.3 %collective-permute-start.3 = (bf16[1024,256]{1,0:T(8,128)(2,1)S(1)}, bf16[1024,256]{1,0:T(8,128)(2,1)}, u32[]{:S(2)}, u32[]{:S(2)}) collective-permute-start(bf16[1024,256]{1,0:T(8,128)(2,1)S(1)} %bitcast.639), channel_id=1, source_target_pairs={{0,16},{8,24},{16,32},{24,40},{32,48},{40,56},{48,64},{56,72},{64,... | collective-permute-start | bytes 1572872 | tf_op jit(solution)/shard_map/ppermute | solution.py:19
  52.7 15.0 %all-to-all-start.2 = ((bf16[128,8,256]{2,0,1:T(8,128)(2,1)}), bf16[128,8,256]{2,0,1:T(8,128)(2,1)S(1)}, u32[]{:S(2)}, u32[]{:S(2)}) async-start(bf16[128,8,256]{2,0,1:T(8,128)(2,1)} %bitcast.513), calls=%async_computation.2 | async-start | bytes 1048576 | tf_op jit(solution)/shard_map/all_to_all | solution.py:114
  99.5 33.7 %copy-start.6 = (bf16[2,512,2,1,128]{4,2,1,0,3:T(2,128)(2,1)}, bf16[2,512,2,1,128]{4,2,1,0,3:T(2,128)(2,1)S(1)}, u32[]{:S(2)}) copy-start(bf16[2,512,2,1,128]{4,2,1,0,3:T(2,128)(2,1)S(1)} %get-tuple-element.3707) | copy-start | bytes 1572868 | tf_op jit(solution)/shard_map/while
  230.5 35.2 %copy-start.6 = (bf16[2,512,2,1,128]{4,2,1,0,3:T(2,128)(2,1)}, bf16[2,512,2,1,128]{4,2,1,0,3:T(2,128)(2,1)S(1)}, u32[]{:S(2)}) copy-start(bf16[2,512,2,1,128]{4,2,1,0,3:T(2,128)(2,1)S(1)} %get-tuple-element.3707) | copy-start | bytes 1572868 | tf_op jit(solution)/shard_map/while
  371.9 17.2 %all-to-all-start.4 = ((bf16[8,128,256]{2,1,0:T(8,128)(2,1)}), bf16[8,128,256]{2,1,0:T(8,128)(2,1)S(1)}, u32[]{:S(2)}, u32[]{:S(2)}) async-start(bf16[8,128,256]{2,1,0:T(8,128)(2,1)} %all_to_all.116), calls=%async_computation.4 | async-start | bytes 1048576 | tf_op jit(solution)/shard_map/all_to_all | solution.py:265
  376.4 7.1 %copy-start.2 = (f32[2,512,2,128]{3,1,2,0:T(8,128)S(1)}, f32[2,512,2,128]{3,1,2,0:T(8,128)}, u32[]{:S(2)}) copy-start(f32[2,512,2,128]{3,1,2,0:T(8,128)} %get-tuple-element.1454) | copy-start | bytes 3145732
  377.9 24.5 %collective-permute-start.5 = (bf16[1024,256]{1,0:T(8,128)(2,1)}, bf16[1024,256]{1,0:T(8,128)(2,1)S(1)}, u32[]{:S(2)}, u32[]{:S(2)}) collective-permute-start(bf16[1024,256]{1,0:T(8,128)(2,1)} %bitcast.511), channel_id=1, source_target_pairs={{16,0},{24,8},{32,16},{40,24},{48,32},{56,40},{64,48},{72,56},{80,... | collective-permute-start | bytes 1572872 | tf_op jit(solution)/shard_map/ppermute | solution.py:19
  383.6 10.3 %copy-start.5 = (f32[2,512,2,128]{3,1,2,0:T(8,128)S(1)}, f32[2,512,2,128]{3,1,2,0:T(8,128)}, u32[]{:S(2)}) copy-start(f32[2,512,2,128]{3,1,2,0:T(8,128)} %get-tuple-element.1458) | copy-start | bytes 3145732
  385.0 56.7 %collective-permute-start.4 = (bf16[1024,256]{1,0:T(8,128)(2,1)}, bf16[1024,256]{1,0:T(8,128)(2,1)}, u32[]{:S(2)}, u32[]{:S(2)}) collective-permute-start(bf16[1024,256]{1,0:T(8,128)(2,1)} %bitcast.512), channel_id=1, source_target_pairs={{8,0},{16,8},{24,16},{32,24},{40,32},{48,40},{56,48},{64,56},{72,6... | collective-permute-start | bytes 1572872 | tf_op jit(solution)/shard_map/ppermute | solution.py:19
  389.1 55.1 %all-to-all-start.5 = ((bf16[8,128,256]{2,1,0:T(8,128)(2,1)}), bf16[8,128,256]{2,1,0:T(8,128)(2,1)}, u32[]{:S(2)}, u32[]{:S(2)}) async-start(bf16[8,128,256]{2,1,0:T(8,128)(2,1)} %all_to_all.120), calls=%async_computation.5 | async-start | bytes 1048576 | tf_op jit(solution)/shard_map/all_to_all | solution.py:266
  395.4 54.1 %collective-permute-start.7 = (bf16[1024,256]{1,0:T(8,128)(2,1)}, bf16[1024,256]{1,0:T(8,128)(2,1)}, u32[]{:S(2)}, u32[]{:S(2)}) collective-permute-start(bf16[1024,256]{1,0:T(8,128)(2,1)} %bitcast.509), channel_id=1, source_target_pairs={{16,0},{24,8},{32,16},{40,24},{48,32},{56,40},{64,48},{72,56},{80,... | collective-permute-start | bytes 1572872 | tf_op jit(solution)/shard_map/ppermute | solution.py:19
  399.7 63.1 %collective-permute-start.6 = (bf16[1024,256]{1,0:T(8,128)(2,1)}, bf16[1024,256]{1,0:T(8,128)(2,1)}, u32[]{:S(2)}, u32[]{:S(2)}) collective-permute-start(bf16[1024,256]{1,0:T(8,128)(2,1)} %bitcast.510), channel_id=1, source_target_pairs={{8,0},{16,8},{24,16},{32,24},{40,32},{48,40},{56,48},{64,56},{72,6... | collective-permute-start | bytes 1572872 | tf_op jit(solution)/shard_map/ppermute | solution.py:19
  402.4 39.3 %copy-start.8 = (bf16[1024,256]{1,0:T(8,128)(2,1)}, bf16[1024,256]{1,0:T(8,128)(2,1)S(1)}, u32[]{:S(2)}) copy-start(bf16[1024,256]{1,0:T(8,128)(2,1)S(1)} %collective-permute-done.5) | copy-start | bytes 1572868
  444.2 20.9 %all-to-all-start.6 = ((bf16[8,128,256]{1,2,0:T(8,128)(2,1)}), bf16[8,128,256]{1,2,0:T(8,128)(2,1)S(1)}, u32[]{:S(2)}, u32[]{:S(2)}) async-start(bf16[8,128,256]{1,2,0:T(8,128)(2,1)} %copy.189), calls=%async_computation.6 | async-start | bytes 1048576 | tf_op jit(solution)/shard_map/all_to_all | solution.py:249
  465.1 14.5 %all-to-all-start.7 = ((bf16[8,128,256]{1,2,0:T(8,128)(2,1)}), bf16[8,128,256]{1,2,0:T(8,128)(2,1)S(1)}, u32[]{:S(2)}, u32[]{:S(2)}) async-start(bf16[8,128,256]{1,2,0:T(8,128)(2,1)} %copy.193), calls=%async_computation.7 | async-start | bytes 1048576 | tf_op jit(solution)/shard_map/all_to_all | solution.py:252
  (10 other events, 37.5 us)
where the time goes:
time: 484 us; the launch traced here: 480 us
  local copies, waits for them, and re-layouts  162 us (33%)
  waiting for transfers between devices  106 us (22%)
  loops' own time  91.7 us (19%)
  starting transfers between devices  61.4 us (13%)
  other arithmetic  33.1 us (7%)
  matrix products  24.6 us (5%)
    slice x144, local copies, waits for them, and re-layouts, pair_live(): return (k_label[-1] >= q_label[0]) & (k_place[0] <= q_place[-1])  83.6 us
    ppermute x8, waiting for transfers between devices, passed_along(): lax.ppermute(value, axis, [(source, source + steps) for source in range(f...  76 us
    another operation x6, loops' own time, per_block(): lax.scan(stats_visit, stats_state, (k_all, v_all, k_labels, k_places))  30.2 us
    another operation x6, loops' own time, per_block(): lax.scan(value_visit, summed, (k_all, v_all, k_labels, k_places))  30.2 us
    another operation x6, loops' own time, per_block(): lax.scan(back_visit, grad_q, (k_all, v_all, k_labels, k_places))  29.7 us
    ppermute x8, starting transfers between devices, passed_along(): lax.ppermute(value, axis, [(source, source + steps) for source in range(f...  27.3 us
    add x6, other arithmetic, per_block(): grads_acc[piece_number][1] + part_v  20.6 us
    while x28, local copies, waits for them, and re-layouts  14.4 us
  transfers between devices with their start and end apart: 16, of which 9 were waited for; matrix products, arithmetic and copies ran while one was open for 6% of the time, Pallas kernels for 0%

commit v1 on v0

v1 whole, which is shorter than its diff:
```python
import math

import jax
import jax.numpy as jnp
from jax import lax
from jax.sharding import PartitionSpec as P

HD = 128
BLK = 128
MOST_BLK = 16
Q_ROWS = 256


MASK_FILL = -1e30


def passed_along(value, axis, steps):
    count = lax.axis_size(axis)
    first, last = (max(0, -steps), min(count, count - steps))
    return lax.ppermute(value, axis, [(source, source + steps) for source in range(first, last)])


def lifted(row_data):
    return lax.optimization_barrier(row_data).astype(jnp.float32)


def doc_index(doc_lengths, first_place, row_count):
    doc_ends = jnp.cumsum(doc_lengths) * BLK
    places = first_place + jnp.arange(row_count, dtype=jnp.int32)
    labels = jnp.sum((places[:, None] >= doc_ends[None, :]).astype(jnp.int32), axis=1)
    return jnp.where(places < 0, -1, labels)


def widen_heads(row_data, copies):
    tokens_here = row_data.shape[0]
    head_count = row_data.shape[1] // HD
    shaped = row_data.reshape(tokens_here, head_count, 1, HD)
    shaped = jnp.broadcast_to(shaped, (tokens_here, head_count, copies, HD))
    return shaped.reshape(tokens_here, head_count * copies * HD)


def block_pass(q_block, g_block, k_win, v_win, allowed, score_scale):
    scores = (
        jnp.einsum("qhd,kd->hqk", q_block, k_win, preferred_element_type=jnp.float32)
        * score_scale
    )
    scores = jnp.where(allowed[None], scores, MASK_FILL)
    highest = jnp.max(scores, axis=-1, keepdims=True)
    row_total = jnp.sum(jnp.exp(scores - highest), axis=-1, keepdims=True)
    log_total = highest + jnp.log(row_total)
    weights = jnp.exp(scores - log_total)
    probs_bf = weights.astype(jnp.bfloat16)
    attn_block = jnp.einsum(
        "hqk,kd->qhd", probs_bf, v_win, preferred_element_type=jnp.float32
    ).astype(jnp.bfloat16)
    row_delta = jnp.transpose(jnp.sum(lifted(g_block) * lifted(attn_block), axis=-1), (1, 0))
    dprobs = jnp.einsum("qhd,kd->hqk", g_block, v_win, preferred_element_type=jnp.float32)
    dscores = (weights * (dprobs - row_delta[..., None])).astype(jnp.bfloat16)
    dq_block = (
        jnp.einsum("hqk,kd->qhd", dscores, k_win, preferred_element_type=jnp.float32)
        * score_scale
    ).astype(jnp.bfloat16)
    grad_k = jnp.einsum("hqk,qhd->kd", dscores, q_block, preferred_element_type=jnp.float32)
    grad_v = jnp.einsum("hqk,qhd->kd", probs_bf, g_block, preferred_element_type=jnp.float32)
    return attn_block, dq_block, grad_k, grad_v


def local(queries, key_rows, value_rows, out_grad, doc_lengths):
    seq_width = lax.axis_size("sp")
    tok_dev = queries.shape[0]
    span_rows = tok_dev * seq_width
    heads_q = queries.shape[1] // HD
    heads_k = key_rows.shape[1] // HD
    local_q = heads_q // seq_width
    copies = seq_width // heads_k
    score_scale = 1.0 / math.sqrt(HD)
    q_seq, g_seq = (
        lax.all_to_all(queries, "sp", split_axis=1, concat_axis=0, tiled=True),
        lax.all_to_all(out_grad, "sp", split_axis=1, concat_axis=0, tiled=True),
    )
    k_seq, v_seq = (
        lax.all_to_all(
            widen_heads(key_rows, copies), "sp", split_axis=1, concat_axis=0, tiled=True
        ),
        lax.all_to_all(
            widen_heads(value_rows, copies), "sp", split_axis=1, concat_axis=0, tiled=True
        ),
    )
    reach = MOST_BLK * BLK
    reach_groups = (reach - 1) // span_rows + 1
    first_place = lax.axis_index("fsdp") * span_rows
    earlier = [passed_along((k_seq, v_seq), "fsdp", d) for d in range(reach_groups, 0, -1)]
    k_all = jnp.concatenate([piece[0] for piece in earlier] + [k_seq], axis=0)
    v_all = jnp.concatenate([piece[1] for piece in earlier] + [v_seq], axis=0)
    base_place = first_place - reach_groups * span_rows
    key_count = (reach_groups + 1) * span_rows
    labels = doc_index(doc_lengths, base_place, key_count)
    places = base_place + jnp.arange(key_count, dtype=jnp.int32)
    window = reach + Q_ROWS
    own_start = reach_groups * span_rows
    grad_k_all = jnp.zeros((key_count, HD), jnp.float32)
    grad_v_all = jnp.zeros((key_count, HD), jnp.float32)
    attn_parts, dq_parts = [], []
    for block in range(span_rows // Q_ROWS):
        q_lo = block * Q_ROWS
        k_lo = own_start + q_lo + Q_ROWS - window
        q_label = labels[own_start + q_lo : own_start + q_lo + Q_ROWS]
        q_place = places[own_start + q_lo : own_start + q_lo + Q_ROWS]
        k_label = labels[k_lo : k_lo + window]
        k_place = places[k_lo : k_lo + window]
        allowed = (q_label[:, None] == k_label[None, :]) & (k_place[None, :] <= q_place[:, None])
        q_block = q_seq[q_lo : q_lo + Q_ROWS].reshape(Q_ROWS, local_q, HD)
        g_block = g_seq[q_lo : q_lo + Q_ROWS].reshape(Q_ROWS, local_q, HD)
        attn_block, dq_block, grad_k, grad_v = block_pass(
            q_block,
            g_block,
            k_all[k_lo : k_lo + window],
            v_all[k_lo : k_lo + window],
            allowed,
            score_scale,
        )
        attn_parts.append(attn_block.reshape(Q_ROWS, local_q * HD))
        dq_parts.append(dq_block.reshape(Q_ROWS, local_q * HD))
        grad_k_all = grad_k_all.at[k_lo : k_lo + window].add(grad_k)
        grad_v_all = grad_v_all.at[k_lo : k_lo + window].add(grad_v)
    key_sum = grad_k_all[own_start:]
    value_sum = grad_v_all[own_start:]
    for distance in range(1, reach_groups + 1):
        lo = (reach_groups - distance) * span_rows
        back_k, back_v = passed_along(
            (
                grad_k_all[lo : lo + span_rows].astype(jnp.bfloat16),
                grad_v_all[lo : lo + span_rows].astype(jnp.bfloat16),
            ),
            "fsdp",
            -distance,
        )
        key_sum = key_sum + back_k
        value_sum = value_sum + back_v
    key_back, value_back = (
        lax.all_to_all(
            (key_sum * score_scale).astype(jnp.bfloat16),
            "sp",
            split_axis=0,
            concat_axis=1,
            tiled=True,
        ),
        lax.all_to_all(
            value_sum.astype(jnp.bfloat16), "sp", split_axis=0, concat_axis=1, tiled=True
        ),
    )
    grad_keys = jnp.sum(
        key_back.astype(jnp.float32).reshape(tok_dev, heads_k, copies, HD), axis=2
    ).reshape(tok_dev, heads_k * HD)
    grad_values = jnp.sum(
        value_back.astype(jnp.float32).reshape(tok_dev, heads_k, copies, HD), axis=2
    ).reshape(tok_dev, heads_k * HD)
    attn_seq = jnp.concatenate(attn_parts, axis=0)
    dq_seq = jnp.concatenate(dq_parts, axis=0)
    attn_out, grad_queries = (
        lax.all_to_all(attn_seq, "sp", split_axis=0, concat_axis=1, tiled=True),
        lax.all_to_all(dq_seq, "sp", split_axis=0, concat_axis=1, tiled=True),
    )
    return (
        attn_out,
        grad_queries,
        grad_keys.astype(jnp.bfloat16),
        grad_values.astype(jnp.bfloat16),
    )


def solution(mesh):
    in_specs = (
        P(("fsdp", "sp"), None),
        P(("fsdp", "sp"), None),
        P(("fsdp", "sp"), None),
        P(("fsdp", "sp"), None),
        P(),
    )
    out_specs = (
        P(("fsdp", "sp"), None),
        P(("fsdp", "sp"), None),
        P(("fsdp", "sp"), None),
        P(("fsdp", "sp"), None),
    )
    return jax.shard_map(local, mesh=mesh, in_specs=in_specs, out_specs=out_specs, check_vma=False)
```

time: 484 us -> 156 us (0.32)
  the two profiles are of different devices: /device:TPU:166 before, /device:TPU:230 now
where the time goes in v1:
time: 156 us; the launch traced here: 155 us
  starting transfers between devices  62.3 us (40%)
  local copies, waits for them, and re-layouts  30.9 us (20%)
  waiting for transfers between devices  22.4 us (14%)
  matrix products  22 us (14%)
  other arithmetic  15.9 us (10%)
    ppermute x8, starting transfers between devices, passed_along(): lax.ppermute(value, axis, [(source, source + steps) for source in range(f...  29 us
    unnamed x53, local copies, waits for them, and re-layouts  9.55 us
    ppermute x8, waiting for transfers between devices, passed_along(): lax.ppermute(value, axis, [(source, source + steps) for source in range(f...  7.93 us
    and x2, other arithmetic, local(): (q_label[:, None] == k_label[None, :]) & (k_place[None, :] <= q_place[:,...  6.08 us
    reshape x4, local copies, waits for them, and re-layouts, local(): q_block = q_seq[q_lo:q_lo + Q_ROWS].reshape(Q_ROWS, local_q, HD)  4.87 us
    dot_general x4, matrix products, block_pass(): jnp.einsum('qhd,kd->hqk', g_block, v_win, preferred_element_type=jnp.floa...  4.84 us
    all_to_all x1, starting transfers between devices, local(): lax.all_to_all(dq_seq, 'sp', split_axis=0, concat_axis=1, tiled=True)  4.82 us
    all_to_all x1, starting transfers between devices, local(): lax.all_to_all(out_grad, 'sp', split_axis=1, concat_axis=0, tiled=True)  4.68 us
  transfers between devices with their start and end apart: 16, of which 8 were waited for; matrix products, arithmetic and copies ran while one was open for 36% of the time, Pallas kernels for 0%

profile of v1, /device:TPU:230, one launch (start us, length us, event | category | flops | bytes accessed | tf_op | source)
XLA Modules:
  0.0 155.0 jit_solution(3936405891178311095)
XLA Ops:
  2.3 4.6 %all-to-all-start.1 = ((bf16[128,8,128]{2,0,1:T(8,128)(2,1)}), bf16[128,8,128]{2,0,1:T(8,128)(2,1)S(1)}, u32[]{:S(2)}, u32[]{:S(2)}) async-start(bf16[128,8,128]{2,0,1:T(8,128)(2,1)} %bitcast.5), calls=%async_computation.1 | async-start | bytes 524288 | tf_op jit(solution)/shard_map/all_to_all | solution.py:82
  10.9 3.5 %all-to-all-done.1 = bf16[128,8,128]{2,0,1:T(8,128)(2,1)S(1)} async-done(((bf16[128,8,128]{2,0,1:T(8,128)(2,1)}), bf16[128,8,128]{2,0,1:T(8,128)(2,1)S(1)}, u32[]{:S(2)}, u32[]{:S(2)}) %all-to-all-start.1) | async-done | bytes 262176 | tf_op jit(solution)/shard_map/all_to_all | solution.py:82
  15.2 3.4 %all-to-all-start = ((bf16[128,8,128]{0,2,1:T(8,128)(2,1)}), bf16[128,8,128]{0,2,1:T(8,128)(2,1)S(1)}, u32[]{:S(2)}, u32[]{:S(2)}) async-start(bf16[128,8,128]{0,2,1:T(8,128)(2,1)} %bitcast.1), calls=%async_computation | async-start | bytes 524288 | tf_op jit(solution)/shard_map/all_to_all | solution.py:85
  18.6 2.2 %compare_and_fusion.2 = (pred[256,2304]{0,1:T(8,128)(4,1)S(1)}, pred[256,2304]{0,1:T(8,128)(4,1)S(1)}) fusion(s32[256]{0:T(256)S(1)} %get-tuple-element.130, s32[256]{0:T(256)S(1)} %get-tuple-element.127, s32[2304]{0:T(1024)S(1)} %get-tuple-element.123, s32[2304]{0:T(1024)S(1)} %get-tuple-element.119, s32[256]{0:T(256)S(1)} %get-tuple-element.128, ...), kind=kLoop, calls=%fused_computation.60 | loop fusion | flops 3538944 | bytes 1220608 | tf_op jit(solution)/shard_map/and | solution.py:111
  22.7 3.4 %all-to-all-done = bf16[128,8,128]{0,2,1:T(8,128)(2,1)S(1)} async-done(((bf16[128,8,128]{0,2,1:T(8,128)(2,1)}), bf16[128,8,128]{0,2,1:T(8,128)(2,1)S(1)}, u32[]{:S(2)}, u32[]{:S(2)}) %all-to-all-start) | async-done | bytes 262176 | tf_op jit(solution)/shard_map/all_to_all | solution.py:85
  26.1 3.5 %all-to-all-start.2 = ((bf16[128,8,256]{2,0,1:T(8,128)(2,1)}), bf16[128,8,256]{2,0,1:T(8,128)(2,1)S(1)}, u32[]{:S(2)}, u32[]{:S(2)}) async-start(bf16[128,8,256]{2,0,1:T(8,128)(2,1)} %bitcast.232), calls=%async_computation.2 | async-start | bytes 1048576 | tf_op jit(solution)/shard_map/all_to_all | solution.py:78
  29.6 3.8 %compare_and_fusion = (pred[256,2304]{0,1:T(8,128)(4,1)S(1)}, pred[256,2304]{0,1:T(8,128)(4,1)}) fusion(s32[256]{0:T(256)S(1)} %get-tuple-element.131, s32[256]{0:T(256)S(1)} %get-tuple-element.125, s32[2304]{0:T(1024)S(1)} %get-tuple-element.121, s32[2304]{0:T(1024)S(1)} %get-tuple-element.117, s32[256]{0:T(256)S(1)} %get-tuple-element.129, ...), kind=kLoop, calls=%fused_computation.58 | loop fusion | flops 3538944 | bytes 1220608 | tf_op jit(solution)/shard_map/and | solution.py:111
  33.4 5.9 %collective-permute-start.2 = (bf16[1024,128]{1,0:T(8,128)(2,1)S(1)}, bf16[1024,128]{1,0:T(8,128)(2,1)}, u32[]{:S(2)}, u32[]{:S(2)}) collective-permute-start(bf16[1024,128]{1,0:T(8,128)(2,1)S(1)} %bitcast.246), channel_id=1, source_target_pairs={{0,16},{8,24},{16,32},{24,40},{32,48},{40,56},{48,64},{56,72},{64,... | collective-permute-start | bytes 786440 | tf_op jit(solution)/shard_map/ppermute | solution.py:20
  39.3 4.0 %collective-permute-start.3 = (bf16[1024,128]{1,0:T(8,128)(2,1)S(1)}, bf16[1024,128]{1,0:T(8,128)(2,1)}, u32[]{:S(2)}, u32[]{:S(2)}) collective-permute-start(bf16[1024,128]{1,0:T(8,128)(2,1)S(1)} %bitcast.247), channel_id=1, source_target_pairs={{0,8},{8,16},{16,24},{24,32},{32,40},{40,48},{48,56},{56,64},{64,7... | collective-permute-start | bytes 786440 | tf_op jit(solution)/shard_map/ppermute | solution.py:20
  43.3 4.7 %all-to-all-start.4 = ((bf16[128,8,256]{0,2,1:T(8,128)(2,1)}), bf16[128,8,256]{0,2,1:T(8,128)(2,1)S(1)}, u32[]{:S(2)}, u32[]{:S(2)}) async-start(bf16[128,8,256]{0,2,1:T(8,128)(2,1)} %bitcast.34), calls=%async_computation.4 | async-start | bytes 1048576 | tf_op jit(solution)/shard_map/all_to_all | solution.py:79
  48.7 2.3 %collective-permute-start = (bf16[1024,128]{0,1:T(8,128)(2,1)}, bf16[1024,128]{0,1:T(8,128)(2,1)}, u32[]{:S(2)}, u32[]{:S(2)}) collective-permute-start(bf16[1024,128]{0,1:T(8,128)(2,1)} %copy_bitcast_fusion.1), channel_id=1, source_target_pairs={{0,16},{8,24},{16,32},{24,40},{32,48},{40,56},{48,64},{56,72},{64,... | collective-permute-start | bytes 786440 | tf_op jit(solution)/shard_map/ppermute | solution.py:20
  51.0 4.8 %collective-permute-start.1 = (bf16[1024,128]{0,1:T(8,128)(2,1)}, bf16[1024,128]{0,1:T(8,128)(2,1)}, u32[]{:S(2)}, u32[]{:S(2)}) collective-permute-start(bf16[1024,128]{0,1:T(8,128)(2,1)} %copy_bitcast_fusion.1), channel_id=1, source_target_pairs={{0,8},{8,16},{16,24},{24,32},{32,40},{40,48},{48,56},{56,64},{64,7... | collective-permute-start | bytes 786440 | tf_op jit(solution)/shard_map/ppermute | solution.py:20
  85.7 2.3 %collective-permute-start.7 = (bf16[1024,128]{1,0:T(8,128)(2,1)}, bf16[1024,128]{1,0:T(8,128)(2,1)}, u32[]{:S(2)}, u32[]{:S(2)}) collective-permute-start(bf16[1024,128]{1,0:T(8,128)(2,1)} %slice.408), channel_id=1, source_target_pairs={{16,0},{24,8},{32,16},{40,24},{48,32},{56,40},{64,48},{72,56},{80,... | collective-permute-start | bytes 786440 | tf_op jit(solution)/shard_map/ppermute | solution.py:20
  88.0 3.3 %collective-permute-start.6 = (bf16[1024,128]{1,0:T(8,128)(2,1)}, bf16[1024,128]{1,0:T(8,128)(2,1)}, u32[]{:S(2)}, u32[]{:S(2)}) collective-permute-start(bf16[1024,128]{1,0:T(8,128)(2,1)} %slice.409), channel_id=1, source_target_pairs={{8,0},{16,8},{24,16},{32,24},{40,32},{48,40},{56,48},{64,56},{72,6... | collective-permute-start | bytes 786440 | tf_op jit(solution)/shard_map/ppermute | solution.py:20
  100.0 4.8 %all-to-all-start.5 = ((bf16[8,128,256]{2,1,0:T(8,128)(2,1)}), bf16[8,128,256]{2,1,0:T(8,128)(2,1)S(1)}, u32[]{:S(2)}, u32[]{:S(2)}) async-start(bf16[8,128,256]{2,1,0:T(8,128)(2,1)} %bitcast.58), calls=%async_computation.5 | async-start | bytes 1048576 | tf_op jit(solution)/shard_map/all_to_all | solution.py:162
  104.8 2.1 %fusion.28 = f32[2304,128]{1,0:T(8,128)S(1)} fusion(bf16[2,256,2304]{1,2,0:T(8,128)(2,1)S(1)} %fusion.19, f32[3072,128]{1,0:T(8,128)} %copy-done.1, bf16[256,2,128]{2,1,0:T(2,128)(2,1)S(1)} %copy-done.13), kind=kOutput, calls=%fused_computation.52 | convolution fusion | flops 302284800 | bytes 4849664 | tf_op jit(solution)/shard_map/hqk,qhd->kd/dot_general | solution.py:63
  111.6 3.5 %all-to-all-done.5 = bf16[8,128,256]{2,1,0:T(8,128)(2,1)S(1)} async-done(((bf16[8,128,256]{2,1,0:T(8,128)(2,1)}), bf16[8,128,256]{2,1,0:T(8,128)(2,1)S(1)}, u32[]{:S(2)}, u32[]{:S(2)}) %all-to-all-start.5) | async-done | bytes 524320 | tf_op jit(solution)/shard_map/all_to_all | solution.py:162
  115.1 4.2 %all-to-all-start.3 = ((bf16[8,128,256]{2,1,0:T(8,128)(2,1)}), bf16[8,128,256]{2,1,0:T(8,128)(2,1)}, u32[]{:S(2)}, u32[]{:S(2)}) async-start(bf16[8,128,256]{2,1,0:T(8,128)(2,1)} %bitcast.234), calls=%async_computation.3 | async-start | bytes 1048576 | tf_op jit(solution)/shard_map/all_to_all | solution.py:161
  120.1 4.0 %collective-permute-start.5 = (bf16[1024,128]{1,0:T(8,128)(2,1)}, bf16[1024,128]{1,0:T(8,128)(2,1)S(1)}, u32[]{:S(2)}, u32[]{:S(2)}) collective-permute-start(bf16[1024,128]{1,0:T(8,128)(2,1)} %slice.410), channel_id=1, source_target_pairs={{16,0},{24,8},{32,16},{40,24},{48,32},{56,40},{64,48},{72,56},{80,... | collective-permute-start | bytes 786440 | tf_op jit(solution)/shard_map/ppermute | solution.py:20
  124.1 2.5 %collective-permute-start.4 = (bf16[1024,128]{1,0:T(8,128)(2,1)}, bf16[1024,128]{1,0:T(8,128)(2,1)S(1)}, u32[]{:S(2)}, u32[]{:S(2)}) collective-permute-start(bf16[1024,128]{1,0:T(8,128)(2,1)} %slice.411), channel_id=1, source_target_pairs={{8,0},{16,8},{24,16},{32,24},{40,32},{48,40},{56,48},{64,56},{72,6... | collective-permute-start | bytes 786440 | tf_op jit(solution)/shard_map/ppermute | solution.py:20
  129.6 3.6 %all-to-all-start.7 = ((bf16[8,128,128]{2,1,0:T(8,128)(2,1)}), bf16[8,128,128]{2,1,0:T(8,128)(2,1)S(1)}, u32[]{:S(2)}, u32[]{:S(2)}) async-start(bf16[8,128,128]{2,1,0:T(8,128)(2,1)} %bitcast.73), calls=%async_computation.7 | async-start | bytes 524288 | tf_op jit(solution)/shard_map/all_to_all | solution.py:148
  134.5 6.7 %collective-permute-done.4 = bf16[1024,128]{1,0:T(8,128)(2,1)S(1)} collective-permute-done((bf16[1024,128]{1,0:T(8,128)(2,1)}, bf16[1024,128]{1,0:T(8,128)(2,1)S(1)}, u32[]{:S(2)}, u32[]{:S(2)}) %collective-permute-start.4) | collective-permute-done | bytes 262176 | tf_op jit(solution)/shard_map/ppermute | solution.py:20
  142.0 4.5 %all-to-all-start.6 = ((bf16[8,128,128]{2,1,0:T(8,128)(2,1)}), bf16[8,128,128]{2,1,0:T(8,128)(2,1)S(1)}, u32[]{:S(2)}, u32[]{:S(2)}) async-start(bf16[8,128,128]{2,1,0:T(8,128)(2,1)} %bitcast.65), calls=%async_computation.6 | async-start | bytes 524288 | tf_op jit(solution)/shard_map/all_to_all | solution.py:141
  151.0 3.0 %all-to-all-done.6 = bf16[8,128,128]{2,1,0:T(8,128)(2,1)S(1)} async-done(((bf16[8,128,128]{2,1,0:T(8,128)(2,1)}), bf16[8,128,128]{2,1,0:T(8,128)(2,1)S(1)}, u32[]{:S(2)}, u32[]{:S(2)}) %all-to-all-start.6) | async-done | bytes 262176 | tf_op jit(solution)/shard_map/all_to_all | solution.py:141
  (151 shorter events, 63.0 us)
Async XLA Ops:
  0.6 20.2 %copy-start.19 = (bf16[128,2048]{1,0:T(8,128)(2,1)S(1)}, bf16[128,2048]{1,0:T(8,128)(2,1)}, u32[]{:S(2)}) copy-start(bf16[128,2048]{1,0:T(8,128)(2,1)} %param.21) | copy-start | bytes 1572868
  2.3 19.4 %copy-start.20 = (bf16[128,2048]{1,0:T(8,128)(2,1)S(1)}, bf16[128,2048]{1,0:T(8,128)(2,1)}, u32[]{:S(2)}) copy-start(bf16[128,2048]{1,0:T(8,128)(2,1)} %param.24) | copy-start | bytes 1572868
  2.3 12.1 %all-to-all-start.1 = ((bf16[128,8,128]{2,0,1:T(8,128)(2,1)}), bf16[128,8,128]{2,0,1:T(8,128)(2,1)S(1)}, u32[]{:S(2)}, u32[]{:S(2)}) async-start(bf16[128,8,128]{2,0,1:T(8,128)(2,1)} %bitcast.5), calls=%async_computation.1 | async-start | bytes 524288 | tf_op jit(solution)/shard_map/all_to_all | solution.py:82
  15.2 10.9 %all-to-all-start = ((bf16[128,8,128]{0,2,1:T(8,128)(2,1)}), bf16[128,8,128]{0,2,1:T(8,128)(2,1)S(1)}, u32[]{:S(2)}, u32[]{:S(2)}) async-start(bf16[128,8,128]{0,2,1:T(8,128)(2,1)} %bitcast.1), calls=%async_computation | async-start | bytes 524288 | tf_op jit(solution)/shard_map/all_to_all | solution.py:85
  26.1 17.3 %all-to-all-start.2 = ((bf16[128,8,256]{2,0,1:T(8,128)(2,1)}), bf16[128,8,256]{2,0,1:T(8,128)(2,1)S(1)}, u32[]{:S(2)}, u32[]{:S(2)}) async-start(bf16[128,8,256]{2,0,1:T(8,128)(2,1)} %bitcast.232), calls=%async_computation.2 | async-start | bytes 1048576 | tf_op jit(solution)/shard_map/all_to_all | solution.py:78
  33.4 30.8 %collective-permute-start.2 = (bf16[1024,128]{1,0:T(8,128)(2,1)S(1)}, bf16[1024,128]{1,0:T(8,128)(2,1)}, u32[]{:S(2)}, u32[]{:S(2)}) collective-permute-start(bf16[1024,128]{1,0:T(8,128)(2,1)S(1)} %bitcast.246), channel_id=1, source_target_pairs={{0,16},{8,24},{16,32},{24,40},{32,48},{40,56},{48,64},{56,72},{64,... | collective-permute-start | bytes 786440 | tf_op jit(solution)/shard_map/ppermute | solution.py:20
  39.3 24.9 %collective-permute-start.3 = (bf16[1024,128]{1,0:T(8,128)(2,1)S(1)}, bf16[1024,128]{1,0:T(8,128)(2,1)}, u32[]{:S(2)}, u32[]{:S(2)}) collective-permute-start(bf16[1024,128]{1,0:T(8,128)(2,1)S(1)} %bitcast.247), channel_id=1, source_target_pairs={{0,8},{8,16},{16,24},{24,32},{32,40},{40,48},{48,56},{56,64},{64,7... | collective-permute-start | bytes 786440 | tf_op jit(solution)/shard_map/ppermute | solution.py:20
  43.3 15.0 %all-to-all-start.4 = ((bf16[128,8,256]{0,2,1:T(8,128)(2,1)}), bf16[128,8,256]{0,2,1:T(8,128)(2,1)S(1)}, u32[]{:S(2)}, u32[]{:S(2)}) async-start(bf16[128,8,256]{0,2,1:T(8,128)(2,1)} %bitcast.34), calls=%async_computation.4 | async-start | bytes 1048576 | tf_op jit(solution)/shard_map/all_to_all | solution.py:79
  48.7 27.6 %collective-permute-start = (bf16[1024,128]{0,1:T(8,128)(2,1)}, bf16[1024,128]{0,1:T(8,128)(2,1)}, u32[]{:S(2)}, u32[]{:S(2)}) collective-permute-start(bf16[1024,128]{0,1:T(8,128)(2,1)} %copy_bitcast_fusion.1), channel_id=1, source_target_pairs={{0,16},{8,24},{16,32},{24,40},{32,48},{40,56},{48,64},{56,72},{64,... | collective-permute-start | bytes 786440 | tf_op jit(solution)/shard_map/ppermute | solution.py:20
  51.0 26.3 %collective-permute-start.1 = (bf16[1024,128]{0,1:T(8,128)(2,1)}, bf16[1024,128]{0,1:T(8,128)(2,1)}, u32[]{:S(2)}, u32[]{:S(2)}) collective-permute-start(bf16[1024,128]{0,1:T(8,128)(2,1)} %copy_bitcast_fusion.1), channel_id=1, source_target_pairs={{0,8},{8,16},{16,24},{24,32},{32,40},{40,48},{48,56},{56,64},{64,7... | collective-permute-start | bytes 786440 | tf_op jit(solution)/shard_map/ppermute | solution.py:20
  60.3 7.3 %copy-start.15 = (bf16[256,2,128]{2,1,0:T(2,128)(2,1)}, bf16[256,2,128]{2,1,0:T(2,128)(2,1)S(1)}, u32[]{:S(2)}) copy-start(bf16[256,2,128]{2,1,0:T(2,128)(2,1)S(1)} %reshape.597) | copy-start | bytes 393220
  80.5 11.0 %copy-start.6 = (bf16[128,2,256]{2,0,1:T(8,128)(2,1)}, bf16[128,2,256]{2,0,1:T(8,128)(2,1)S(1)}, u32[]{:S(2)}) copy-start(bf16[128,2,256]{2,0,1:T(8,128)(2,1)S(1)} %convolution_convert_fusion.2) | copy-start | bytes 393220
  81.4 13.0 %copy-start.8 = (bf16[128,2,256]{2,0,1:T(8,128)(2,1)}, bf16[128,2,256]{2,0,1:T(8,128)(2,1)S(1)}, u32[]{:S(2)}) copy-start(bf16[128,2,256]{2,0,1:T(8,128)(2,1)S(1)} %convolution_convert_fusion.1) | copy-start | bytes 393220
  82.4 14.7 %copy-start.10 = (bf16[128,2,256]{2,0,1:T(8,128)(2,1)}, bf16[128,2,256]{2,0,1:T(8,128)(2,1)S(1)}, u32[]{:S(2)}) copy-start(bf16[128,2,256]{2,0,1:T(8,128)(2,1)S(1)} %convolution_convert_fusion) | copy-start | bytes 393220
  85.7 40.9 %collective-permute-start.7 = (bf16[1024,128]{1,0:T(8,128)(2,1)}, bf16[1024,128]{1,0:T(8,128)(2,1)}, u32[]{:S(2)}, u32[]{:S(2)}) collective-permute-start(bf16[1024,128]{1,0:T(8,128)(2,1)} %slice.408), channel_id=1, source_target_pairs={{16,0},{24,8},{32,16},{40,24},{48,32},{56,40},{64,48},{72,56},{80,... | collective-permute-start | bytes 786440 | tf_op jit(solution)/shard_map/ppermute | solution.py:20
  88.0 38.6 %collective-permute-start.6 = (bf16[1024,128]{1,0:T(8,128)(2,1)}, bf16[1024,128]{1,0:T(8,128)(2,1)}, u32[]{:S(2)}, u32[]{:S(2)}) collective-permute-start(bf16[1024,128]{1,0:T(8,128)(2,1)} %slice.409), channel_id=1, source_target_pairs={{8,0},{16,8},{24,16},{32,24},{40,32},{48,40},{56,48},{64,56},{72,6... | collective-permute-start | bytes 786440 | tf_op jit(solution)/shard_map/ppermute | solution.py:20
  100.0 15.2 %all-to-all-start.5 = ((bf16[8,128,256]{2,1,0:T(8,128)(2,1)}), bf16[8,128,256]{2,1,0:T(8,128)(2,1)S(1)}, u32[]{:S(2)}, u32[]{:S(2)}) async-start(bf16[8,128,256]{2,1,0:T(8,128)(2,1)} %bitcast.58), calls=%async_computation.5 | async-start | bytes 1048576 | tf_op jit(solution)/shard_map/all_to_all | solution.py:162
  107.9 11.4 %copy-start.2 = (f32[3072,128]{1,0:T(8,128)S(1)}, f32[3072,128]{1,0:T(8,128)}, u32[]{:S(2)}) copy-start(f32[3072,128]{1,0:T(8,128)} %copy-done.1) | copy-start | bytes 4718596
  108.7 10.6 %copy-start.5 = (f32[2304,128]{1,0:T(8,128)S(1)}, f32[2304,128]{1,0:T(8,128)}, u32[]{:S(2)}) copy-start(f32[2304,128]{1,0:T(8,128)} %copy-done.4) | copy-start | bytes 3538948
  115.1 14.5 %all-to-all-start.3 = ((bf16[8,128,256]{2,1,0:T(8,128)(2,1)}), bf16[8,128,256]{2,1,0:T(8,128)(2,1)}, u32[]{:S(2)}, u32[]{:S(2)}) async-start(bf16[8,128,256]{2,1,0:T(8,128)(2,1)} %bitcast.234), calls=%async_computation.3 | async-start | bytes 1048576 | tf_op jit(solution)/shard_map/all_to_all | solution.py:161
  120.1 14.4 %collective-permute-start.5 = (bf16[1024,128]{1,0:T(8,128)(2,1)}, bf16[1024,128]{1,0:T(8,128)(2,1)S(1)}, u32[]{:S(2)}, u32[]{:S(2)}) collective-permute-start(bf16[1024,128]{1,0:T(8,128)(2,1)} %slice.410), channel_id=1, source_target_pairs={{16,0},{24,8},{32,16},{40,24},{48,32},{56,40},{64,48},{72,56},{80,... | collective-permute-start | bytes 786440 | tf_op jit(solution)/shard_map/ppermute | solution.py:20
  124.1 17.1 %collective-permute-start.4 = (bf16[1024,128]{1,0:T(8,128)(2,1)}, bf16[1024,128]{1,0:T(8,128)(2,1)S(1)}, u32[]{:S(2)}, u32[]{:S(2)}) collective-permute-start(bf16[1024,128]{1,0:T(8,128)(2,1)} %slice.411), channel_id=1, source_target_pairs={{8,0},{16,8},{24,16},{32,24},{40,32},{48,40},{56,48},{64,56},{72,6... | collective-permute-start | bytes 786440 | tf_op jit(solution)/shard_map/ppermute | solution.py:20
  129.6 12.4 %all-to-all-start.7 = ((bf16[8,128,128]{2,1,0:T(8,128)(2,1)}), bf16[8,128,128]{2,1,0:T(8,128)(2,1)S(1)}, u32[]{:S(2)}, u32[]{:S(2)}) async-start(bf16[8,128,128]{2,1,0:T(8,128)(2,1)} %bitcast.73), calls=%async_computation.7 | async-start | bytes 524288 | tf_op jit(solution)/shard_map/all_to_all | solution.py:148
  142.0 12.0 %all-to-all-start.6 = ((bf16[8,128,128]{2,1,0:T(8,128)(2,1)}), bf16[8,128,128]{2,1,0:T(8,128)(2,1)S(1)}, u32[]{:S(2)}, u32[]{:S(2)}) async-start(bf16[8,128,128]{2,1,0:T(8,128)(2,1)} %bitcast.65), calls=%async_computation.6 | async-start | bytes 524288 | tf_op jit(solution)/shard_map/all_to_all | solution.py:141
  (15 other events, 38.9 us)

commit v2 on v1

--- a/solution.py
+++ b/solution.py
@@ -74,24 +74,28 @@
     local_q = heads_q // seq_width
     copies = seq_width // heads_k
     score_scale = 1.0 / math.sqrt(HD)
-    q_seq, g_seq = (
-        lax.all_to_all(queries, "sp", split_axis=1, concat_axis=0, tiled=True),
-        lax.all_to_all(out_grad, "sp", split_axis=1, concat_axis=0, tiled=True),
+    packed = jnp.concatenate(
+        [
+            queries.reshape(tok_dev, seq_width, local_q * HD),
+            out_grad.reshape(tok_dev, seq_width, local_q * HD),
+            widen_heads(key_rows, copies).reshape(tok_dev, seq_width, HD),
+            widen_heads(value_rows, copies).reshape(tok_dev, seq_width, HD),
+        ],
+        axis=2,
     )
-    k_seq, v_seq = (
-        lax.all_to_all(
-            widen_heads(key_rows, copies), "sp", split_axis=1, concat_axis=0, tiled=True
-        ),
-        lax.all_to_all(
-            widen_heads(value_rows, copies), "sp", split_axis=1, concat_axis=0, tiled=True
-        ),
-    )
+    packed = lax.all_to_all(packed, "sp", split_axis=1, concat_axis=0, tiled=True)
+    packed = packed.reshape(span_rows, packed.shape[-1])
+    q_width = local_q * HD
+    q_seq = packed[:, :q_width]
+    g_seq = packed[:, q_width : 2 * q_width]
+    kv_seq = packed[:, 2 * q_width :]
     reach = MOST_BLK * BLK
     reach_groups = (reach - 1) // span_rows + 1
     first_place = lax.axis_index("fsdp") * span_rows
-    earlier = [passed_along((k_seq, v_seq), "fsdp", d) for d in range(reach_groups, 0, -1)]
-    k_all = jnp.concatenate([piece[0] for piece in earlier] + [k_seq], axis=0)
-    v_all = jnp.concatenate([piece[1] for piece in earlier] + [v_seq], axis=0)
+    earlier = [passed_along(kv_seq, "fsdp", d) for d in range(reach_groups, 0, -1)]
+    kv_all = jnp.concatenate(earlier + [kv_seq], axis=0)
+    k_all = kv_all[:, :HD]
+    v_all = kv_all[:, HD:]
     base_place = first_place - reach_groups * span_rows
     key_count = (reach_groups + 1) * span_rows
     labels = doc_index(doc_lengths, base_place, key_count)
@@ -123,44 +127,29 @@
         dq_parts.append(dq_block.reshape(Q_ROWS, local_q * HD))
         grad_k_all = grad_k_all.at[k_lo : k_lo + window].add(grad_k)
         grad_v_all = grad_v_all.at[k_lo : k_lo + window].add(grad_v)
-    key_sum = grad_k_all[own_start:]
-    value_sum = grad_v_all[own_start:]
+    grad_kv_all = jnp.concatenate([grad_k_all, grad_v_all], axis=1)
+    kv_sum = grad_kv_all[own_start:]
     for distance in range(1, reach_groups + 1):
         lo = (reach_groups - distance) * span_rows
-        back_k, back_v = passed_along(
-            (
-                grad_k_all[lo : lo + span_rows].astype(jnp.bfloat16),
-                grad_v_all[lo : lo + span_rows].astype(jnp.bfloat16),
-            ),
-            "fsdp",
-            -distance,
+        back = passed_along(
+            grad_kv_all[lo : lo + span_rows].astype(jnp.bfloat16), "fsdp", -distance
         )
-        key_sum = key_sum + back_k
-        value_sum = value_sum + back_v
-    key_back, value_back = (
-        lax.all_to_all(
-            (key_sum * score_scale).astype(jnp.bfloat16),
-            "sp",
-            split_axis=0,
-            concat_axis=1,
-            tiled=True,
-        ),
-        lax.all_to_all(
-            value_sum.astype(jnp.bfloat16), "sp", split_axis=0, concat_axis=1, tiled=True
-        ),
-    )
+        kv_sum = kv_sum + back
+    kv_sum = jnp.concatenate([kv_sum[:, :HD] * score_scale, kv_sum[:, HD:]], axis=1)
+    attn_seq = jnp.concatenate(attn_parts, axis=0)
+    dq_seq = jnp.concatenate(dq_parts, axis=0)
+    outgoing = jnp.concatenate([attn_seq, dq_seq, kv_sum.astype(jnp.bfloat16)], axis=1)
+    back_all = lax.all_to_all(outgoing, "sp", split_axis=0, concat_axis=1, tiled=True)
+    back_all = back_all.reshape(tok_dev, seq_width, outgoing.shape[1])
+    attn_out = back_all[:, :, :q_width].reshape(tok_dev, heads_q * HD)
+    grad_queries = back_all[:, :, q_width : 2 * q_width].reshape(tok_dev, heads_q * HD)
+    kv_back = back_all[:, :, 2 * q_width :].astype(jnp.float32)
     grad_keys = jnp.sum(
-        key_back.astype(jnp.float32).reshape(tok_dev, heads_k, copies, HD), axis=2
+        kv_back[:, :, :HD].reshape(tok_dev, heads_k, copies, HD), axis=2
     ).reshape(tok_dev, heads_k * HD)
     grad_values = jnp.sum(
-        value_back.astype(jnp.float32).reshape(tok_dev, heads_k, copies, HD), axis=2
+        kv_back[:, :, HD:].reshape(tok_dev, heads_k, copies, HD), axis=2
     ).reshape(tok_dev, heads_k * HD)
-    attn_seq = jnp.concatenate(attn_parts, axis=0)
-    dq_seq = jnp.concatenate(dq_parts, axis=0)
-    attn_out, grad_queries = (
-        lax.all_to_all(attn_seq, "sp", split_axis=0, concat_axis=1, tiled=True),
-        lax.all_to_all(dq_seq, "sp", split_axis=0, concat_axis=1, tiled=True),
-    )
     return (
         attn_out,
         grad_queries,

time: 156 us -> 159 us (1.019)
  the two profiles are of different devices: /device:TPU:230 before, /device:TPU:196 now
where the time goes in v2:
time: 159 us; the launch traced here: 158 us
  waiting for transfers between devices  44.2 us (28%)
  starting transfers between devices  24.6 us (15%)
  blocking collectives  24.5 us (15%)
  local copies, waits for them, and re-layouts  22.3 us (14%)
  matrix products  21.3 us (13%)
  other arithmetic  20.1 us (13%)
    ppermute x4, waiting for transfers between devices, passed_along(): lax.ppermute(value, axis, [(source, source + steps) for source in range(f...  28.8 us
    all_to_all x1, blocking collectives, local(): lax.all_to_all(outgoing, 'sp', split_axis=0, concat_axis=1, tiled=True)  24.5 us
    ppermute x4, starting transfers between devices, passed_along(): lax.ppermute(value, axis, [(source, source + steps) for source in range(f...  20 us
    all_to_all x1, waiting for transfers between devices, local(): lax.all_to_all(packed, 'sp', split_axis=1, concat_axis=0, tiled=True)  15.4 us
    and x2, other arithmetic, local(): (q_label[:, None] == k_label[None, :]) & (k_place[None, :] <= q_place[:,...  7.82 us
    unnamed x56, local copies, waits for them, and re-layouts  6.4 us
    all_to_all x1, starting transfers between devices, local(): lax.all_to_all(packed, 'sp', split_axis=1, concat_axis=0, tiled=True)  4.6 us
    dot_general x4, matrix products, block_pass(): jnp.einsum('hqk,qhd->kd', probs_bf, g_block, preferred_element_type=jnp.f...  4.34 us
  transfers between devices with their start and end apart: 5, of which 5 were waited for; matrix products, arithmetic and copies ran while one was open for 15% of the time, Pallas kernels for 0%

profile of v2, /device:TPU:196, one launch (start us, length us, event | category | flops | bytes accessed | tf_op | source)
XLA Modules:
  0.0 158.5 jit_solution(11667819237316488024)
XLA Ops:
  2.5 1.3 copy_bitcast_fusion
  3.9 1.3 pad_maximum_fusion.1
  5.2 4.6 %all-to-all-start = ((bf16[128,8,768]{2,0,1:T(8,128)(2,1)}), bf16[128,8,768]{2,0,1:T(8,128)(2,1)S(1)}, u32[]{:S(2)}, u32[]{:S(2)}) async-start(bf16[128,8,768]{2,0,1:T(8,128)(2,1)} %pad_maximum_fusion.1), calls=%async_computation | async-start | bytes 3145728 | tf_op jit(solution)/shard_map/all_to_all | solution.py:86
  10.2 1.9 %convert_reduce_fusion = s32[3072]{0:T(1024)S(1)} fusion(s32[128]{0:T(128)S(1)} %multiply_reduce_fusion.4, s32[3072]{0:T(1024)S(1)} %iota_add_fusion), kind=kLoop, calls=%fused_computation.71 | loop fusion | flops 1176576 | bytes 25088 | tf_op jit(solution)/shard_map/reduce_sum | solution.py:30
  12.2 3.8 %compare_and_fusion = (pred[256,2304]{0,1:T(8,128)(4,1)}, pred[256,2304]{0,1:T(8,128)(4,1)S(1)}) fusion(s32[256]{0:T(256)S(1)} %get-tuple-element.139, s32[256]{0:T(256)S(1)} %get-tuple-element.135, s32[2304]{0:T(1024)S(1)} %get-tuple-element.131, s32[2304]{0:T(1024)S(1)} %get-tuple-element.127, s32[256]{0:T(256)S(1)} %get-tuple-element.140, ...), kind=kLoop, calls=%fused_computation.64 | loop fusion | flops 3538944 | bytes 1220608 | tf_op jit(solution)/shard_map/and | solution.py:115
  16.0 15.4 %all-to-all-done = bf16[128,8,768]{2,0,1:T(8,128)(2,1)S(1)} async-done(((bf16[128,8,768]{2,0,1:T(8,128)(2,1)}), bf16[128,8,768]{2,0,1:T(8,128)(2,1)S(1)}, u32[]{:S(2)}, u32[]{:S(2)}) %all-to-all-start) | async-done | bytes 1572896 | tf_op jit(solution)/shard_map/all_to_all | solution.py:86
  31.4 3.1 %collective-permute-start.1 = (bf16[1024,256]{1,0:T(8,128)(2,1)S(1)}, bf16[1024,256]{1,0:T(8,128)(2,1)}, u32[]{:S(2)}, u32[]{:S(2)}) collective-permute-start(bf16[1024,256]{1,0:T(8,128)(2,1)S(1)} %slice.347), channel_id=1, source_target_pairs={{0,8},{8,16},{16,24},{24,32},{32,40},{40,48},{48,56},{56,64},{64,7... | collective-permute-start | bytes 1572872 | tf_op jit(solution)/shard_map/ppermute | solution.py:20
  34.5 4.1 %collective-permute-start = (bf16[1024,256]{1,0:T(8,128)(2,1)S(1)}, bf16[1024,256]{1,0:T(8,128)(2,1)}, u32[]{:S(2)}, u32[]{:S(2)}) collective-permute-start(bf16[1024,256]{1,0:T(8,128)(2,1)S(1)} %slice.347), channel_id=1, source_target_pairs={{0,16},{8,24},{16,32},{24,40},{32,48},{40,56},{48,64},{56,72},{64,... | collective-permute-start | bytes 1572872 | tf_op jit(solution)/shard_map/ppermute | solution.py:20
  38.6 4.0 %compare_and_fusion.2 = (pred[256,2304]{0,1:T(8,128)(4,1)}, pred[256,2304]{0,1:T(8,128)(4,1)}) fusion(s32[256]{0:T(256)S(1)} %get-tuple-element.141, s32[256]{0:T(256)S(1)} %get-tuple-element.137, s32[2304]{0:T(1024)S(1)} %get-tuple-element.133, s32[2304]{0:T(1024)S(1)} %get-tuple-element.129, s32[256]{0:T(256)S(1)} %get-tuple-element.142, ...), kind=kLoop, calls=%fused_computation.66 | loop fusion | flops 3538944 | bytes 1220608 | tf_op jit(solution)/shard_map/and | solution.py:115
  45.0 1.7 %copy.376 = bf16[256,256]{0,1:T(8,128)(2,1)} copy(bf16[256,256]{1,0:T(8,128)(2,1)} %get-tuple-element.119) | data formatting | bytes 262144 | tf_op jit(solution)/shard_map/reshape | solution.py:116
  49.4 6.4 %collective-permute-done.1 = bf16[1024,256]{1,0:T(8,128)(2,1)} collective-permute-done((bf16[1024,256]{1,0:T(8,128)(2,1)S(1)}, bf16[1024,256]{1,0:T(8,128)(2,1)}, u32[]{:S(2)}, u32[]{:S(2)}) %collective-permute-start.1) | collective-permute-done | bytes 524320 | tf_op jit(solution)/shard_map/ppermute | solution.py:20
  55.8 2.3 %collective-permute-done = bf16[1024,256]{1,0:T(8,128)(2,1)} collective-permute-done((bf16[1024,256]{1,0:T(8,128)(2,1)S(1)}, bf16[1024,256]{1,0:T(8,128)(2,1)}, u32[]{:S(2)}, u32[]{:S(2)}) %collective-permute-start) | collective-permute-done | bytes 524320 | tf_op jit(solution)/shard_map/ppermute | solution.py:20
  58.1 1.3 pad_maximum_fusion.2
  72.0 1.3 fusion.18
  78.2 1.1 fusion.33
  86.2 10.7 %collective-permute-start.2 = (bf16[1024,256]{0,1:T(8,128)(2,1)}, bf16[1024,256]{0,1:T(8,128)(2,1)}, u32[]{:S(2)}, u32[]{:S(2)}) collective-permute-start(bf16[1024,256]{0,1:T(8,128)(2,1)} %get-tuple-element.117), channel_id=1, source_target_pairs={{8,0},{16,8},{24,16},{32,24},{40,32},{48,40},{56,48},{64,56},{72,6... | collective-permute-start | bytes 1572872 | tf_op jit(solution)/shard_map/ppermute | solution.py:20
  96.9 2.1 %collective-permute-start.3 = (bf16[1024,256]{0,1:T(8,128)(2,1)}, bf16[1024,256]{0,1:T(8,128)(2,1)}, u32[]{:S(2)}, u32[]{:S(2)}) collective-permute-start(bf16[1024,256]{0,1:T(8,128)(2,1)} %get-tuple-element.118), channel_id=1, source_target_pairs={{16,0},{24,8},{32,16},{40,24},{48,32},{56,40},{64,48},{72,56},{80,... | collective-permute-start | bytes 1572872 | tf_op jit(solution)/shard_map/ppermute | solution.py:20
  100.4 2.1 %copy.316 = bf16[1024,256]{1,0:T(8,128)(2,1)} copy(bf16[1024,256]{0,1:T(8,128)(2,1)} %pad_maximum_fusion.5) | data formatting | bytes 1048576 | tf_op jit(solution)/shard_map/concatenate | solution.py:140
  102.5 1.8 %pad_maximum_fusion.4 = bf16[1024,256]{0,1:T(8,128)(2,1)} fusion(bf16[256,256]{0,1:T(8,128)(2,1)} %bitcast.243, bf16[256,256]{0,1:T(8,128)(2,1)} %bitcast.241, bf16[256,256]{0,1:T(8,128)(2,1)S(1)} %bitcast.239, bf16[256,256]{0,1:T(8,128)(2,1)S(1)} %bitcast.237), kind=kLoop, calls=%fused_computation.101 | loop fusion | flops 2097152 | bytes 1048576 | tf_op jit(solution)/shard_map/concatenate | solution.py:139
  104.3 2.1 %copy.299 = bf16[1024,256]{1,0:T(8,128)(2,1)} copy(bf16[1024,256]{0,1:T(8,128)(2,1)} %pad_maximum_fusion.4) | data formatting | bytes 1048576 | tf_op jit(solution)/shard_map/concatenate | solution.py:139
  106.3 12.1 %collective-permute-done.2 = bf16[1024,256]{0,1:T(8,128)(2,1)} collective-permute-done((bf16[1024,256]{0,1:T(8,128)(2,1)}, bf16[1024,256]{0,1:T(8,128)(2,1)}, u32[]{:S(2)}, u32[]{:S(2)}) %collective-permute-start.2) | collective-permute-done | bytes 524320 | tf_op jit(solution)/shard_map/ppermute | solution.py:20
  118.5 8.0 %collective-permute-done.3 = bf16[1024,256]{0,1:T(8,128)(2,1)} collective-permute-done((bf16[1024,256]{0,1:T(8,128)(2,1)}, bf16[1024,256]{0,1:T(8,128)(2,1)}, u32[]{:S(2)}, u32[]{:S(2)}) %collective-permute-start.3) | collective-permute-done | bytes 524320 | tf_op jit(solution)/shard_map/ppermute | solution.py:20
  126.5 1.4 fusion.43
  129.2 24.5 %all_to_all.28 = bf16[8,128,768]{2,1,0:T(8,128)(2,1)S(1)} all-to-all(bf16[8,128,768]{2,1,0:T(8,128)(2,1)S(1)} %pad_maximum_fusion.3), channel_id=1, replica_groups=mesh['fsdp'=64,'sp'=8] {'sp'}, dimensions={0} | all-to-all | bytes 3145728 | tf_op jit(solution)/shard_map/all_to_all | solution.py:142
  (133 shorter events, 38.7 us)
Async XLA Ops:
  5.2 4.6 %copy-start.25 = (s32[128]{0:T(128)S(1)}, s32[128]{0:T(128)}, u32[]{:S(2)}) copy-start(s32[128]{0:T(128)} %param.25) | copy-start | bytes 1540
  5.2 26.2 %all-to-all-start = ((bf16[128,8,768]{2,0,1:T(8,128)(2,1)}), bf16[128,8,768]{2,0,1:T(8,128)(2,1)S(1)}, u32[]{:S(2)}, u32[]{:S(2)}) async-start(bf16[128,8,768]{2,0,1:T(8,128)(2,1)} %pad_maximum_fusion.1), calls=%async_computation | async-start | bytes 3145728 | tf_op jit(solution)/shard_map/all_to_all | solution.py:86
  31.4 24.4 %collective-permute-start.1 = (bf16[1024,256]{1,0:T(8,128)(2,1)S(1)}, bf16[1024,256]{1,0:T(8,128)(2,1)}, u32[]{:S(2)}, u32[]{:S(2)}) collective-permute-start(bf16[1024,256]{1,0:T(8,128)(2,1)S(1)} %slice.347), channel_id=1, source_target_pairs={{0,8},{8,16},{16,24},{24,32},{32,40},{40,48},{48,56},{56,64},{64,7... | collective-permute-start | bytes 1572872 | tf_op jit(solution)/shard_map/ppermute | solution.py:20
  34.5 23.6 %collective-permute-start = (bf16[1024,256]{1,0:T(8,128)(2,1)S(1)}, bf16[1024,256]{1,0:T(8,128)(2,1)}, u32[]{:S(2)}, u32[]{:S(2)}) collective-permute-start(bf16[1024,256]{1,0:T(8,128)(2,1)S(1)} %slice.347), channel_id=1, source_target_pairs={{0,16},{8,24},{16,32},{24,40},{32,48},{40,56},{48,64},{56,72},{64,... | collective-permute-start | bytes 1572872 | tf_op jit(solution)/shard_map/ppermute | solution.py:20
  43.4 5.7 %copy-start.21 = (bf16[256,256]{1,0:T(8,128)(2,1)S(1)}, bf16[256,256]{1,0:T(8,128)(2,1)}, u32[]{:S(2)}) copy-start(bf16[256,256]{1,0:T(8,128)(2,1)} %get-tuple-element.124) | copy-start | bytes 393220
  43.4 5.8 %copy-start.20 = (bf16[256,256]{1,0:T(8,128)(2,1)S(1)}, bf16[256,256]{1,0:T(8,128)(2,1)}, u32[]{:S(2)}) copy-start(bf16[256,256]{1,0:T(8,128)(2,1)} %get-tuple-element.125) | copy-start | bytes 393220
  43.4 5.9 %copy-start.19 = (bf16[256,256]{1,0:T(8,128)(2,1)S(1)}, bf16[256,256]{1,0:T(8,128)(2,1)}, u32[]{:S(2)}) copy-start(bf16[256,256]{1,0:T(8,128)(2,1)} %get-tuple-element.126) | copy-start | bytes 393220
  43.9 24.0 %copy-start.3 = (bf16[256,2,128]{0,2,1:T(8,128)(2,1)}, bf16[256,2,128]{0,2,1:T(8,128)(2,1)S(1)}, u32[]{:S(2)}) copy-start(bf16[256,2,128]{0,2,1:T(8,128)(2,1)S(1)} %copy.327) | copy-start | bytes 393220
  46.8 12.6 %copy-start.13 = (pred[256,2304]{0,1:T(8,128)(4,1)S(1)}, pred[256,2304]{0,1:T(8,128)(4,1)}, u32[]{:S(2)}) copy-start(pred[256,2304]{0,1:T(8,128)(4,1)} %get-tuple-element.156) | copy-start | bytes 1769476
  49.2 20.3 %copy-start.15 = (bf16[256,256]{0,1:T(8,128)(2,1)}, bf16[256,256]{0,1:T(8,128)(2,1)S(1)}, u32[]{:S(2)}) copy-start(bf16[256,256]{0,1:T(8,128)(2,1)S(1)} %copy.375) | copy-start | bytes 393220
  49.3 16.0 %copy-start.17 = (bf16[256,256]{0,1:T(8,128)(2,1)}, bf16[256,256]{0,1:T(8,128)(2,1)S(1)}, u32[]{:S(2)}) copy-start(bf16[256,256]{0,1:T(8,128)(2,1)S(1)} %copy.374) | copy-start | bytes 393220
  64.4 1.1 copy-start.12
  67.8 1.1 copy-start.7
  71.9 3.2 %copy-start.9 = (bf16[128,2,256]{2,0,1:T(8,128)(2,1)}, bf16[128,2,256]{2,0,1:T(8,128)(2,1)S(1)}, u32[]{:S(2)}) copy-start(bf16[128,2,256]{2,0,1:T(8,128)(2,1)S(1)} %convolution_convert_fusion.1) | copy-start | bytes 393220
  78.1 1.2 copy-start.11
  78.1 1.2 copy-start.14
  81.7 1.2 copy-start.10
  81.7 1.1 copy-start.22
  86.2 32.3 %collective-permute-start.2 = (bf16[1024,256]{0,1:T(8,128)(2,1)}, bf16[1024,256]{0,1:T(8,128)(2,1)}, u32[]{:S(2)}, u32[]{:S(2)}) collective-permute-start(bf16[1024,256]{0,1:T(8,128)(2,1)} %get-tuple-element.117), channel_id=1, source_target_pairs={{8,0},{16,8},{24,16},{32,24},{40,32},{48,40},{56,48},{64,56},{72,6... | collective-permute-start | bytes 1572872 | tf_op jit(solution)/shard_map/ppermute | solution.py:20
  96.9 5.6 %copy-start.6 = (bf16[128,2,256]{2,0,1:T(8,128)(2,1)S(1)}, bf16[128,2,256]{2,0,1:T(8,128)(2,1)}, u32[]{:S(2)}) copy-start(bf16[128,2,256]{2,0,1:T(8,128)(2,1)} %copy-done.5) | copy-start | bytes 393220
  96.9 5.6 %copy-start.8 = (bf16[128,2,256]{2,0,1:T(8,128)(2,1)S(1)}, bf16[128,2,256]{2,0,1:T(8,128)(2,1)}, u32[]{:S(2)}) copy-start(bf16[128,2,256]{2,0,1:T(8,128)(2,1)} %copy-done.7) | copy-start | bytes 393220
  96.9 29.6 %collective-permute-start.3 = (bf16[1024,256]{0,1:T(8,128)(2,1)}, bf16[1024,256]{0,1:T(8,128)(2,1)}, u32[]{:S(2)}, u32[]{:S(2)}) collective-permute-start(bf16[1024,256]{0,1:T(8,128)(2,1)} %get-tuple-element.118), channel_id=1, source_target_pairs={{16,0},{24,8},{32,16},{40,24},{48,32},{56,40},{64,48},{72,56},{80,... | collective-permute-start | bytes 1572872 | tf_op jit(solution)/shard_map/ppermute | solution.py:20
  127.9 1.0 copy-start.1
  127.9 1.2 copy-start.2
  (7 other events, 6.6 us)

commit v3 on v2

--- a/solution.py
+++ b/solution.py
@@ -74,21 +74,27 @@
     local_q = heads_q // seq_width
     copies = seq_width // heads_k
     score_scale = 1.0 / math.sqrt(HD)
-    packed = jnp.concatenate(
+    kv_pack = jnp.concatenate(
         [
-            queries.reshape(tok_dev, seq_width, local_q * HD),
-            out_grad.reshape(tok_dev, seq_width, local_q * HD),
             widen_heads(key_rows, copies).reshape(tok_dev, seq_width, HD),
             widen_heads(value_rows, copies).reshape(tok_dev, seq_width, HD),
         ],
         axis=2,
     )
-    packed = lax.all_to_all(packed, "sp", split_axis=1, concat_axis=0, tiled=True)
-    packed = packed.reshape(span_rows, packed.shape[-1])
+    kv_seq = lax.all_to_all(kv_pack, "sp", split_axis=1, concat_axis=0, tiled=True)
+    kv_seq = kv_seq.reshape(span_rows, 2 * HD)
     q_width = local_q * HD
-    q_seq = packed[:, :q_width]
-    g_seq = packed[:, q_width : 2 * q_width]
-    kv_seq = packed[:, 2 * q_width :]
+    qg_pack = jnp.concatenate(
+        [
+            queries.reshape(tok_dev, seq_width, q_width),
+            out_grad.reshape(tok_dev, seq_width, q_width),
+        ],
+        axis=2,
+    )
+    qg_seq = lax.all_to_all(qg_pack, "sp", split_axis=1, concat_axis=0, tiled=True)
+    qg_seq = qg_seq.reshape(span_rows, 2 * q_width)
+    q_seq = qg_seq[:, :q_width]
+    g_seq = qg_seq[:, q_width:]
     reach = MOST_BLK * BLK
     reach_groups = (reach - 1) // span_rows + 1
     first_place = lax.axis_index("fsdp") * span_rows
@@ -128,22 +134,29 @@
         grad_k_all = grad_k_all.at[k_lo : k_lo + window].add(grad_k)
         grad_v_all = grad_v_all.at[k_lo : k_lo + window].add(grad_v)
     grad_kv_all = jnp.concatenate([grad_k_all, grad_v_all], axis=1)
-    kv_sum = grad_kv_all[own_start:]
-    for distance in range(1, reach_groups + 1):
-        lo = (reach_groups - distance) * span_rows
-        back = passed_along(
+    backs = [
+        passed_along(
             grad_kv_all[lo : lo + span_rows].astype(jnp.bfloat16), "fsdp", -distance
         )
-        kv_sum = kv_sum + back
-    kv_sum = jnp.concatenate([kv_sum[:, :HD] * score_scale, kv_sum[:, HD:]], axis=1)
+        for distance, lo in (
+            (d, (reach_groups - d) * span_rows) for d in range(1, reach_groups + 1)
+        )
+    ]
     attn_seq = jnp.concatenate(attn_parts, axis=0)
     dq_seq = jnp.concatenate(dq_parts, axis=0)
-    outgoing = jnp.concatenate([attn_seq, dq_seq, kv_sum.astype(jnp.bfloat16)], axis=1)
+    outgoing = jnp.concatenate([attn_seq, dq_seq], axis=1)
     back_all = lax.all_to_all(outgoing, "sp", split_axis=0, concat_axis=1, tiled=True)
     back_all = back_all.reshape(tok_dev, seq_width, outgoing.shape[1])
     attn_out = back_all[:, :, :q_width].reshape(tok_dev, heads_q * HD)
-    grad_queries = back_all[:, :, q_width : 2 * q_width].reshape(tok_dev, heads_q * HD)
-    kv_back = back_all[:, :, 2 * q_width :].astype(jnp.float32)
+    grad_queries = back_all[:, :, q_width:].reshape(tok_dev, heads_q * HD)
+    kv_sum = grad_kv_all[own_start:]
+    for back in backs:
+        kv_sum = kv_sum + back
+    kv_sum = jnp.concatenate([kv_sum[:, :HD] * score_scale, kv_sum[:, HD:]], axis=1)
+    kv_back = lax.all_to_all(
+        kv_sum.astype(jnp.bfloat16), "sp", split_axis=0, concat_axis=1, tiled=True
+    )
+    kv_back = kv_back.reshape(tok_dev, seq_width, 2 * HD).astype(jnp.float32)
     grad_keys = jnp.sum(
         kv_back[:, :, :HD].reshape(tok_dev, heads_k, copies, HD), axis=2
     ).reshape(tok_dev, heads_k * HD)

time: 159 us -> 138 us (0.87)
  the two profiles are of different devices: /device:TPU:196 before, /device:TPU:260 now
where the time goes in v3:
time: 138 us; the launch traced here: 137 us
  waiting for transfers between devices  53.3 us (39%)
  starting transfers between devices  30.9 us (22%)
  matrix products  21.2 us (15%)
  other arithmetic  18.3 us (13%)
  local copies, waits for them, and re-layouts  12.6 us (9%)
    ppermute x4, waiting for transfers between devices, passed_along(): lax.ppermute(value, axis, [(source, source + steps) for source in range(f...  37.6 us
    ppermute x4, starting transfers between devices, passed_along(): lax.ppermute(value, axis, [(source, source + steps) for source in range(f...  13.9 us
    all_to_all x1, waiting for transfers between devices, local(): lax.all_to_all(kv_sum.astype(jnp.bfloat16), 'sp', split_axis=0, concat_ax...  6.61 us
    all_to_all x1, waiting for transfers between devices, local(): lax.all_to_all(kv_pack, 'sp', split_axis=1, concat_axis=0, tiled=True)  6.36 us
    and x2, other arithmetic, local(): (q_label[:, None] == k_label[None, :]) & (k_place[None, :] <= q_place[:,...  6.27 us
    unnamed x17, local copies, waits for them, and re-layouts  5.26 us
    all_to_all x1, starting transfers between devices, local(): lax.all_to_all(kv_pack, 'sp', split_axis=1, concat_axis=0, tiled=True)  4.47 us
    all_to_all x1, starting transfers between devices, local(): lax.all_to_all(outgoing, 'sp', split_axis=0, concat_axis=1, tiled=True)  4.46 us
  transfers between devices with their start and end apart: 8, of which 7 were waited for; matrix products, arithmetic and copies ran while one was open for 15% of the time, Pallas kernels for 0%

profile of v3, /device:TPU:260, one launch (start us, length us, event | category | flops | bytes accessed | tf_op | source)
XLA Modules:
  0.0 137.4 jit_solution(8748465400182907777)
XLA Ops:
  3.5 4.5 %all-to-all-start = ((bf16[128,8,256]{2,0,1:T(8,128)(2,1)}), bf16[128,8,256]{2,0,1:T(8,128)(2,1)S(1)}, u32[]{:S(2)}, u32[]{:S(2)}) async-start(bf16[128,8,256]{2,0,1:T(8,128)(2,1)} %pad_maximum_fusion.3), calls=%async_computation | async-start | bytes 1048576 | tf_op jit(solution)/shard_map/all_to_all | solution.py:84
  8.4 1.9 %convert_reduce_fusion = s32[3072]{0:T(1024)S(1)} fusion(s32[128]{0:T(128)S(1)} %multiply_reduce_fusion.4, s32[3072]{0:T(1024)S(1)} %iota_add_fusion), kind=kLoop, calls=%fused_computation.69 | loop fusion | flops 1176576 | bytes 25088 | tf_op jit(solution)/shard_map/reduce_sum | solution.py:30
  12.0 6.4 %all-to-all-done = bf16[128,8,256]{2,0,1:T(8,128)(2,1)S(1)} async-done(((bf16[128,8,256]{2,0,1:T(8,128)(2,1)}), bf16[128,8,256]{2,0,1:T(8,128)(2,1)S(1)}, u32[]{:S(2)}, u32[]{:S(2)}) %all-to-all-start) | async-done | bytes 524320 | tf_op jit(solution)/shard_map/all_to_all | solution.py:84
  18.3 3.6 %all-to-all-start.1 = ((bf16[128,8,512]{0,2,1:T(8,128)(2,1)}), bf16[128,8,512]{0,2,1:T(8,128)(2,1)S(1)}, u32[]{:S(2)}, u32[]{:S(2)}) async-start(bf16[128,8,512]{0,2,1:T(8,128)(2,1)} %pad_maximum_fusion.2), calls=%async_computation.1 | async-start | bytes 2097152 | tf_op jit(solution)/shard_map/all_to_all | solution.py:94
  21.9 3.9 %compare_and_fusion.2 = (pred[256,2304]{0,1:T(8,128)(4,1)S(1)}, pred[256,2304]{0,1:T(8,128)(4,1)}) fusion(s32[256]{0:T(256)S(1)} %get-tuple-element.136, s32[256]{0:T(256)S(1)} %get-tuple-element.133, s32[2304]{0:T(1024)S(1)} %get-tuple-element.129, s32[2304]{0:T(1024)S(1)} %get-tuple-element.125, s32[256]{0:T(256)S(1)} %get-tuple-element.134, ...), kind=kLoop, calls=%fused_computation.66 | loop fusion | flops 3538944 | bytes 1220608 | tf_op jit(solution)/shard_map/and | solution.py:121
  25.7 2.9 %collective-permute-start = (bf16[1024,256]{1,0:T(8,128)(2,1)S(1)}, bf16[1024,256]{1,0:T(8,128)(2,1)}, u32[]{:S(2)}, u32[]{:S(2)}) collective-permute-start(bf16[1024,256]{1,0:T(8,128)(2,1)S(1)} %bitcast.265), channel_id=1, source_target_pairs={{0,16},{8,24},{16,32},{24,40},{32,48},{40,56},{48,64},{56,72},{64,... | collective-permute-start | bytes 1572872 | tf_op jit(solution)/shard_map/ppermute | solution.py:20
  28.6 4.0 %collective-permute-start.1 = (bf16[1024,256]{1,0:T(8,128)(2,1)S(1)}, bf16[1024,256]{1,0:T(8,128)(2,1)}, u32[]{:S(2)}, u32[]{:S(2)}) collective-permute-start(bf16[1024,256]{1,0:T(8,128)(2,1)S(1)} %bitcast.266), channel_id=1, source_target_pairs={{0,8},{8,16},{16,24},{24,32},{32,40},{40,48},{48,56},{56,64},{64,7... | collective-permute-start | bytes 1572872 | tf_op jit(solution)/shard_map/ppermute | solution.py:20
  32.6 2.4 %compare_and_fusion = (pred[256,2304]{0,1:T(8,128)(4,1)S(1)}, pred[256,2304]{0,1:T(8,128)(4,1)S(1)}) fusion(s32[256]{0:T(256)S(1)} %get-tuple-element.137, s32[256]{0:T(256)S(1)} %get-tuple-element.131, s32[2304]{0:T(1024)S(1)} %get-tuple-element.127, s32[2304]{0:T(1024)S(1)} %get-tuple-element.123, s32[256]{0:T(256)S(1)} %get-tuple-element.135, ...), kind=kLoop, calls=%fused_computation.64 | loop fusion | flops 3538944 | bytes 1220608 | tf_op jit(solution)/shard_map/and | solution.py:121
  35.1 2.7 %all-to-all-done.1 = bf16[128,8,512]{0,2,1:T(8,128)(2,1)S(1)} async-done(((bf16[128,8,512]{0,2,1:T(8,128)(2,1)}), bf16[128,8,512]{0,2,1:T(8,128)(2,1)S(1)}, u32[]{:S(2)}, u32[]{:S(2)}) %all-to-all-start.1) | async-done | bytes 1048608 | tf_op jit(solution)/shard_map/all_to_all | solution.py:94
  38.8 5.2 %collective-permute-done = bf16[1024,256]{1,0:T(8,128)(2,1)} collective-permute-done((bf16[1024,256]{1,0:T(8,128)(2,1)S(1)}, bf16[1024,256]{1,0:T(8,128)(2,1)}, u32[]{:S(2)}, u32[]{:S(2)}) %collective-permute-start) | collective-permute-done | bytes 524320 | tf_op jit(solution)/shard_map/ppermute | solution.py:20
  44.0 10.6 %collective-permute-done.1 = bf16[1024,256]{1,0:T(8,128)(2,1)} collective-permute-done((bf16[1024,256]{1,0:T(8,128)(2,1)S(1)}, bf16[1024,256]{1,0:T(8,128)(2,1)}, u32[]{:S(2)}, u32[]{:S(2)}) %collective-permute-start.1) | collective-permute-done | bytes 524320 | tf_op jit(solution)/shard_map/ppermute | solution.py:20
  54.7 1.3 pad_maximum_fusion.1
  67.9 1.1 fusion.33
  81.3 2.5 %collective-permute-start.2 = (bf16[1024,256]{0,1:T(8,128)(2,1)}, bf16[1024,256]{0,1:T(8,128)(2,1)}, u32[]{:S(2)}, u32[]{:S(2)}) collective-permute-start(bf16[1024,256]{0,1:T(8,128)(2,1)} %get-tuple-element.110), channel_id=1, source_target_pairs={{8,0},{16,8},{24,16},{32,24},{40,32},{48,40},{56,48},{64,56},{72,6... | collective-permute-start | bytes 1572872 | tf_op jit(solution)/shard_map/ppermute | solution.py:20
  83.8 4.6 %collective-permute-start.3 = (bf16[1024,256]{0,1:T(8,128)(2,1)}, bf16[1024,256]{0,1:T(8,128)(2,1)}, u32[]{:S(2)}, u32[]{:S(2)}) collective-permute-start(bf16[1024,256]{0,1:T(8,128)(2,1)} %get-tuple-element.111), channel_id=1, source_target_pairs={{16,0},{24,8},{32,16},{40,24},{48,32},{56,40},{64,48},{72,56},{80,... | collective-permute-start | bytes 1572872 | tf_op jit(solution)/shard_map/ppermute | solution.py:20
  88.8 1.2 maximum_maximum_fusion
  90.0 2.3 %copy.207 = bf16[1024,512]{1,0:T(8,128)(2,1)} copy(bf16[1024,512]{0,1:T(8,128)(2,1)} %maximum_maximum_fusion) | data formatting | bytes 2097152 | tf_op jit(solution)/shard_map/concatenate | solution.py:147
  92.3 4.5 %all-to-all-start.2 = ((bf16[8,128,512]{2,1,0:T(8,128)(2,1)}), bf16[8,128,512]{2,1,0:T(8,128)(2,1)}, u32[]{:S(2)}, u32[]{:S(2)}) async-start(bf16[8,128,512]{2,1,0:T(8,128)(2,1)} %bitcast.249), calls=%async_computation.2 | async-start | bytes 2097152 | tf_op jit(solution)/shard_map/all_to_all | solution.py:148
  96.8 1.5 %collective-permute-done.2 = bf16[1024,256]{0,1:T(8,128)(2,1)} collective-permute-done((bf16[1024,256]{0,1:T(8,128)(2,1)}, bf16[1024,256]{0,1:T(8,128)(2,1)}, u32[]{:S(2)}, u32[]{:S(2)}) %collective-permute-start.2) | collective-permute-done | bytes 524320 | tf_op jit(solution)/shard_map/ppermute | solution.py:20
  98.2 20.3 %collective-permute-done.3 = bf16[1024,256]{0,1:T(8,128)(2,1)} collective-permute-done((bf16[1024,256]{0,1:T(8,128)(2,1)}, bf16[1024,256]{0,1:T(8,128)(2,1)}, u32[]{:S(2)}, u32[]{:S(2)}) %collective-permute-start.3) | collective-permute-done | bytes 524320 | tf_op jit(solution)/shard_map/ppermute | solution.py:20
  118.6 1.4 %fusion.43 = f32[1024,256]{0,1:T(8,128)S(1)} fusion(f32[3072,128]{0,1:T(8,128)S(1)} %fusion.29, f32[3072,128]{0,1:T(8,128)S(1)} %fusion.35, bf16[1024,256]{0,1:T(8,128)(2,1)} %collective-permute-done.3, bf16[1024,256]{0,1:T(8,128)(2,1)} %collective-permute-done.2), kind=kLoop, calls=%fused_computation.84 | loop fusion | flops 1310720 | bytes 5242880 | tf_op jit(solution)/shard_map/add | solution.py:154
  120.9 4.5 %all-to-all-start.3 = ((bf16[8,128,256]{1,2,0:T(8,128)(2,1)}), bf16[8,128,256]{1,2,0:T(8,128)(2,1)S(1)}, u32[]{:S(2)}, u32[]{:S(2)}) async-start(bf16[8,128,256]{1,2,0:T(8,128)(2,1)} %pad_maximum_fusion.4), calls=%async_computation.3 | async-start | bytes 1048576 | tf_op jit(solution)/shard_map/all_to_all | solution.py:156
  125.4 1.6 %copy.208 = bf16[8,128,512]{1,2,0:T(8,128)(2,1)S(1)} copy(bf16[8,128,512]{2,1,0:T(8,128)(2,1)} %all-to-all-done.2) | data formatting | bytes 2097152 | tf_op jit(solution)/shard_map/all_to_all | solution.py:148
  129.1 6.6 %all-to-all-done.3 = bf16[8,128,256]{1,2,0:T(8,128)(2,1)S(1)} async-done(((bf16[8,128,256]{1,2,0:T(8,128)(2,1)}), bf16[8,128,256]{1,2,0:T(8,128)(2,1)S(1)}, u32[]{:S(2)}, u32[]{:S(2)}) %all-to-all-start.3) | async-done | bytes 524320 | tf_op jit(solution)/shard_map/all_to_all | solution.py:156
  (80 shorter events, 35.0 us)
Async XLA Ops:
  0.6 0.9 copy-start
  0.6 7.3 %copy-start.4 = (s32[128]{0:T(128)S(1)}, s32[128]{0:T(128)}, u32[]{:S(2)}) copy-start(s32[128]{0:T(128)} %param.25) | copy-start | bytes 1540
  0.7 9.6 %copy-start.2 = (bf16[128,2048]{1,0:T(8,128)(2,1)S(1)}, bf16[128,2048]{1,0:T(8,128)(2,1)}, u32[]{:S(2)}) copy-start(bf16[128,2048]{1,0:T(8,128)(2,1)} %param.21) | copy-start | bytes 1572868
  1.5 9.0 %copy-start.3 = (bf16[128,2048]{1,0:T(8,128)(2,1)S(1)}, bf16[128,2048]{1,0:T(8,128)(2,1)}, u32[]{:S(2)}) copy-start(bf16[128,2048]{1,0:T(8,128)(2,1)} %param.24) | copy-start | bytes 1572868
  3.5 14.8 %all-to-all-start = ((bf16[128,8,256]{2,0,1:T(8,128)(2,1)}), bf16[128,8,256]{2,0,1:T(8,128)(2,1)S(1)}, u32[]{:S(2)}, u32[]{:S(2)}) async-start(bf16[128,8,256]{2,0,1:T(8,128)(2,1)} %pad_maximum_fusion.3), calls=%async_computation | async-start | bytes 1048576 | tf_op jit(solution)/shard_map/all_to_all | solution.py:84
  18.3 19.4 %all-to-all-start.1 = ((bf16[128,8,512]{0,2,1:T(8,128)(2,1)}), bf16[128,8,512]{0,2,1:T(8,128)(2,1)S(1)}, u32[]{:S(2)}, u32[]{:S(2)}) async-start(bf16[128,8,512]{0,2,1:T(8,128)(2,1)} %pad_maximum_fusion.2), calls=%async_computation.1 | async-start | bytes 2097152 | tf_op jit(solution)/shard_map/all_to_all | solution.py:94
  25.7 18.3 %collective-permute-start = (bf16[1024,256]{1,0:T(8,128)(2,1)S(1)}, bf16[1024,256]{1,0:T(8,128)(2,1)}, u32[]{:S(2)}, u32[]{:S(2)}) collective-permute-start(bf16[1024,256]{1,0:T(8,128)(2,1)S(1)} %bitcast.265), channel_id=1, source_target_pairs={{0,16},{8,24},{16,32},{24,40},{32,48},{40,56},{48,64},{56,72},{64,... | collective-permute-start | bytes 1572872 | tf_op jit(solution)/shard_map/ppermute | solution.py:20
  28.6 26.0 %collective-permute-start.1 = (bf16[1024,256]{1,0:T(8,128)(2,1)S(1)}, bf16[1024,256]{1,0:T(8,128)(2,1)}, u32[]{:S(2)}, u32[]{:S(2)}) collective-permute-start(bf16[1024,256]{1,0:T(8,128)(2,1)S(1)} %bitcast.266), channel_id=1, source_target_pairs={{0,8},{8,16},{16,24},{24,32},{32,40},{40,48},{48,56},{56,64},{64,7... | collective-permute-start | bytes 1572872 | tf_op jit(solution)/shard_map/ppermute | solution.py:20
  38.7 17.2 %copy-start.1 = (pred[256,2304]{0,1:T(8,128)(4,1)S(1)}, pred[256,2304]{0,1:T(8,128)(4,1)}, u32[]{:S(2)}) copy-start(pred[256,2304]{0,1:T(8,128)(4,1)} %get-tuple-element.149) | copy-start | bytes 1769476
  81.3 17.0 %collective-permute-start.2 = (bf16[1024,256]{0,1:T(8,128)(2,1)}, bf16[1024,256]{0,1:T(8,128)(2,1)}, u32[]{:S(2)}, u32[]{:S(2)}) collective-permute-start(bf16[1024,256]{0,1:T(8,128)(2,1)} %get-tuple-element.110), channel_id=1, source_target_pairs={{8,0},{16,8},{24,16},{32,24},{40,32},{48,40},{56,48},{64,56},{72,6... | collective-permute-start | bytes 1572872 | tf_op jit(solution)/shard_map/ppermute | solution.py:20
  83.8 34.8 %collective-permute-start.3 = (bf16[1024,256]{0,1:T(8,128)(2,1)}, bf16[1024,256]{0,1:T(8,128)(2,1)}, u32[]{:S(2)}, u32[]{:S(2)}) collective-permute-start(bf16[1024,256]{0,1:T(8,128)(2,1)} %get-tuple-element.111), channel_id=1, source_target_pairs={{16,0},{24,8},{32,16},{40,24},{48,32},{56,40},{64,48},{72,56},{80,... | collective-permute-start | bytes 1572872 | tf_op jit(solution)/shard_map/ppermute | solution.py:20
  92.3 28.6 %all-to-all-start.2 = ((bf16[8,128,512]{2,1,0:T(8,128)(2,1)}), bf16[8,128,512]{2,1,0:T(8,128)(2,1)}, u32[]{:S(2)}, u32[]{:S(2)}) async-start(bf16[8,128,512]{2,1,0:T(8,128)(2,1)} %bitcast.249), calls=%async_computation.2 | async-start | bytes 2097152 | tf_op jit(solution)/shard_map/all_to_all | solution.py:148
  120.9 14.8 %all-to-all-start.3 = ((bf16[8,128,256]{1,2,0:T(8,128)(2,1)}), bf16[8,128,256]{1,2,0:T(8,128)(2,1)S(1)}, u32[]{:S(2)}, u32[]{:S(2)}) async-start(bf16[8,128,256]{1,2,0:T(8,128)(2,1)} %pad_maximum_fusion.4), calls=%async_computation.3 | async-start | bytes 1048576 | tf_op jit(solution)/shard_map/all_to_all | solution.py:156

commit v4 on v3

--- a/solution.py
+++ b/solution.py
@@ -98,7 +98,22 @@
     reach = MOST_BLK * BLK
     reach_groups = (reach - 1) // span_rows + 1
     first_place = lax.axis_index("fsdp") * span_rows
-    earlier = [passed_along(kv_seq, "fsdp", d) for d in range(reach_groups, 0, -1)]
+    core = lax.axis_index("sp") % 2
+    half = span_rows // 2
+    sibling = [(s, s ^ 1) for s in range(seq_width)]
+    my_half = lax.dynamic_slice_in_dim(kv_seq, core * half, half, 0)
+    received = [passed_along(my_half, "fsdp", d) for d in range(reach_groups, 0, -1)]
+    swapped = lax.ppermute(jnp.concatenate(received, axis=0), "sp", sibling)
+    earlier = []
+    for index, mine in enumerate(received):
+        theirs = swapped[index * half : (index + 1) * half]
+        earlier.append(
+            jnp.where(
+                core == 0,
+                jnp.concatenate([mine, theirs], axis=0),
+                jnp.concatenate([theirs, mine], axis=0),
+            )
+        )
     kv_all = jnp.concatenate(earlier + [kv_seq], axis=0)
     k_all = kv_all[:, :HD]
     v_all = kv_all[:, HD:]
@@ -134,13 +149,13 @@
         grad_k_all = grad_k_all.at[k_lo : k_lo + window].add(grad_k)
         grad_v_all = grad_v_all.at[k_lo : k_lo + window].add(grad_v)
     grad_kv_all = jnp.concatenate([grad_k_all, grad_v_all], axis=1)
+    earlier_parts = grad_kv_all[:own_start].reshape(reach_groups, 2, half, 2 * HD)
+    mine_part = lax.dynamic_index_in_dim(earlier_parts, core, 1, keepdims=False)
+    their_part = lax.dynamic_index_in_dim(earlier_parts, 1 - core, 1, keepdims=False)
+    pair_sum = mine_part + lax.ppermute(their_part, "sp", sibling)
     backs = [
-        passed_along(
-            grad_kv_all[lo : lo + span_rows].astype(jnp.bfloat16), "fsdp", -distance
-        )
-        for distance, lo in (
-            (d, (reach_groups - d) * span_rows) for d in range(1, reach_groups + 1)
-        )
+        passed_along(pair_sum[reach_groups - d].astype(jnp.bfloat16), "fsdp", -d)
+        for d in range(1, reach_groups + 1)
     ]
     attn_seq = jnp.concatenate(attn_parts, axis=0)
     dq_seq = jnp.concatenate(dq_parts, axis=0)
@@ -149,9 +164,13 @@
     back_all = back_all.reshape(tok_dev, seq_width, outgoing.shape[1])
     attn_out = back_all[:, :, :q_width].reshape(tok_dev, heads_q * HD)
     grad_queries = back_all[:, :, q_width:].reshape(tok_dev, heads_q * HD)
+    back_half = backs[0].astype(jnp.float32)
+    for back in backs[1:]:
+        back_half = back_half + back
     kv_sum = grad_kv_all[own_start:]
-    for back in backs:
-        kv_sum = kv_sum + back
+    kv_sum = lax.dynamic_update_slice_in_dim(
+        kv_sum, lax.dynamic_slice_in_dim(kv_sum, core * half, half, 0) + back_half, core * half, 0
+    )
     kv_sum = jnp.concatenate([kv_sum[:, :HD] * score_scale, kv_sum[:, HD:]], axis=1)
     kv_back = lax.all_to_all(
         kv_sum.astype(jnp.bfloat16), "sp", split_axis=0, concat_axis=1, tiled=True

time: 138 us -> 139 us (level)
  the two profiles are of different devices: /device:TPU:260 before, /device:TPU:384 now
where the time goes in v4:
time: 139 us
  starting transfers between devices  36.5 us (26%)
  waiting for transfers between devices  34.3 us (25%)
  local copies, waits for them, and re-layouts  24.2 us (17%)
  matrix products  21.3 us (15%)
  other arithmetic  21.1 us (15%)
  between operations  1.41 us (1%)
    ppermute x4, starting transfers between devices, passed_along(): lax.ppermute(value, axis, [(source, source + steps) for source in range(f...  15.9 us
    all_to_all x1, waiting for transfers between devices, local(): lax.all_to_all(outgoing, 'sp', split_axis=0, concat_axis=1, tiled=True)  13.4 us
    unnamed x51, local copies, waits for them, and re-layouts  8.2 us
    ppermute x4, waiting for transfers between devices, passed_along(): lax.ppermute(value, axis, [(source, source + steps) for source in range(f...  7.92 us
    and x2, other arithmetic, local(): (q_label[:, None] == k_label[None, :]) & (k_place[None, :] <= q_place[:,...  7.84 us
    all_to_all x1, waiting for transfers between devices, local(): lax.all_to_all(kv_sum.astype(jnp.bfloat16), 'sp', split_axis=0, concat_ax...  6.52 us
    all_to_all x1, waiting for transfers between devices, local(): lax.all_to_all(kv_pack, 'sp', split_axis=1, concat_axis=0, tiled=True)  6.38 us
    dynamic_slice x1, local copies, waits for them, and re-layouts, local(): mine_part = lax.dynamic_index_in_dim(earlier_parts, core, 1, keepdims=False)  4.53 us
  transfers between devices with their start and end apart: 10, of which 6 were waited for; matrix products, arithmetic and copies ran while one was open for 18% of the time, Pallas kernels for 0%

profile of v4, /device:TPU:384, one launch (start us, length us, event | category | flops | bytes accessed | tf_op | source)
XLA Modules:
  0.0 138.7 jit_solution(6456991293540146393)
XLA Ops:
  3.5 4.5 %all-to-all-start = ((bf16[128,8,256]{2,0,1:T(8,128)(2,1)}), bf16[128,8,256]{2,0,1:T(8,128)(2,1)S(1)}, u32[]{:S(2)}, u32[]{:S(2)}) async-start(bf16[128,8,256]{2,0,1:T(8,128)(2,1)} %pad_maximum_fusion.7), calls=%async_computation | async-start | bytes 1048576 | tf_op jit(solution)/shard_map/all_to_all | solution.py:84
  8.4 1.9 %convert_reduce_fusion = s32[3072]{0:T(1024)S(1)} fusion(s32[128]{0:T(128)S(1)} %multiply_reduce_fusion.4, s32[3072]{0:T(1024)S(1)} %iota_add_fusion), kind=kLoop, calls=%fused_computation.66 | loop fusion | flops 1176576 | bytes 25088 | tf_op jit(solution)/shard_map/reduce_sum | solution.py:30
  11.9 6.4 %all-to-all-done = bf16[128,8,256]{2,0,1:T(8,128)(2,1)S(1)} async-done(((bf16[128,8,256]{2,0,1:T(8,128)(2,1)}), bf16[128,8,256]{2,0,1:T(8,128)(2,1)S(1)}, u32[]{:S(2)}, u32[]{:S(2)}) %all-to-all-start) | async-done | bytes 524320 | tf_op jit(solution)/shard_map/all_to_all | solution.py:84
  18.3 3.6 %all-to-all-start.1 = ((bf16[128,8,512]{0,2,1:T(8,128)(2,1)}), bf16[128,8,512]{0,2,1:T(8,128)(2,1)S(1)}, u32[]{:S(2)}, u32[]{:S(2)}) async-start(bf16[128,8,512]{0,2,1:T(8,128)(2,1)} %pad_maximum_fusion.2), calls=%async_computation.1 | async-start | bytes 2097152 | tf_op jit(solution)/shard_map/all_to_all | solution.py:94
  21.9 3.4 %collective-permute-start.1 = (bf16[512,256]{1,0:T(8,128)(2,1)S(1)}, bf16[512,256]{1,0:T(8,128)(2,1)S(1)}, u32[]{:S(2)}, u32[]{:S(2)}) collective-permute-start(bf16[512,256]{1,0:T(8,128)(2,1)S(1)} %constant_dynamic-slice_fusion.2), channel_id=1, source_target_pairs={{0,8},{8,16},{16,24},{24,32},{32,40},{40,48},{48,56},{56,64},{64,7... | collective-permute-start | bytes 786440 | tf_op jit(solution)/shard_map/ppermute | solution.py:20
  25.4 4.6 %collective-permute-start = (bf16[512,256]{1,0:T(8,128)(2,1)S(1)}, bf16[512,256]{1,0:T(8,128)(2,1)S(1)}, u32[]{:S(2)}, u32[]{:S(2)}) collective-permute-start(bf16[512,256]{1,0:T(8,128)(2,1)S(1)} %constant_dynamic-slice_fusion.2), channel_id=1, source_target_pairs={{0,16},{8,24},{16,32},{24,40},{32,48},{40,56},{48,64},{56,72},{64,... | collective-permute-start | bytes 786440 | tf_op jit(solution)/shard_map/ppermute | solution.py:20
  30.0 3.8 %compare_and_fusion.2 = (pred[256,2304]{0,1:T(8,128)(4,1)}, pred[256,2304]{0,1:T(8,128)(4,1)S(1)}) fusion(s32[256]{0:T(256)S(1)} %get-tuple-element.140, s32[256]{0:T(256)S(1)} %get-tuple-element.137, s32[2304]{0:T(1024)S(1)} %get-tuple-element.133, s32[2304]{0:T(1024)S(1)} %get-tuple-element.129, s32[256]{0:T(256)S(1)} %get-tuple-element.138, ...), kind=kLoop, calls=%fused_computation.62 | loop fusion | flops 3538944 | bytes 1220608 | tf_op jit(solution)/shard_map/and | solution.py:136
  33.8 4.0 %collective-permute-done.1 = bf16[512,256]{1,0:T(8,128)(2,1)S(1)} collective-permute-done((bf16[512,256]{1,0:T(8,128)(2,1)S(1)}, bf16[512,256]{1,0:T(8,128)(2,1)S(1)}, u32[]{:S(2)}, u32[]{:S(2)}) %collective-permute-start.1) | collective-permute-done | bytes 262176 | tf_op jit(solution)/shard_map/ppermute | solution.py:20
  37.9 3.5 %collective-permute-done = bf16[512,256]{1,0:T(8,128)(2,1)S(1)} collective-permute-done((bf16[512,256]{1,0:T(8,128)(2,1)S(1)}, bf16[512,256]{1,0:T(8,128)(2,1)S(1)}, u32[]{:S(2)}, u32[]{:S(2)}) %collective-permute-start) | collective-permute-done | bytes 262176 | tf_op jit(solution)/shard_map/ppermute | solution.py:20
  42.2 1.9 %collective-permute-start.2 = (bf16[1024,256]{1,0:T(8,128)(2,1)}, bf16[1024,256]{1,0:T(8,128)(2,1)S(1)}, u32[]{:S(2)}, u32[]{:S(2)}) collective-permute-start(bf16[1024,256]{1,0:T(8,128)(2,1)} %pad_maximum_fusion.5), channel_id=1, source_target_pairs={{0,1},{1,0},{2,3},{3,2},{4,5},{5,4},{6,7},{7,6},{8,9},{9,8},{10,11... | collective-permute-start | bytes 1572872 | tf_op jit(solution)/shard_map/ppermute | solution.py:106
  44.1 4.0 %compare_and_fusion = (pred[256,2304]{0,1:T(8,128)(4,1)}, pred[256,2304]{0,1:T(8,128)(4,1)}) fusion(s32[256]{0:T(256)S(1)} %get-tuple-element.141, s32[256]{0:T(256)S(1)} %get-tuple-element.135, s32[2304]{0:T(1024)S(1)} %get-tuple-element.131, s32[2304]{0:T(1024)S(1)} %get-tuple-element.127, s32[256]{0:T(256)S(1)} %get-tuple-element.139, ...), kind=kLoop, calls=%fused_computation.60 | loop fusion | flops 3538944 | bytes 1220608 | tf_op jit(solution)/shard_map/and | solution.py:136
  74.5 1.5 %pad_maximum_fusion = f32[2048,256]{0,1:T(8,128)} fusion(f32[3072,128]{0,1:T(8,128)S(1)} %fusion.35, f32[3072,128]{0,1:T(8,128)S(1)} %fusion.29), kind=kLoop, calls=%fused_computation.64 | loop fusion | flops 524288 | bytes 5242880 | tf_op jit(solution)/shard_map/concatenate | solution.py:151
  76.0 4.1 %reshape.610 = f32[2,2,512,256]{2,1,0,3:T(2,128)} reshape(f32[2048,256]{0,1:T(8,128)} %pad_maximum_fusion) | data formatting | bytes 4194304 | tf_op jit(solution)/shard_map/reshape | solution.py:152
  80.0 4.5 %constant_dynamic-slice_fusion.1 = (f32[2,1,512,256]{2,1,0,3:T(1,128)S(1)}, f32[2,1,512,256]{2,1,0,3:T(1,128)S(1)}) fusion(f32[2,2,512,256]{2,1,0,3:T(2,128)} %reshape.610, s32[]{:T(128)S(6)} %select_n.58, s32[]{:T(128)S(6)} %select_n.59), kind=kLoop, calls=%fused_computation.128 | loop fusion | bytes 4194312 | tf_op jit(solution)/shard_map/jit(dynamic_index_in_dim)/dynamic_slice | solution.py:153
  84.8 2.9 %collective-permute-start.3 = (f32[2,512,256]{1,2,0:T(8,128)S(1)}, f32[2,512,256]{1,2,0:T(8,128)S(1)}, u32[]{:S(2)}, u32[]{:S(2)}) collective-permute-start(f32[2,512,256]{1,2,0:T(8,128)S(1)} %bitcast.292), channel_id=1, source_target_pairs={{0,1},{1,0},{2,3},{3,2},{4,5},{5,4},{6,7},{7,6},{8,9},{9,8},{10,11... | collective-permute-start | bytes 3145736 | tf_op jit(solution)/shard_map/ppermute | solution.py:155
  91.6 3.0 %collective-permute-start.4 = (bf16[512,256]{0,1:T(8,128)(2,1)}, bf16[512,256]{0,1:T(8,128)(2,1)}, u32[]{:S(2)}, u32[]{:S(2)}) collective-permute-start(bf16[512,256]{0,1:T(8,128)(2,1)} %get-tuple-element.122), channel_id=1, source_target_pairs={{8,0},{16,8},{24,16},{32,24},{40,32},{48,40},{56,48},{64,56},{72,6... | collective-permute-start | bytes 786440 | tf_op jit(solution)/shard_map/ppermute | solution.py:20
  94.6 4.8 %collective-permute-start.5 = (bf16[512,256]{0,1:T(8,128)(2,1)}, bf16[512,256]{0,1:T(8,128)(2,1)}, u32[]{:S(2)}, u32[]{:S(2)}) collective-permute-start(bf16[512,256]{0,1:T(8,128)(2,1)} %get-tuple-element.123), channel_id=1, source_target_pairs={{16,0},{24,8},{32,16},{40,24},{48,32},{56,40},{64,48},{72,56},{80,... | collective-permute-start | bytes 786440 | tf_op jit(solution)/shard_map/ppermute | solution.py:20
  99.5 1.2 maximum_maximum_fusion
  100.6 2.3 %copy.215 = bf16[1024,512]{1,0:T(8,128)(2,1)} copy(bf16[1024,512]{0,1:T(8,128)(2,1)} %maximum_maximum_fusion) | data formatting | bytes 2097152 | tf_op jit(solution)/shard_map/concatenate | solution.py:162
  102.9 4.2 %all-to-all-start.2 = ((bf16[8,128,512]{2,1,0:T(8,128)(2,1)}), bf16[8,128,512]{2,1,0:T(8,128)(2,1)}, u32[]{:S(2)}, u32[]{:S(2)}) async-start(bf16[8,128,512]{2,1,0:T(8,128)(2,1)} %bitcast.262), calls=%async_computation.2 | async-start | bytes 2097152 | tf_op jit(solution)/shard_map/all_to_all | solution.py:163
  109.8 13.4 %all-to-all-done.2 = bf16[8,128,512]{2,1,0:T(8,128)(2,1)} async-done(((bf16[8,128,512]{2,1,0:T(8,128)(2,1)}), bf16[8,128,512]{2,1,0:T(8,128)(2,1)}, u32[]{:S(2)}, u32[]{:S(2)}) %all-to-all-start.2) | async-done | bytes 1048608 | tf_op jit(solution)/shard_map/all_to_all | solution.py:163
  123.2 3.5 %all-to-all-start.3 = ((bf16[8,128,256]{1,2,0:T(8,128)(2,1)}), bf16[8,128,256]{1,2,0:T(8,128)(2,1)S(1)}, u32[]{:S(2)}, u32[]{:S(2)}) async-start(bf16[8,128,256]{1,2,0:T(8,128)(2,1)} %pad_maximum_fusion.8), calls=%async_computation.3 | async-start | bytes 1048576 | tf_op jit(solution)/shard_map/all_to_all | solution.py:175
  126.7 1.6 %copy.216 = bf16[8,128,512]{1,2,0:T(8,128)(2,1)S(1)} copy(bf16[8,128,512]{2,1,0:T(8,128)(2,1)} %all-to-all-done.2) | data formatting | bytes 2097152 | tf_op jit(solution)/shard_map/all_to_all | solution.py:163
  130.5 6.5 %all-to-all-done.3 = bf16[8,128,256]{1,2,0:T(8,128)(2,1)S(1)} async-done(((bf16[8,128,256]{1,2,0:T(8,128)(2,1)}), bf16[8,128,256]{1,2,0:T(8,128)(2,1)S(1)}, u32[]{:S(2)}, u32[]{:S(2)}) %all-to-all-start.3) | async-done | bytes 524320 | tf_op jit(solution)/shard_map/all_to_all | solution.py:175
  (127 shorter events, 42.1 us)
Async XLA Ops:
  0.6 7.3 %copy-start.21 = (s32[128]{0:T(128)S(1)}, s32[128]{0:T(128)}, u32[]{:S(2)}) copy-start(s32[128]{0:T(128)} %param.25) | copy-start | bytes 1540
  0.7 9.6 %copy-start.19 = (bf16[128,2048]{1,0:T(8,128)(2,1)S(1)}, bf16[128,2048]{1,0:T(8,128)(2,1)}, u32[]{:S(2)}) copy-start(bf16[128,2048]{1,0:T(8,128)(2,1)} %param.21) | copy-start | bytes 1572868
  1.5 9.0 %copy-start.20 = (bf16[128,2048]{1,0:T(8,128)(2,1)S(1)}, bf16[128,2048]{1,0:T(8,128)(2,1)}, u32[]{:S(2)}) copy-start(bf16[128,2048]{1,0:T(8,128)(2,1)} %param.24) | copy-start | bytes 1572868
  3.5 14.8 %all-to-all-start = ((bf16[128,8,256]{2,0,1:T(8,128)(2,1)}), bf16[128,8,256]{2,0,1:T(8,128)(2,1)S(1)}, u32[]{:S(2)}, u32[]{:S(2)}) async-start(bf16[128,8,256]{2,0,1:T(8,128)(2,1)} %pad_maximum_fusion.7), calls=%async_computation | async-start | bytes 1048576 | tf_op jit(solution)/shard_map/all_to_all | solution.py:84
  18.3 29.8 %all-to-all-start.1 = ((bf16[128,8,512]{0,2,1:T(8,128)(2,1)}), bf16[128,8,512]{0,2,1:T(8,128)(2,1)S(1)}, u32[]{:S(2)}, u32[]{:S(2)}) async-start(bf16[128,8,512]{0,2,1:T(8,128)(2,1)} %pad_maximum_fusion.2), calls=%async_computation.1 | async-start | bytes 2097152 | tf_op jit(solution)/shard_map/all_to_all | solution.py:94
  21.9 15.9 %collective-permute-start.1 = (bf16[512,256]{1,0:T(8,128)(2,1)S(1)}, bf16[512,256]{1,0:T(8,128)(2,1)S(1)}, u32[]{:S(2)}, u32[]{:S(2)}) collective-permute-start(bf16[512,256]{1,0:T(8,128)(2,1)S(1)} %constant_dynamic-slice_fusion.2), channel_id=1, source_target_pairs={{0,8},{8,16},{16,24},{24,32},{32,40},{40,48},{48,56},{56,64},{64,7... | collective-permute-start | bytes 786440 | tf_op jit(solution)/shard_map/ppermute | solution.py:20
  25.4 16.0 %collective-permute-start = (bf16[512,256]{1,0:T(8,128)(2,1)S(1)}, bf16[512,256]{1,0:T(8,128)(2,1)S(1)}, u32[]{:S(2)}, u32[]{:S(2)}) collective-permute-start(bf16[512,256]{1,0:T(8,128)(2,1)S(1)} %constant_dynamic-slice_fusion.2), channel_id=1, source_target_pairs={{0,16},{8,24},{16,32},{24,40},{32,48},{40,56},{48,64},{56,72},{64,... | collective-permute-start | bytes 786440 | tf_op jit(solution)/shard_map/ppermute | solution.py:20
  42.2 7.0 %collective-permute-start.2 = (bf16[1024,256]{1,0:T(8,128)(2,1)}, bf16[1024,256]{1,0:T(8,128)(2,1)S(1)}, u32[]{:S(2)}, u32[]{:S(2)}) collective-permute-start(bf16[1024,256]{1,0:T(8,128)(2,1)} %pad_maximum_fusion.5), channel_id=1, source_target_pairs={{0,1},{1,0},{2,3},{3,2},{4,5},{5,4},{6,7},{7,6},{8,9},{9,8},{10,11... | collective-permute-start | bytes 1572872 | tf_op jit(solution)/shard_map/ppermute | solution.py:106
  49.6 20.5 %copy-start.2 = (bf16[3072,256]{1,0:T(8,128)(2,1)}, bf16[3072,256]{1,0:T(8,128)(2,1)S(1)}, u32[]{:S(2)}) copy-start(bf16[3072,256]{1,0:T(8,128)(2,1)S(1)} %pad_maximum_fusion.1) | copy-start | bytes 4718596
  56.5 17.0 %copy-start.6 = (bf16[2,256,2304]{1,2,0:T(8,128)(2,1)}, bf16[2,256,2304]{1,2,0:T(8,128)(2,1)S(1)}, u32[]{:S(2)}) copy-start(bf16[2,256,2304]{1,2,0:T(8,128)(2,1)S(1)} %fusion.19) | copy-start | bytes 7077892
  60.7 11.4 %copy-start.8 = (bf16[2,256,2304]{1,2,0:T(8,128)(2,1)}, bf16[2,256,2304]{1,2,0:T(8,128)(2,1)S(1)}, u32[]{:S(2)}) copy-start(bf16[2,256,2304]{1,2,0:T(8,128)(2,1)S(1)} %fusion.18) | copy-start | bytes 7077892
  66.6 3.4 %copy-start.14 = (bf16[128,2,256]{2,0,1:T(8,128)(2,1)}, bf16[128,2,256]{2,0,1:T(8,128)(2,1)S(1)}, u32[]{:S(2)}) copy-start(bf16[128,2,256]{2,0,1:T(8,128)(2,1)S(1)} %convolution_convert_fusion.2) | copy-start | bytes 393220
  80.0 7.7 %copy-start.3 = (bf16[3072,256]{1,0:T(8,128)(2,1)S(1)}, bf16[3072,256]{1,0:T(8,128)(2,1)}, u32[]{:S(2)}) copy-start(bf16[3072,256]{1,0:T(8,128)(2,1)} %copy-done.2) | copy-start | bytes 4718596
  80.0 7.7 %copy-start.7 = (bf16[2,256,2304]{1,2,0:T(8,128)(2,1)S(1)}, bf16[2,256,2304]{1,2,0:T(8,128)(2,1)}, u32[]{:S(2)}) copy-start(bf16[2,256,2304]{1,2,0:T(8,128)(2,1)} %copy-done.6) | copy-start | bytes 7077892
  84.6 3.7 %copy-start.9 = (bf16[2,256,2304]{1,2,0:T(8,128)(2,1)S(1)}, bf16[2,256,2304]{1,2,0:T(8,128)(2,1)}, u32[]{:S(2)}) copy-start(bf16[2,256,2304]{1,2,0:T(8,128)(2,1)} %copy-done.8) | copy-start | bytes 7077892
  84.8 4.1 %copy-start.5 = (bf16[2,256,2304]{1,2,0:T(8,128)(2,1)S(1)}, bf16[2,256,2304]{1,2,0:T(8,128)(2,1)}, u32[]{:S(2)}) copy-start(bf16[2,256,2304]{1,2,0:T(8,128)(2,1)} %copy-done.4) | copy-start | bytes 7077892
  84.8 5.7 %collective-permute-start.3 = (f32[2,512,256]{1,2,0:T(8,128)S(1)}, f32[2,512,256]{1,2,0:T(8,128)S(1)}, u32[]{:S(2)}, u32[]{:S(2)}) collective-permute-start(f32[2,512,256]{1,2,0:T(8,128)S(1)} %bitcast.292), channel_id=1, source_target_pairs={{0,1},{1,0},{2,3},{3,2},{4,5},{5,4},{6,7},{7,6},{8,9},{9,8},{10,11... | collective-permute-start | bytes 3145736 | tf_op jit(solution)/shard_map/ppermute | solution.py:155
  90.5 9.0 %copy-start.13 = (bf16[128,2,256]{2,0,1:T(8,128)(2,1)S(1)}, bf16[128,2,256]{2,0,1:T(8,128)(2,1)}, u32[]{:S(2)}) copy-start(bf16[128,2,256]{2,0,1:T(8,128)(2,1)} %copy-done.12) | copy-start | bytes 393220
  90.5 9.0 %copy-start.15 = (bf16[128,2,256]{2,0,1:T(8,128)(2,1)S(1)}, bf16[128,2,256]{2,0,1:T(8,128)(2,1)}, u32[]{:S(2)}) copy-start(bf16[128,2,256]{2,0,1:T(8,128)(2,1)} %copy-done.14) | copy-start | bytes 393220
  91.6 16.1 %collective-permute-start.4 = (bf16[512,256]{0,1:T(8,128)(2,1)}, bf16[512,256]{0,1:T(8,128)(2,1)}, u32[]{:S(2)}, u32[]{:S(2)}) collective-permute-start(bf16[512,256]{0,1:T(8,128)(2,1)} %get-tuple-element.122), channel_id=1, source_target_pairs={{8,0},{16,8},{24,16},{32,24},{40,32},{48,40},{56,48},{64,56},{72,6... | collective-permute-start | bytes 786440 | tf_op jit(solution)/shard_map/ppermute | solution.py:20
  94.6 13.1 %collective-permute-start.5 = (bf16[512,256]{0,1:T(8,128)(2,1)}, bf16[512,256]{0,1:T(8,128)(2,1)}, u32[]{:S(2)}, u32[]{:S(2)}) collective-permute-start(bf16[512,256]{0,1:T(8,128)(2,1)} %get-tuple-element.123), channel_id=1, source_target_pairs={{16,0},{24,8},{32,16},{40,24},{48,32},{56,40},{64,48},{72,56},{80,... | collective-permute-start | bytes 786440 | tf_op jit(solution)/shard_map/ppermute | solution.py:20
  102.9 20.3 %all-to-all-start.2 = ((bf16[8,128,512]{2,1,0:T(8,128)(2,1)}), bf16[8,128,512]{2,1,0:T(8,128)(2,1)}, u32[]{:S(2)}, u32[]{:S(2)}) async-start(bf16[8,128,512]{2,1,0:T(8,128)(2,1)} %bitcast.262), calls=%async_computation.2 | async-start | bytes 2097152 | tf_op jit(solution)/shard_map/all_to_all | solution.py:163
  123.2 13.8 %all-to-all-start.3 = ((bf16[8,128,256]{1,2,0:T(8,128)(2,1)}), bf16[8,128,256]{1,2,0:T(8,128)(2,1)S(1)}, u32[]{:S(2)}, u32[]{:S(2)}) async-start(bf16[8,128,256]{1,2,0:T(8,128)(2,1)} %pad_maximum_fusion.8), calls=%async_computation.3 | async-start | bytes 1048576 | tf_op jit(solution)/shard_map/all_to_all | solution.py:175
  128.4 10.2 %copy-start.1 = (bf16[128,512]{1,0:T(8,128)(2,1)S(1)}, bf16[128,512]{1,0:T(8,128)(2,1)}, u32[]{:S(2)}) copy-start(bf16[128,512]{1,0:T(8,128)(2,1)} %param.22) | copy-start | bytes 393220
  (8 other events, 9.3 us)

commit v5 on v4

--- a/solution.py
+++ b/solution.py
@@ -149,9 +149,14 @@
         grad_k_all = grad_k_all.at[k_lo : k_lo + window].add(grad_k)
         grad_v_all = grad_v_all.at[k_lo : k_lo + window].add(grad_v)
     grad_kv_all = jnp.concatenate([grad_k_all, grad_v_all], axis=1)
-    earlier_parts = grad_kv_all[:own_start].reshape(reach_groups, 2, half, 2 * HD)
-    mine_part = lax.dynamic_index_in_dim(earlier_parts, core, 1, keepdims=False)
-    their_part = lax.dynamic_index_in_dim(earlier_parts, 1 - core, 1, keepdims=False)
+    low_rows = jnp.stack(
+        [grad_kv_all[g * span_rows : g * span_rows + half] for g in range(reach_groups)]
+    )
+    high_rows = jnp.stack(
+        [grad_kv_all[g * span_rows + half : (g + 1) * span_rows] for g in range(reach_groups)]
+    )
+    mine_part = jnp.where(core == 0, low_rows, high_rows)
+    their_part = jnp.where(core == 0, high_rows, low_rows)
     pair_sum = mine_part + lax.ppermute(their_part, "sp", sibling)
     backs = [
         passed_along(pair_sum[reach_groups - d].astype(jnp.bfloat16), "fsdp", -d)

time: 139 us -> 127 us (0.914)
  local copies, waits for them, and re-layouts: 24.2 us -> 14.2 us
  starting transfers between devices: 36.5 us -> 34.1 us
  waiting for transfers between devices: 34.3 us -> 36.1 us
    dynamic_slice x2 -> x0, local copies, waits for them, and re-layouts: 4.73 us -> none  [the longest x1 4.53 us: local(): mine_part = lax.dynamic_index_in_dim(earlier_parts, core, 1, keepdims=False)]
    reshape x1 -> x0, local copies, waits for them, and re-layouts: 4.05 us -> none  [local(): grad_kv_all[:own_start].reshape(reach_groups, 2, half, 2 * HD)]
    ppermute x4, waiting for transfers between devices: 7.92 us -> 10.9 us  [passed_along(): lax.ppermute(value, axis, [(source, source + steps) for source in range(f...]
    unnamed x51 -> x21, local copies, waits for them, and re-layouts: 8.2 us -> 5.92 us
    ppermute x4, starting transfers between devices: 15.9 us -> 13.8 us  [passed_along(): lax.ppermute(value, axis, [(source, source + steps) for source in range(f...]
    all_to_all x1, waiting for transfers between devices: 13.4 us -> 12 us  [local(): lax.all_to_all(outgoing, 'sp', split_axis=0, concat_axis=1, tiled=True)]
  transfers between devices with their start and end apart: 10 -> 10, of which waited for: 6 -> 7; matrix products, arithmetic and copies ran while one was open for 18% -> 20% of each run, Pallas kernels for 0% -> 0%
where the time goes in v5:
time: 127 us
  waiting for transfers between devices  36.1 us (28%)
  starting transfers between devices  34.1 us (27%)
  matrix products  21.2 us (17%)
  other arithmetic  20 us (16%)
  local copies, waits for them, and re-layouts  14.2 us (11%)
    ppermute x4, starting transfers between devices, passed_along(): lax.ppermute(value, axis, [(source, source + steps) for source in range(f...  13.8 us
    all_to_all x1, waiting for transfers between devices, local(): lax.all_to_all(outgoing, 'sp', split_axis=0, concat_axis=1, tiled=True)  12 us
    ppermute x4, waiting for transfers between devices, passed_along(): lax.ppermute(value, axis, [(source, source + steps) for source in range(f...  10.9 us
    and x2, other arithmetic, local(): (q_label[:, None] == k_label[None, :]) & (k_place[None, :] <= q_place[:,...  7.72 us
    all_to_all x1, waiting for transfers between devices, local(): lax.all_to_all(kv_sum.astype(jnp.bfloat16), 'sp', split_axis=0, concat_ax...  6.52 us
    all_to_all x1, waiting for transfers between devices, local(): lax.all_to_all(kv_pack, 'sp', split_axis=1, concat_axis=0, tiled=True)  6.37 us
    unnamed x21, local copies, waits for them, and re-layouts  5.92 us
    all_to_all x1, starting transfers between devices, local(): lax.all_to_all(kv_pack, 'sp', split_axis=1, concat_axis=0, tiled=True)  4.47 us
  transfers between devices with their start and end apart: 10, of which 7 were waited for; matrix products, arithmetic and copies ran while one was open for 20% of the time, Pallas kernels for 0%

profile of v5, /device:TPU:384, one launch (start us, length us, event | category | flops | bytes accessed | tf_op | source)
XLA Modules:
  0.0 126.7 jit_solution(4724942034896243324)
XLA Ops:
  3.5 4.5 %all-to-all-start = ((bf16[128,8,256]{2,0,1:T(8,128)(2,1)}), bf16[128,8,256]{2,0,1:T(8,128)(2,1)S(1)}, u32[]{:S(2)}, u32[]{:S(2)}) async-start(bf16[128,8,256]{2,0,1:T(8,128)(2,1)} %pad_maximum_fusion.8), calls=%async_computation | async-start | bytes 1048576 | tf_op jit(solution)/shard_map/all_to_all | solution.py:84
  8.4 1.9 %convert_reduce_fusion = s32[3072]{0:T(1024)S(1)} fusion(s32[128]{0:T(128)S(1)} %multiply_reduce_fusion.4, s32[3072]{0:T(1024)S(1)} %iota_add_fusion), kind=kLoop, calls=%fused_computation.73 | loop fusion | flops 1176576 | bytes 25088 | tf_op jit(solution)/shard_map/reduce_sum | solution.py:30
  12.0 6.4 %all-to-all-done = bf16[128,8,256]{2,0,1:T(8,128)(2,1)S(1)} async-done(((bf16[128,8,256]{2,0,1:T(8,128)(2,1)}), bf16[128,8,256]{2,0,1:T(8,128)(2,1)S(1)}, u32[]{:S(2)}, u32[]{:S(2)}) %all-to-all-start) | async-done | bytes 524320 | tf_op jit(solution)/shard_map/all_to_all | solution.py:84
  18.3 3.6 %all-to-all-start.1 = ((bf16[128,8,512]{0,2,1:T(8,128)(2,1)}), bf16[128,8,512]{0,2,1:T(8,128)(2,1)S(1)}, u32[]{:S(2)}, u32[]{:S(2)}) async-start(bf16[128,8,512]{0,2,1:T(8,128)(2,1)} %pad_maximum_fusion.1), calls=%async_computation.1 | async-start | bytes 2097152 | tf_op jit(solution)/shard_map/all_to_all | solution.py:94
  21.9 5.0 %collective-permute-start = (bf16[512,256]{1,0:T(8,128)(2,1)S(1)}, bf16[512,256]{1,0:T(8,128)(2,1)S(1)}, u32[]{:S(2)}, u32[]{:S(2)}) collective-permute-start(bf16[512,256]{1,0:T(8,128)(2,1)S(1)} %constant_dynamic-slice_fusion), channel_id=1, source_target_pairs={{0,16},{8,24},{16,32},{24,40},{32,48},{40,56},{48,64},{56,72},{64,... | collective-permute-start | bytes 786440 | tf_op jit(solution)/shard_map/ppermute | solution.py:20
  26.9 2.5 %collective-permute-start.1 = (bf16[512,256]{1,0:T(8,128)(2,1)S(1)}, bf16[512,256]{1,0:T(8,128)(2,1)S(1)}, u32[]{:S(2)}, u32[]{:S(2)}) collective-permute-start(bf16[512,256]{1,0:T(8,128)(2,1)S(1)} %constant_dynamic-slice_fusion), channel_id=1, source_target_pairs={{0,8},{8,16},{16,24},{24,32},{32,40},{40,48},{48,56},{56,64},{64,7... | collective-permute-start | bytes 786440 | tf_op jit(solution)/shard_map/ppermute | solution.py:20
  29.4 3.9 %compare_and_fusion.2 = (pred[256,2304]{0,1:T(8,128)(4,1)S(1)}, pred[256,2304]{0,1:T(8,128)(4,1)}) fusion(s32[256]{0:T(256)S(1)} %get-tuple-element.142, s32[256]{0:T(256)S(1)} %get-tuple-element.139, s32[2304]{0:T(1024)S(1)} %get-tuple-element.135, s32[2304]{0:T(1024)S(1)} %get-tuple-element.131, s32[256]{0:T(256)S(1)} %get-tuple-element.140, ...), kind=kLoop, calls=%fused_computation.70 | loop fusion | flops 3538944 | bytes 1220608 | tf_op jit(solution)/shard_map/and | solution.py:136
  33.3 2.9 %collective-permute-done = bf16[512,256]{1,0:T(8,128)(2,1)S(1)} collective-permute-done((bf16[512,256]{1,0:T(8,128)(2,1)S(1)}, bf16[512,256]{1,0:T(8,128)(2,1)S(1)}, u32[]{:S(2)}, u32[]{:S(2)}) %collective-permute-start) | collective-permute-done | bytes 262176 | tf_op jit(solution)/shard_map/ppermute | solution.py:20
  36.1 6.1 %collective-permute-done.1 = bf16[512,256]{1,0:T(8,128)(2,1)S(1)} collective-permute-done((bf16[512,256]{1,0:T(8,128)(2,1)S(1)}, bf16[512,256]{1,0:T(8,128)(2,1)S(1)}, u32[]{:S(2)}, u32[]{:S(2)}) %collective-permute-start.1) | collective-permute-done | bytes 262176 | tf_op jit(solution)/shard_map/ppermute | solution.py:20
  43.1 1.9 %collective-permute-start.2 = (bf16[1024,256]{1,0:T(8,128)(2,1)}, bf16[1024,256]{1,0:T(8,128)(2,1)}, u32[]{:S(2)}, u32[]{:S(2)}) collective-permute-start(bf16[1024,256]{1,0:T(8,128)(2,1)} %pad_maximum_fusion.5), channel_id=1, source_target_pairs={{0,1},{1,0},{2,3},{3,2},{4,5},{5,4},{6,7},{7,6},{8,9},{9,8},{10,11... | collective-permute-start | bytes 1572872 | tf_op jit(solution)/shard_map/ppermute | solution.py:106
  45.0 3.9 %compare_and_fusion = (pred[256,2304]{0,1:T(8,128)(4,1)S(1)}, pred[256,2304]{0,1:T(8,128)(4,1)}) fusion(s32[256]{0:T(256)S(1)} %get-tuple-element.143, s32[256]{0:T(256)S(1)} %get-tuple-element.137, s32[2304]{0:T(1024)S(1)} %get-tuple-element.133, s32[2304]{0:T(1024)S(1)} %get-tuple-element.129, s32[256]{0:T(256)S(1)} %get-tuple-element.141, ...), kind=kLoop, calls=%fused_computation.68 | loop fusion | flops 3538944 | bytes 1220608 | tf_op jit(solution)/shard_map/and | solution.py:136
  64.1 1.2 convolution_convert_fusion
  65.3 1.1 fusion.35
  74.9 2.4 %collective-permute-start.3 = (f32[2,512,256]{1,2,0:T(8,128)S(1)}, f32[2,512,256]{1,2,0:T(8,128)S(1)}, u32[]{:S(2)}, u32[]{:S(2)}) collective-permute-start(f32[2,512,256]{1,2,0:T(8,128)S(1)} %fusion.41), channel_id=1, source_target_pairs={{0,1},{1,0},{2,3},{3,2},{4,5},{5,4},{6,7},{7,6},{8,9},{9,8},{10,11... | collective-permute-start | bytes 3145736 | tf_op jit(solution)/shard_map/ppermute | solution.py:160
  80.9 2.3 %collective-permute-start.4 = (bf16[512,256]{0,1:T(8,128)(2,1)}, bf16[512,256]{0,1:T(8,128)(2,1)S(1)}, u32[]{:S(2)}, u32[]{:S(2)}) collective-permute-start(bf16[512,256]{0,1:T(8,128)(2,1)} %get-tuple-element.124), channel_id=1, source_target_pairs={{8,0},{16,8},{24,16},{32,24},{40,32},{48,40},{56,48},{64,56},{72,6... | collective-permute-start | bytes 786440 | tf_op jit(solution)/shard_map/ppermute | solution.py:20
  83.1 4.1 %collective-permute-start.5 = (bf16[512,256]{0,1:T(8,128)(2,1)}, bf16[512,256]{0,1:T(8,128)(2,1)}, u32[]{:S(2)}, u32[]{:S(2)}) collective-permute-start(bf16[512,256]{0,1:T(8,128)(2,1)} %get-tuple-element.125), channel_id=1, source_target_pairs={{16,0},{24,8},{32,16},{40,24},{48,32},{56,40},{64,48},{72,56},{80,... | collective-permute-start | bytes 786440 | tf_op jit(solution)/shard_map/ppermute | solution.py:20
  87.2 1.2 maximum_maximum_fusion
  88.4 2.3 %copy.207 = bf16[1024,512]{1,0:T(8,128)(2,1)} copy(bf16[1024,512]{0,1:T(8,128)(2,1)} %maximum_maximum_fusion) | data formatting | bytes 2097152 | tf_op jit(solution)/shard_map/concatenate | solution.py:167
  90.7 4.5 %all-to-all-start.2 = ((bf16[8,128,512]{2,1,0:T(8,128)(2,1)}), bf16[8,128,512]{2,1,0:T(8,128)(2,1)}, u32[]{:S(2)}, u32[]{:S(2)}) async-start(bf16[8,128,512]{2,1,0:T(8,128)(2,1)} %bitcast.261), calls=%async_computation.2 | async-start | bytes 2097152 | tf_op jit(solution)/shard_map/all_to_all | solution.py:168
  95.3 1.9 %collective-permute-done.4 = bf16[512,256]{0,1:T(8,128)(2,1)S(1)} collective-permute-done((bf16[512,256]{0,1:T(8,128)(2,1)}, bf16[512,256]{0,1:T(8,128)(2,1)S(1)}, u32[]{:S(2)}, u32[]{:S(2)}) %collective-permute-start.4) | collective-permute-done | bytes 262176 | tf_op jit(solution)/shard_map/ppermute | solution.py:20
  99.2 12.0 %all-to-all-done.2 = bf16[8,128,512]{2,1,0:T(8,128)(2,1)} async-done(((bf16[8,128,512]{2,1,0:T(8,128)(2,1)}), bf16[8,128,512]{2,1,0:T(8,128)(2,1)}, u32[]{:S(2)}, u32[]{:S(2)}) %all-to-all-start.2) | async-done | bytes 1048608 | tf_op jit(solution)/shard_map/all_to_all | solution.py:168
  111.2 3.5 %all-to-all-start.3 = ((bf16[8,128,256]{1,2,0:T(8,128)(2,1)}), bf16[8,128,256]{1,2,0:T(8,128)(2,1)S(1)}, u32[]{:S(2)}, u32[]{:S(2)}) async-start(bf16[8,128,256]{1,2,0:T(8,128)(2,1)} %pad_maximum_fusion.9), calls=%async_computation.3 | async-start | bytes 1048576 | tf_op jit(solution)/shard_map/all_to_all | solution.py:180
  114.7 1.6 %copy.208 = bf16[8,128,512]{1,2,0:T(8,128)(2,1)S(1)} copy(bf16[8,128,512]{2,1,0:T(8,128)(2,1)} %all-to-all-done.2) | data formatting | bytes 2097152 | tf_op jit(solution)/shard_map/all_to_all | solution.py:168
  118.5 6.5 %all-to-all-done.3 = bf16[8,128,256]{1,2,0:T(8,128)(2,1)S(1)} async-done(((bf16[8,128,256]{1,2,0:T(8,128)(2,1)}), bf16[8,128,256]{1,2,0:T(8,128)(2,1)S(1)}, u32[]{:S(2)}, u32[]{:S(2)}) %all-to-all-start.3) | async-done | bytes 524320 | tf_op jit(solution)/shard_map/all_to_all | solution.py:180
  (95 shorter events, 38.5 us)
Async XLA Ops:
  0.6 0.9 copy-start
  0.6 7.3 %copy-start.6 = (s32[128]{0:T(128)S(1)}, s32[128]{0:T(128)}, u32[]{:S(2)}) copy-start(s32[128]{0:T(128)} %param.25) | copy-start | bytes 1540
  0.7 9.6 %copy-start.4 = (bf16[128,2048]{1,0:T(8,128)(2,1)S(1)}, bf16[128,2048]{1,0:T(8,128)(2,1)}, u32[]{:S(2)}) copy-start(bf16[128,2048]{1,0:T(8,128)(2,1)} %param.21) | copy-start | bytes 1572868
  1.5 9.0 %copy-start.5 = (bf16[128,2048]{1,0:T(8,128)(2,1)S(1)}, bf16[128,2048]{1,0:T(8,128)(2,1)}, u32[]{:S(2)}) copy-start(bf16[128,2048]{1,0:T(8,128)(2,1)} %param.24) | copy-start | bytes 1572868
  3.5 14.8 %all-to-all-start = ((bf16[128,8,256]{2,0,1:T(8,128)(2,1)}), bf16[128,8,256]{2,0,1:T(8,128)(2,1)S(1)}, u32[]{:S(2)}, u32[]{:S(2)}) async-start(bf16[128,8,256]{2,0,1:T(8,128)(2,1)} %pad_maximum_fusion.8), calls=%async_computation | async-start | bytes 1048576 | tf_op jit(solution)/shard_map/all_to_all | solution.py:84
  18.3 30.6 %all-to-all-start.1 = ((bf16[128,8,512]{0,2,1:T(8,128)(2,1)}), bf16[128,8,512]{0,2,1:T(8,128)(2,1)S(1)}, u32[]{:S(2)}, u32[]{:S(2)}) async-start(bf16[128,8,512]{0,2,1:T(8,128)(2,1)} %pad_maximum_fusion.1), calls=%async_computation.1 | async-start | bytes 2097152 | tf_op jit(solution)/shard_map/all_to_all | solution.py:94
  21.9 14.2 %collective-permute-start = (bf16[512,256]{1,0:T(8,128)(2,1)S(1)}, bf16[512,256]{1,0:T(8,128)(2,1)S(1)}, u32[]{:S(2)}, u32[]{:S(2)}) collective-permute-start(bf16[512,256]{1,0:T(8,128)(2,1)S(1)} %constant_dynamic-slice_fusion), channel_id=1, source_target_pairs={{0,16},{8,24},{16,32},{24,40},{32,48},{40,56},{48,64},{56,72},{64,... | collective-permute-start | bytes 786440 | tf_op jit(solution)/shard_map/ppermute | solution.py:20
  26.9 15.4 %collective-permute-start.1 = (bf16[512,256]{1,0:T(8,128)(2,1)S(1)}, bf16[512,256]{1,0:T(8,128)(2,1)S(1)}, u32[]{:S(2)}, u32[]{:S(2)}) collective-permute-start(bf16[512,256]{1,0:T(8,128)(2,1)S(1)} %constant_dynamic-slice_fusion), channel_id=1, source_target_pairs={{0,8},{8,16},{16,24},{24,32},{32,40},{40,48},{48,56},{56,64},{64,7... | collective-permute-start | bytes 786440 | tf_op jit(solution)/shard_map/ppermute | solution.py:20
  43.1 6.8 %collective-permute-start.2 = (bf16[1024,256]{1,0:T(8,128)(2,1)}, bf16[1024,256]{1,0:T(8,128)(2,1)}, u32[]{:S(2)}, u32[]{:S(2)}) collective-permute-start(bf16[1024,256]{1,0:T(8,128)(2,1)} %pad_maximum_fusion.5), channel_id=1, source_target_pairs={{0,1},{1,0},{2,3},{3,2},{4,5},{5,4},{6,7},{7,6},{8,9},{9,8},{10,11... | collective-permute-start | bytes 1572872 | tf_op jit(solution)/shard_map/ppermute | solution.py:106
  51.0 1.1 copy-start.2
  58.0 1.1 copy-start.3
  74.9 4.7 %collective-permute-start.3 = (f32[2,512,256]{1,2,0:T(8,128)S(1)}, f32[2,512,256]{1,2,0:T(8,128)S(1)}, u32[]{:S(2)}, u32[]{:S(2)}) collective-permute-start(f32[2,512,256]{1,2,0:T(8,128)S(1)} %fusion.41), channel_id=1, source_target_pairs={{0,1},{1,0},{2,3},{3,2},{4,5},{5,4},{6,7},{7,6},{8,9},{9,8},{10,11... | collective-permute-start | bytes 3145736 | tf_op jit(solution)/shard_map/ppermute | solution.py:160
  80.9 16.3 %collective-permute-start.4 = (bf16[512,256]{0,1:T(8,128)(2,1)}, bf16[512,256]{0,1:T(8,128)(2,1)S(1)}, u32[]{:S(2)}, u32[]{:S(2)}) collective-permute-start(bf16[512,256]{0,1:T(8,128)(2,1)} %get-tuple-element.124), channel_id=1, source_target_pairs={{8,0},{16,8},{24,16},{32,24},{40,32},{48,40},{56,48},{64,56},{72,6... | collective-permute-start | bytes 786440 | tf_op jit(solution)/shard_map/ppermute | solution.py:20
  83.1 14.0 %collective-permute-start.5 = (bf16[512,256]{0,1:T(8,128)(2,1)}, bf16[512,256]{0,1:T(8,128)(2,1)}, u32[]{:S(2)}, u32[]{:S(2)}) collective-permute-start(bf16[512,256]{0,1:T(8,128)(2,1)} %get-tuple-element.125), channel_id=1, source_target_pairs={{16,0},{24,8},{32,16},{40,24},{48,32},{56,40},{64,48},{72,56},{80,... | collective-permute-start | bytes 786440 | tf_op jit(solution)/shard_map/ppermute | solution.py:20
  90.7 20.5 %all-to-all-start.2 = ((bf16[8,128,512]{2,1,0:T(8,128)(2,1)}), bf16[8,128,512]{2,1,0:T(8,128)(2,1)}, u32[]{:S(2)}, u32[]{:S(2)}) async-start(bf16[8,128,512]{2,1,0:T(8,128)(2,1)} %bitcast.261), calls=%async_computation.2 | async-start | bytes 2097152 | tf_op jit(solution)/shard_map/all_to_all | solution.py:168
  111.2 13.8 %all-to-all-start.3 = ((bf16[8,128,256]{1,2,0:T(8,128)(2,1)}), bf16[8,128,256]{1,2,0:T(8,128)(2,1)S(1)}, u32[]{:S(2)}, u32[]{:S(2)}) async-start(bf16[8,128,256]{1,2,0:T(8,128)(2,1)} %pad_maximum_fusion.9), calls=%async_computation.3 | async-start | bytes 1048576 | tf_op jit(solution)/shard_map/all_to_all | solution.py:180
  116.5 10.2 %copy-start.1 = (bf16[128,512]{1,0:T(8,128)(2,1)S(1)}, bf16[128,512]{1,0:T(8,128)(2,1)}, u32[]{:S(2)}) copy-start(bf16[128,512]{1,0:T(8,128)(2,1)} %param.22) | copy-start | bytes 393220

commit v6 on v5

--- a/solution.py
+++ b/solution.py
@@ -39,7 +39,7 @@
     return shaped.reshape(tokens_here, head_count * copies * HD)
 
 
-def block_pass(q_block, g_block, k_win, v_win, allowed, score_scale):
+def forward_pass(q_block, k_win, v_win, allowed, score_scale):
     scores = (
         jnp.einsum("qhd,kd->hqk", q_block, k_win, preferred_element_type=jnp.float32)
         * score_scale
@@ -53,6 +53,10 @@
     attn_block = jnp.einsum(
         "hqk,kd->qhd", probs_bf, v_win, preferred_element_type=jnp.float32
     ).astype(jnp.bfloat16)
+    return weights, probs_bf, attn_block
+
+
+def backward_pass(q_block, g_block, k_win, v_win, weights, probs_bf, attn_block, score_scale):
     row_delta = jnp.transpose(jnp.sum(lifted(g_block) * lifted(attn_block), axis=-1), (1, 0))
     dprobs = jnp.einsum("qhd,kd->hqk", g_block, v_win, preferred_element_type=jnp.float32)
     dscores = (weights * (dprobs - row_delta[..., None])).astype(jnp.bfloat16)
@@ -62,7 +66,7 @@
     ).astype(jnp.bfloat16)
     grad_k = jnp.einsum("hqk,qhd->kd", dscores, q_block, preferred_element_type=jnp.float32)
     grad_v = jnp.einsum("hqk,qhd->kd", probs_bf, g_block, preferred_element_type=jnp.float32)
-    return attn_block, dq_block, grad_k, grad_v
+    return dq_block, grad_k, grad_v
 
 
 def local(queries, key_rows, value_rows, out_grad, doc_lengths):
@@ -84,17 +88,9 @@
     kv_seq = lax.all_to_all(kv_pack, "sp", split_axis=1, concat_axis=0, tiled=True)
     kv_seq = kv_seq.reshape(span_rows, 2 * HD)
     q_width = local_q * HD
-    qg_pack = jnp.concatenate(
-        [
-            queries.reshape(tok_dev, seq_width, q_width),
-            out_grad.reshape(tok_dev, seq_width, q_width),
-        ],
-        axis=2,
-    )
-    qg_seq = lax.all_to_all(qg_pack, "sp", split_axis=1, concat_axis=0, tiled=True)
-    qg_seq = qg_seq.reshape(span_rows, 2 * q_width)
-    q_seq = qg_seq[:, :q_width]
-    g_seq = qg_seq[:, q_width:]
+    q_seq = lax.all_to_all(
+        queries.reshape(tok_dev, seq_width, q_width), "sp", split_axis=1, concat_axis=0, tiled=True
+    ).reshape(span_rows, q_width)
     reach = MOST_BLK * BLK
     reach_groups = (reach - 1) // span_rows + 1
     first_place = lax.axis_index("fsdp") * span_rows
@@ -115,6 +111,11 @@
             )
         )
     kv_all = jnp.concatenate(earlier + [kv_seq], axis=0)
+    q_seq, kv_all, g_pack = lax.optimization_barrier(
+        (q_seq, kv_all, out_grad.reshape(tok_dev, seq_width, q_width))
+    )
+    g_seq = lax.all_to_all(g_pack, "sp", split_axis=1, concat_axis=0, tiled=True)
+    g_seq = g_seq.reshape(span_rows, q_width)
     k_all = kv_all[:, :HD]
     v_all = kv_all[:, HD:]
     base_place = first_place - reach_groups * span_rows
@@ -125,7 +126,7 @@
     own_start = reach_groups * span_rows
     grad_k_all = jnp.zeros((key_count, HD), jnp.float32)
     grad_v_all = jnp.zeros((key_count, HD), jnp.float32)
-    attn_parts, dq_parts = [], []
+    block_inputs = []
     for block in range(span_rows // Q_ROWS):
         q_lo = block * Q_ROWS
         k_lo = own_start + q_lo + Q_ROWS - window
@@ -135,17 +136,27 @@
         k_place = places[k_lo : k_lo + window]
         allowed = (q_label[:, None] == k_label[None, :]) & (k_place[None, :] <= q_place[:, None])
         q_block = q_seq[q_lo : q_lo + Q_ROWS].reshape(Q_ROWS, local_q, HD)
+        block_inputs.append(
+            (q_lo, k_lo, q_block, k_all[k_lo : k_lo + window], v_all[k_lo : k_lo + window], allowed)
+        )
+    forward_parts = [
+        forward_pass(q_block, k_win, v_win, allowed, score_scale)
+        for _, _, q_block, k_win, v_win, allowed in block_inputs
+    ]
+    attn_seq = jnp.concatenate(
+        [attn.reshape(Q_ROWS, q_width) for _, _, attn in forward_parts], axis=0
+    )
+    attn_out = lax.all_to_all(attn_seq, "sp", split_axis=0, concat_axis=1, tiled=True)
+    attn_out = attn_out.reshape(tok_dev, heads_q * HD)
+    dq_parts = []
+    for (q_lo, k_lo, q_block, k_win, v_win, _), (weights, probs_bf, attn) in zip(
+        block_inputs, forward_parts
+    ):
         g_block = g_seq[q_lo : q_lo + Q_ROWS].reshape(Q_ROWS, local_q, HD)
-        attn_block, dq_block, grad_k, grad_v = block_pass(
-            q_block,
-            g_block,
-            k_all[k_lo : k_lo + window],
-            v_all[k_lo : k_lo + window],
-            allowed,
-            score_scale,
+        dq_block, grad_k, grad_v = backward_pass(
+            q_block, g_block, k_win, v_win, weights, probs_bf, attn, score_scale
         )
-        attn_parts.append(attn_block.reshape(Q_ROWS, local_q * HD))
-        dq_parts.append(dq_block.reshape(Q_ROWS, local_q * HD))
+        dq_parts.append(dq_block.reshape(Q_ROWS, q_width))
         grad_k_all = grad_k_all.at[k_lo : k_lo + window].add(grad_k)
         grad_v_all = grad_v_all.at[k_lo : k_lo + window].add(grad_v)
     grad_kv_all = jnp.concatenate([grad_k_all, grad_v_all], axis=1)
@@ -162,13 +173,9 @@
         passed_along(pair_sum[reach_groups - d].astype(jnp.bfloat16), "fsdp", -d)
         for d in range(1, reach_groups + 1)
     ]
-    attn_seq = jnp.concatenate(attn_parts, axis=0)
     dq_seq = jnp.concatenate(dq_parts, axis=0)
-    outgoing = jnp.concatenate([attn_seq, dq_seq], axis=1)
-    back_all = lax.all_to_all(outgoing, "sp", split_axis=0, concat_axis=1, tiled=True)
-    back_all = back_all.reshape(tok_dev, seq_width, outgoing.shape[1])
-    attn_out = back_all[:, :, :q_width].reshape(tok_dev, heads_q * HD)
-    grad_queries = back_all[:, :, q_width:].reshape(tok_dev, heads_q * HD)
+    grad_queries = lax.all_to_all(dq_seq, "sp", split_axis=0, concat_axis=1, tiled=True)
+    grad_queries = grad_queries.reshape(tok_dev, heads_q * HD)
     back_half = backs[0].astype(jnp.float32)
     for back in backs[1:]:
         back_half = back_half + back

time: 127 us -> 175 us (1.38)
  the two profiles are of different devices: /device:TPU:384 before, /device:TPU:228 now
where the time goes in v6:
time: 175 us; the launch traced here: 174 us
  starting transfers between devices  44.9 us (26%)
  matrix products  39.9 us (23%)
  waiting for transfers between devices  35.2 us (20%)
  local copies, waits for them, and re-layouts  31.6 us (18%)
  other arithmetic  21 us (12%)
    ppermute x4, starting transfers between devices, passed_along(): lax.ppermute(value, axis, [(source, source + steps) for source in range(f...  14.9 us
    dot_general x4, matrix products, backward_pass(): jnp.einsum('hqk,qhd->kd', probs_bf, g_block, preferred_element_type=jnp.f...  14.8 us
    unnamed x96, local copies, waits for them, and re-layouts  14.5 us
    ppermute x4, waiting for transfers between devices, passed_along(): lax.ppermute(value, axis, [(source, source + steps) for source in range(f...  14.2 us
    dot_general x4, matrix products, forward_pass(): jnp.einsum('hqk,kd->qhd', probs_bf, v_win, preferred_element_type=jnp.flo...  8.12 us
    and x2, other arithmetic, local(): (q_label[:, None] == k_label[None, :]) & (k_place[None, :] <= q_place[:,...  7.89 us
    all_to_all x1, waiting for transfers between devices, local(): lax.all_to_all(dq_seq, 'sp', split_axis=0, concat_axis=1, tiled=True)  7.34 us
    all_to_all x1, waiting for transfers between devices, local(): lax.all_to_all(kv_pack, 'sp', split_axis=1, concat_axis=0, tiled=True)  6.96 us
  transfers between devices with their start and end apart: 12, of which 6 were waited for; matrix products, arithmetic and copies ran while one was open for 43% of the time, Pallas kernels for 0%

profile of v6, /device:TPU:228, one launch (start us, length us, event | category | flops | bytes accessed | tf_op | source)
XLA Modules:
  0.0 174.2 jit_solution(16325814417448885640)
XLA Ops:
  3.4 4.5 %all-to-all-start.1 = ((bf16[128,8,256]{2,0,1:T(8,128)(2,1)}), bf16[128,8,256]{2,0,1:T(8,128)(2,1)S(1)}, u32[]{:S(2)}, u32[]{:S(2)}) async-start(bf16[128,8,256]{2,0,1:T(8,128)(2,1)} %pad_maximum_fusion.7), calls=%async_computation.1 | async-start | bytes 1048576 | tf_op jit(solution)/shard_map/all_to_all | solution.py:88
  11.3 7.0 %all-to-all-done.1 = bf16[128,8,256]{2,0,1:T(8,128)(2,1)S(1)} async-done(((bf16[128,8,256]{2,0,1:T(8,128)(2,1)}), bf16[128,8,256]{2,0,1:T(8,128)(2,1)S(1)}, u32[]{:S(2)}, u32[]{:S(2)}) %all-to-all-start.1) | async-done | bytes 524320 | tf_op jit(solution)/shard_map/all_to_all | solution.py:88
  18.3 3.5 %all-to-all-start = ((bf16[128,8,256]{0,2,1:T(8,128)(2,1)}), bf16[128,8,256]{0,2,1:T(8,128)(2,1)S(1)}, u32[]{:S(2)}, u32[]{:S(2)}) async-start(bf16[128,8,256]{0,2,1:T(8,128)(2,1)} %bitcast), calls=%async_computation | async-start | bytes 1048576 | tf_op jit(solution)/shard_map/all_to_all | solution.py:91
  21.8 5.0 %collective-permute-start = (bf16[512,256]{1,0:T(8,128)(2,1)S(1)}, bf16[512,256]{1,0:T(8,128)(2,1)S(1)}, u32[]{:S(2)}, u32[]{:S(2)}) collective-permute-start(bf16[512,256]{1,0:T(8,128)(2,1)S(1)} %constant_dynamic-slice_fusion), channel_id=1, source_target_pairs={{0,16},{8,24},{16,32},{24,40},{32,48},{40,56},{48,64},{56,72},{64,... | collective-permute-start | bytes 786440 | tf_op jit(solution)/shard_map/ppermute | solution.py:20
  26.8 4.0 %collective-permute-start.1 = (bf16[512,256]{1,0:T(8,128)(2,1)S(1)}, bf16[512,256]{1,0:T(8,128)(2,1)S(1)}, u32[]{:S(2)}, u32[]{:S(2)}) collective-permute-start(bf16[512,256]{1,0:T(8,128)(2,1)S(1)} %constant_dynamic-slice_fusion), channel_id=1, source_target_pairs={{0,8},{8,16},{16,24},{24,32},{32,40},{40,48},{48,56},{56,64},{64,7... | collective-permute-start | bytes 786440 | tf_op jit(solution)/shard_map/ppermute | solution.py:20
  30.8 3.9 %compare_and_fusion.2 = (pred[256,2304]{0,1:T(8,128)(4,1)S(1)}, pred[256,2304]{0,1:T(8,128)(4,1)}) fusion(s32[256]{0:T(256)S(1)} %get-tuple-element.146, s32[256]{0:T(256)S(1)} %get-tuple-element.143, s32[2304]{0:T(1024)S(1)} %get-tuple-element.139, s32[2304]{0:T(1024)S(1)} %get-tuple-element.135, s32[256]{0:T(256)S(1)} %get-tuple-element.144, ...), kind=kLoop, calls=%fused_computation.70 | loop fusion | flops 3538944 | bytes 1220608 | tf_op jit(solution)/shard_map/and | solution.py:137
  35.7 3.7 %collective-permute-done.1 = bf16[512,256]{1,0:T(8,128)(2,1)S(1)} collective-permute-done((bf16[512,256]{1,0:T(8,128)(2,1)S(1)}, bf16[512,256]{1,0:T(8,128)(2,1)S(1)}, u32[]{:S(2)}, u32[]{:S(2)}) %collective-permute-start.1) | collective-permute-done | bytes 262176 | tf_op jit(solution)/shard_map/ppermute | solution.py:20
  41.4 4.0 %compare_and_fusion = (pred[256,2304]{0,1:T(8,128)(4,1)}, pred[256,2304]{0,1:T(8,128)(4,1)}) fusion(s32[256]{0:T(256)S(1)} %get-tuple-element.147, s32[256]{0:T(256)S(1)} %get-tuple-element.141, s32[2304]{0:T(1024)S(1)} %get-tuple-element.137, s32[2304]{0:T(1024)S(1)} %get-tuple-element.133, s32[256]{0:T(256)S(1)} %get-tuple-element.145, ...), kind=kLoop, calls=%fused_computation.68 | loop fusion | flops 3538944 | bytes 1220608 | tf_op jit(solution)/shard_map/and | solution.py:137
  52.1 4.6 %all-to-all-start.3 = ((bf16[128,8,256]{0,2,1:T(8,128)(2,1)}), bf16[128,8,256]{0,2,1:T(8,128)(2,1)S(1)}, u32[]{:S(2)}, u32[]{:S(2)}) async-start(bf16[128,8,256]{0,2,1:T(8,128)(2,1)} %bitcast.9), calls=%async_computation.3 | async-start | bytes 1048576 | tf_op jit(solution)/shard_map/all_to_all | solution.py:117
  64.5 5.3 %convolution_convert_fusion.3 = bf16[128,2,256]{2,0,1:T(8,128)(2,1)S(1)} fusion(f32[2,256,2304]{1,2,0:T(8,128)} %copy-done.4, f32[2,256]{1,0:T(2,128)S(1)} %log_add_fusion.3, bf16[3072,256]{1,0:T(8,128)(2,1)S(1)} %pad_maximum_fusion), kind=kOutput, calls=%fused_computation.81 | convolution fusion | flops 304414720 | bytes 5441536 | tf_op jit(solution)/shard_map/hqk,kd->qhd/dot_general | solution.py:53
  74.5 4.8 %all-to-all-start.2 = ((bf16[8,128,256]{2,1,0:T(8,128)(2,1)}), bf16[8,128,256]{2,1,0:T(8,128)(2,1)}, u32[]{:S(2)}, u32[]{:S(2)}) async-start(bf16[8,128,256]{2,1,0:T(8,128)(2,1)} %bitcast.35), calls=%async_computation.2 | async-start | bytes 1048576 | tf_op jit(solution)/shard_map/all_to_all | solution.py:149
  80.2 4.3 %convolution_bitcast_fusion.7 = f32[2304,128]{0,1:T(8,128)} fusion(bf16[256,2,128]{0,2,1:T(8,128)(2,1)S(1)} %reshape.602, f32[2,256,2304]{1,2,0:T(8,128)} %copy-done.4, f32[2,256]{1,0:T(2,128)S(1)} %log_add_fusion.3), kind=kOutput, calls=%fused_computation.51 | convolution fusion | flops 304349184 | bytes 6031360 | tf_op jit(solution)/shard_map/hqk,qhd->kd/dot_general | solution.py:68
  86.3 3.5 %fusion.31 = f32[3072,128]{0,1:T(8,128)S(1)} fusion(f32[3072,128]{0,1:T(8,128)S(1)} %scatter-add.34, bf16[256,2,128]{0,2,1:T(8,128)(2,1)S(1)} %reshape.604, f32[2,256,2304]{1,2,0:T(8,128)} %copy-done.1, f32[2,256]{1,0:T(2,128)S(1)} %log_add_fusion.2), kind=kOutput, calls=%fused_computation.63 | convolution fusion | flops 304644096 | bytes 7211008 | tf_op jit(solution)/shard_map/hqk,qhd->kd/dot_general | solution.py:68
  91.5 3.5 %fusion.33 = f32[3072,128]{0,1:T(8,128)S(1)} fusion(f32[3072,128]{0,1:T(8,128)S(1)} %fusion.31, bf16[256,2,128]{0,2,1:T(8,128)(2,1)S(1)} %reshape.606, f32[2,256,2304]{1,2,0:T(8,128)} %copy-done.2, f32[2,256]{1,0:T(2,128)S(1)} %log_add_fusion.1), kind=kOutput, calls=%fused_computation.65 | convolution fusion | flops 304644096 | bytes 7211008 | tf_op jit(solution)/shard_map/hqk,qhd->kd/dot_general | solution.py:68
  97.5 3.5 %fusion.35 = f32[3072,128]{0,1:T(8,128)S(1)} fusion(f32[3072,128]{0,1:T(8,128)S(1)} %fusion.33, bf16[256,2,128]{0,2,1:T(8,128)(2,1)} %reshape.608, f32[2,256,2304]{1,2,0:T(8,128)} %copy-done.3, f32[2,256]{1,0:T(2,128)S(1)} %log_add_fusion), kind=kOutput, calls=%fused_computation.67 | convolution fusion | flops 304644096 | bytes 7211008 | tf_op jit(solution)/shard_map/hqk,qhd->kd/dot_general | solution.py:68
  101.1 3.8 %fusion.16 = bf16[2,256,2304]{1,2,0:T(8,128)(2,1)S(1)} fusion(bf16[256,2,128]{0,2,1:T(8,128)(2,1)S(1)} %copy-done.10, f32[2,256,2304]{1,2,0:T(8,128)} %copy-done.4, f32[2,256]{1,0:T(2,128)S(1)} %bitcast.315, f32[2,256]{1,0:T(2,128)S(1)} %log_add_fusion.3, bf16[3072,256]{1,0:T(8,128)(2,1)S(1)} %pad_maximum_fusion), kind=kOutput, calls=%fused_computation.40 | convolution fusion | flops 306708480 | bytes 7802880 | tf_op jit(solution)/shard_map/qhd,kd->hqk/dot_general | solution.py:61
  115.4 2.7 %collective-permute-start.3 = (f32[2,512,256]{1,2,0:T(8,128)S(1)}, f32[2,512,256]{1,2,0:T(8,128)S(1)}, u32[]{:S(2)}, u32[]{:S(2)}) collective-permute-start(f32[2,512,256]{1,2,0:T(8,128)S(1)} %fusion.41), channel_id=1, source_target_pairs={{0,1},{1,0},{2,3},{3,2},{4,5},{5,4},{6,7},{7,6},{8,9},{9,8},{10,11... | collective-permute-start | bytes 3145736 | tf_op jit(solution)/shard_map/ppermute | solution.py:171
  121.5 2.5 %collective-permute-start.4 = (bf16[512,256]{0,1:T(8,128)(2,1)}, bf16[512,256]{0,1:T(8,128)(2,1)S(1)}, u32[]{:S(2)}, u32[]{:S(2)}) collective-permute-start(bf16[512,256]{0,1:T(8,128)(2,1)} %get-tuple-element.120), channel_id=1, source_target_pairs={{8,0},{16,8},{24,16},{32,24},{40,32},{48,40},{56,48},{64,56},{72,6... | collective-permute-start | bytes 786440 | tf_op jit(solution)/shard_map/ppermute | solution.py:20
  124.0 3.4 %collective-permute-start.5 = (bf16[512,256]{0,1:T(8,128)(2,1)}, bf16[512,256]{0,1:T(8,128)(2,1)}, u32[]{:S(2)}, u32[]{:S(2)}) collective-permute-start(bf16[512,256]{0,1:T(8,128)(2,1)} %get-tuple-element.121), channel_id=1, source_target_pairs={{16,0},{24,8},{32,16},{40,24},{48,32},{56,40},{64,48},{72,56},{80,... | collective-permute-start | bytes 786440 | tf_op jit(solution)/shard_map/ppermute | solution.py:20
  132.7 9.1 %collective-permute-done.5 = bf16[512,256]{0,1:T(8,128)(2,1)} collective-permute-done((bf16[512,256]{0,1:T(8,128)(2,1)}, bf16[512,256]{0,1:T(8,128)(2,1)}, u32[]{:S(2)}, u32[]{:S(2)}) %collective-permute-start.5) | collective-permute-done | bytes 262176 | tf_op jit(solution)/shard_map/ppermute | solution.py:20
  143.8 4.6 %all-to-all-start.4 = ((bf16[8,128,256]{2,1,0:T(8,128)(2,1)}), bf16[8,128,256]{2,1,0:T(8,128)(2,1)S(1)}, u32[]{:S(2)}, u32[]{:S(2)}) async-start(bf16[8,128,256]{2,1,0:T(8,128)(2,1)} %bitcast.287), calls=%async_computation.4 | async-start | bytes 1048576 | tf_op jit(solution)/shard_map/all_to_all | solution.py:177
  151.4 7.3 %all-to-all-done.4 = bf16[8,128,256]{2,1,0:T(8,128)(2,1)S(1)} async-done(((bf16[8,128,256]{2,1,0:T(8,128)(2,1)}), bf16[8,128,256]{2,1,0:T(8,128)(2,1)S(1)}, u32[]{:S(2)}, u32[]{:S(2)}) %all-to-all-start.4) | async-done | bytes 524320 | tf_op jit(solution)/shard_map/all_to_all | solution.py:177
  158.8 3.5 %all-to-all-start.5 = ((bf16[8,128,256]{1,2,0:T(8,128)(2,1)}), bf16[8,128,256]{1,2,0:T(8,128)(2,1)S(1)}, u32[]{:S(2)}, u32[]{:S(2)}) async-start(bf16[8,128,256]{1,2,0:T(8,128)(2,1)} %pad_maximum_fusion.10), calls=%async_computation.5 | async-start | bytes 1048576 | tf_op jit(solution)/shard_map/all_to_all | solution.py:187
  165.9 6.6 %all-to-all-done.5 = bf16[8,128,256]{1,2,0:T(8,128)(2,1)S(1)} async-done(((bf16[8,128,256]{1,2,0:T(8,128)(2,1)}), bf16[8,128,256]{1,2,0:T(8,128)(2,1)S(1)}, u32[]{:S(2)}, u32[]{:S(2)}) %all-to-all-start.5) | async-done | bytes 524320 | tf_op jit(solution)/shard_map/all_to_all | solution.py:187
  (193 shorter events, 64.0 us)
Async XLA Ops:
  0.6 7.3 %copy-start.34 = (s32[128]{0:T(128)S(1)}, s32[128]{0:T(128)}, u32[]{:S(2)}) copy-start(s32[128]{0:T(128)} %param.25) | copy-start | bytes 1540
  0.7 9.6 %copy-start.29 = (bf16[128,2048]{1,0:T(8,128)(2,1)S(1)}, bf16[128,2048]{1,0:T(8,128)(2,1)}, u32[]{:S(2)}) copy-start(bf16[128,2048]{1,0:T(8,128)(2,1)} %param.21) | copy-start | bytes 1572868
  3.4 14.8 %all-to-all-start.1 = ((bf16[128,8,256]{2,0,1:T(8,128)(2,1)}), bf16[128,8,256]{2,0,1:T(8,128)(2,1)S(1)}, u32[]{:S(2)}, u32[]{:S(2)}) async-start(bf16[128,8,256]{2,0,1:T(8,128)(2,1)} %pad_maximum_fusion.7), calls=%async_computation.1 | async-start | bytes 1048576 | tf_op jit(solution)/shard_map/all_to_all | solution.py:88
  7.9 26.8 %copy-start.30 = (bf16[128,2048]{1,0:T(8,128)(2,1)S(1)}, bf16[128,2048]{1,0:T(8,128)(2,1)}, u32[]{:S(2)}) copy-start(bf16[128,2048]{1,0:T(8,128)(2,1)} %param.24) | copy-start | bytes 1572868
  18.3 27.2 %all-to-all-start = ((bf16[128,8,256]{0,2,1:T(8,128)(2,1)}), bf16[128,8,256]{0,2,1:T(8,128)(2,1)S(1)}, u32[]{:S(2)}, u32[]{:S(2)}) async-start(bf16[128,8,256]{0,2,1:T(8,128)(2,1)} %bitcast), calls=%async_computation | async-start | bytes 1048576 | tf_op jit(solution)/shard_map/all_to_all | solution.py:91
  21.8 13.9 %collective-permute-start = (bf16[512,256]{1,0:T(8,128)(2,1)S(1)}, bf16[512,256]{1,0:T(8,128)(2,1)S(1)}, u32[]{:S(2)}, u32[]{:S(2)}) collective-permute-start(bf16[512,256]{1,0:T(8,128)(2,1)S(1)} %constant_dynamic-slice_fusion), channel_id=1, source_target_pairs={{0,16},{8,24},{16,32},{24,40},{32,48},{40,56},{48,64},{56,72},{64,... | collective-permute-start | bytes 786440 | tf_op jit(solution)/shard_map/ppermute | solution.py:20
  26.8 12.6 %collective-permute-start.1 = (bf16[512,256]{1,0:T(8,128)(2,1)S(1)}, bf16[512,256]{1,0:T(8,128)(2,1)S(1)}, u32[]{:S(2)}, u32[]{:S(2)}) collective-permute-start(bf16[512,256]{1,0:T(8,128)(2,1)S(1)} %constant_dynamic-slice_fusion), channel_id=1, source_target_pairs={{0,8},{8,16},{16,24},{24,32},{32,40},{40,48},{48,56},{56,64},{64,7... | collective-permute-start | bytes 786440 | tf_op jit(solution)/shard_map/ppermute | solution.py:20
  39.5 6.2 %collective-permute-start.2 = (bf16[1024,256]{1,0:T(8,128)(2,1)S(1)}, bf16[1024,256]{1,0:T(8,128)(2,1)}, u32[]{:S(2)}, u32[]{:S(2)}) collective-permute-start(bf16[1024,256]{1,0:T(8,128)(2,1)S(1)} %pad_maximum_fusion.4), channel_id=1, source_target_pairs={{0,1},{1,0},{2,3},{3,2},{4,5},{5,4},{6,7},{7,6},{8,9},{9,8},{10,11... | collective-permute-start | bytes 1572872 | tf_op jit(solution)/shard_map/ppermute | solution.py:102
  49.9 6.8 %copy-start.33 = (bf16[256,256]{1,0:T(8,128)(2,1)S(1)}, bf16[256,256]{1,0:T(8,128)(2,1)}, u32[]{:S(2)}) copy-start(bf16[256,256]{1,0:T(8,128)(2,1)} %get-tuple-element.129) | copy-start | bytes 393220
  52.1 22.4 %all-to-all-start.3 = ((bf16[128,8,256]{0,2,1:T(8,128)(2,1)}), bf16[128,8,256]{0,2,1:T(8,128)(2,1)S(1)}, u32[]{:S(2)}, u32[]{:S(2)}) async-start(bf16[128,8,256]{0,2,1:T(8,128)(2,1)} %bitcast.9), calls=%async_computation.3 | async-start | bytes 1048576 | tf_op jit(solution)/shard_map/all_to_all | solution.py:117
  63.0 6.8 %slice-start = ((s8[4718592]{0:T(1024)(128)(4,1)}), s8[4194304]{0:T(1024)(128)(4,1)S(1)}, s32[]{:S(2)}) async-start(s8[4718592]{0:T(1024)(128)(4,1)} %bitcast.273), calls=%async_computation.6 | async-start | bytes 8388608
  63.8 8.0 %copy-start.3 = (f32[2,256,2304]{1,2,0:T(8,128)}, f32[2,256,2304]{1,2,0:T(8,128)S(1)}, u32[]{:S(2)}) copy-start(f32[2,256,2304]{1,2,0:T(8,128)S(1)} %get-tuple-element.149) | copy-start | bytes 14155780
  63.8 6.0 %slice-start.1 = ((s8[4718592]{0:T(1024)(128)(4,1)}), s8[524288]{0:T(1024)(128)(4,1)S(1)}, s32[]{:S(2)}) async-start(s8[4718592]{0:T(1024)(128)(4,1)} %bitcast.273), calls=%async_computation.7 | async-start | bytes 1048576
  63.8 7.0 %slice-start.4 = ((s8[4718592]{0:T(1024)(128)(4,1)}), s8[4194304]{0:T(1024)(128)(4,1)S(1)}, s32[]{:S(2)}) async-start(s8[4718592]{0:T(1024)(128)(4,1)} %bitcast.277), calls=%async_computation.10 | async-start | bytes 8388608
  64.5 6.3 %slice-start.5 = ((s8[4718592]{0:T(1024)(128)(4,1)}), s8[524288]{0:T(1024)(128)(4,1)S(1)}, s32[]{:S(2)}) async-start(s8[4718592]{0:T(1024)(128)(4,1)} %bitcast.277), calls=%async_computation.11 | async-start | bytes 1048576
  74.5 69.4 %all-to-all-start.2 = ((bf16[8,128,256]{2,1,0:T(8,128)(2,1)}), bf16[8,128,256]{2,1,0:T(8,128)(2,1)}, u32[]{:S(2)}, u32[]{:S(2)}) async-start(bf16[8,128,256]{2,1,0:T(8,128)(2,1)} %bitcast.35), calls=%async_computation.2 | async-start | bytes 1048576 | tf_op jit(solution)/shard_map/all_to_all | solution.py:149
  80.2 4.4 %copy-start.9 = (bf16[256,2,128]{0,2,1:T(8,128)(2,1)}, bf16[256,2,128]{0,2,1:T(8,128)(2,1)S(1)}, u32[]{:S(2)}) copy-start(bf16[256,2,128]{0,2,1:T(8,128)(2,1)S(1)} %reshape.602) | copy-start | bytes 393220
  101.1 5.0 %slice-start.2 = ((s8[4718592]{0:T(1024)(128)(4,1)}), s8[4194304]{0:T(1024)(128)(4,1)S(1)}, s32[]{:S(2)}) async-start(s8[4718592]{0:T(1024)(128)(4,1)} %bitcast.275), calls=%async_computation.8 | async-start | bytes 8388608
  115.4 4.8 %collective-permute-start.3 = (f32[2,512,256]{1,2,0:T(8,128)S(1)}, f32[2,512,256]{1,2,0:T(8,128)S(1)}, u32[]{:S(2)}, u32[]{:S(2)}) collective-permute-start(f32[2,512,256]{1,2,0:T(8,128)S(1)} %fusion.41), channel_id=1, source_target_pairs={{0,1},{1,0},{2,3},{3,2},{4,5},{5,4},{6,7},{7,6},{8,9},{9,8},{10,11... | collective-permute-start | bytes 3145736 | tf_op jit(solution)/shard_map/ppermute | solution.py:171
  120.6 9.6 %copy-start.7 = (f32[3072,128]{0,1:T(8,128)S(1)}, f32[3072,128]{0,1:T(8,128)}, u32[]{:S(2)}) copy-start(f32[3072,128]{0,1:T(8,128)} %copy-done.5) | copy-start | bytes 4718596
  121.5 11.2 %collective-permute-start.4 = (bf16[512,256]{0,1:T(8,128)(2,1)}, bf16[512,256]{0,1:T(8,128)(2,1)S(1)}, u32[]{:S(2)}, u32[]{:S(2)}) collective-permute-start(bf16[512,256]{0,1:T(8,128)(2,1)} %get-tuple-element.120), channel_id=1, source_target_pairs={{8,0},{16,8},{24,16},{32,24},{40,32},{48,40},{56,48},{64,56},{72,6... | collective-permute-start | bytes 786440 | tf_op jit(solution)/shard_map/ppermute | solution.py:20
  124.0 17.8 %collective-permute-start.5 = (bf16[512,256]{0,1:T(8,128)(2,1)}, bf16[512,256]{0,1:T(8,128)(2,1)}, u32[]{:S(2)}, u32[]{:S(2)}) collective-permute-start(bf16[512,256]{0,1:T(8,128)(2,1)} %get-tuple-element.121), channel_id=1, source_target_pairs={{16,0},{24,8},{32,16},{40,24},{48,32},{56,40},{64,48},{72,56},{80,... | collective-permute-start | bytes 786440 | tf_op jit(solution)/shard_map/ppermute | solution.py:20
  143.8 14.9 %all-to-all-start.4 = ((bf16[8,128,256]{2,1,0:T(8,128)(2,1)}), bf16[8,128,256]{2,1,0:T(8,128)(2,1)S(1)}, u32[]{:S(2)}, u32[]{:S(2)}) async-start(bf16[8,128,256]{2,1,0:T(8,128)(2,1)} %bitcast.287), calls=%async_computation.4 | async-start | bytes 1048576 | tf_op jit(solution)/shard_map/all_to_all | solution.py:177
  158.8 13.8 %all-to-all-start.5 = ((bf16[8,128,256]{1,2,0:T(8,128)(2,1)}), bf16[8,128,256]{1,2,0:T(8,128)(2,1)S(1)}, u32[]{:S(2)}, u32[]{:S(2)}) async-start(bf16[8,128,256]{1,2,0:T(8,128)(2,1)} %pad_maximum_fusion.10), calls=%async_computation.5 | async-start | bytes 1048576 | tf_op jit(solution)/shard_map/all_to_all | solution.py:187
  (33 other events, 63.2 us)

commit v7 on v3

--- a/solution.py
+++ b/solution.py
@@ -74,15 +74,22 @@
     local_q = heads_q // seq_width
     copies = seq_width // heads_k
     score_scale = 1.0 / math.sqrt(HD)
-    kv_pack = jnp.concatenate(
-        [
-            widen_heads(key_rows, copies).reshape(tok_dev, seq_width, HD),
-            widen_heads(value_rows, copies).reshape(tok_dev, seq_width, HD),
-        ],
+    core = lax.axis_index("sp") % 2
+    sibling = [(s, s ^ 1) for s in range(seq_width)]
+    part_rows = tok_dev // 2
+    kv_heads = jnp.concatenate(
+        [key_rows.reshape(tok_dev, heads_k, HD), value_rows.reshape(tok_dev, heads_k, HD)],
         axis=2,
     )
-    kv_seq = lax.all_to_all(kv_pack, "sp", split_axis=1, concat_axis=0, tiled=True)
-    kv_seq = kv_seq.reshape(span_rows, 2 * HD)
+    kv_send = jnp.transpose(kv_heads.reshape(2, part_rows, heads_k, 2 * HD), (2, 0, 1, 3))
+    kv_send = kv_send.reshape(seq_width, part_rows, 2 * HD)
+    kv_mine = lax.all_to_all(kv_send, "sp", split_axis=0, concat_axis=0, tiled=True)
+
+    def joined(mine, theirs):
+        return jnp.where(
+            core == 0, jnp.stack([mine, theirs], axis=1), jnp.stack([theirs, mine], axis=1)
+        ).reshape(span_rows, 2 * HD)
+
     q_width = local_q * HD
     qg_pack = jnp.concatenate(
         [
@@ -98,8 +105,11 @@
     reach = MOST_BLK * BLK
     reach_groups = (reach - 1) // span_rows + 1
     first_place = lax.axis_index("fsdp") * span_rows
-    earlier = [passed_along(kv_seq, "fsdp", d) for d in range(reach_groups, 0, -1)]
-    kv_all = jnp.concatenate(earlier + [kv_seq], axis=0)
+    received = [passed_along(kv_mine, "fsdp", d) for d in range(reach_groups, 0, -1)]
+    own_theirs = lax.ppermute(kv_mine, "sp", sibling)
+    swapped = lax.ppermute(jnp.stack(received), "sp", sibling)
+    earlier = [joined(mine, swapped[index]) for index, mine in enumerate(received)]
+    kv_all = jnp.concatenate(earlier + [joined(kv_mine, own_theirs)], axis=0)
     k_all = kv_all[:, :HD]
     v_all = kv_all[:, HD:]
     base_place = first_place - reach_groups * span_rows
@@ -134,13 +144,15 @@
         grad_k_all = grad_k_all.at[k_lo : k_lo + window].add(grad_k)
         grad_v_all = grad_v_all.at[k_lo : k_lo + window].add(grad_v)
     grad_kv_all = jnp.concatenate([grad_k_all, grad_v_all], axis=1)
+    grad_parts = grad_kv_all.reshape(reach_groups + 1, seq_width, 2, part_rows, 2 * HD)
+    low_rows = grad_parts[:, :, 0]
+    high_rows = grad_parts[:, :, 1]
+    mine_part = jnp.where(core == 0, low_rows, high_rows)
+    their_part = jnp.where(core == 0, high_rows, low_rows)
+    pair_sum = mine_part + lax.ppermute(their_part, "sp", sibling)
     backs = [
-        passed_along(
-            grad_kv_all[lo : lo + span_rows].astype(jnp.bfloat16), "fsdp", -distance
-        )
-        for distance, lo in (
-            (d, (reach_groups - d) * span_rows) for d in range(1, reach_groups + 1)
-        )
+        passed_along(pair_sum[reach_groups - d].astype(jnp.bfloat16), "fsdp", -d)
+        for d in range(1, reach_groups + 1)
     ]
     attn_seq = jnp.concatenate(attn_parts, axis=0)
     dq_seq = jnp.concatenate(dq_parts, axis=0)
@@ -149,20 +161,18 @@
     back_all = back_all.reshape(tok_dev, seq_width, outgoing.shape[1])
     attn_out = back_all[:, :, :q_width].reshape(tok_dev, heads_q * HD)
     grad_queries = back_all[:, :, q_width:].reshape(tok_dev, heads_q * HD)
-    kv_sum = grad_kv_all[own_start:]
+    kv_sum = pair_sum[reach_groups]
     for back in backs:
         kv_sum = kv_sum + back
-    kv_sum = jnp.concatenate([kv_sum[:, :HD] * score_scale, kv_sum[:, HD:]], axis=1)
+    kv_sum = jnp.concatenate([kv_sum[..., :HD] * score_scale, kv_sum[..., HD:]], axis=-1)
     kv_back = lax.all_to_all(
-        kv_sum.astype(jnp.bfloat16), "sp", split_axis=0, concat_axis=1, tiled=True
+        kv_sum.astype(jnp.bfloat16), "sp", split_axis=0, concat_axis=0, tiled=True
     )
-    kv_back = kv_back.reshape(tok_dev, seq_width, 2 * HD).astype(jnp.float32)
-    grad_keys = jnp.sum(
-        kv_back[:, :, :HD].reshape(tok_dev, heads_k, copies, HD), axis=2
-    ).reshape(tok_dev, heads_k * HD)
-    grad_values = jnp.sum(
-        kv_back[:, :, HD:].reshape(tok_dev, heads_k, copies, HD), axis=2
-    ).reshape(tok_dev, heads_k * HD)
+    kv_back = jnp.transpose(
+        kv_back.reshape(heads_k, 2, part_rows, 2 * HD), (1, 2, 0, 3)
+    ).reshape(tok_dev, heads_k, 2 * HD)
+    grad_keys = kv_back[:, :, :HD].reshape(tok_dev, heads_k * HD)
+    grad_values = kv_back[:, :, HD:].reshape(tok_dev, heads_k * HD)
     return (
         attn_out,
         grad_queries,

time: 138 us -> 132 us (0.957)
  the two profiles are of different devices: /device:TPU:260 before, /device:TPU:100 now
where the time goes in v7:
time: 132 us; the launch traced here: 131 us
  starting transfers between devices  38.1 us (29%)
  other arithmetic  25.9 us (20%)
  waiting for transfers between devices  24.8 us (19%)
  matrix products  21.3 us (16%)
  local copies, waits for them, and re-layouts  19.9 us (15%)
    ppermute x4, starting transfers between devices, passed_along(): lax.ppermute(value, axis, [(source, source + steps) for source in range(f...  14.9 us
    ppermute x4, waiting for transfers between devices, passed_along(): lax.ppermute(value, axis, [(source, source + steps) for source in range(f...  9.8 us
    all_to_all x1, waiting for transfers between devices, local(): lax.all_to_all(outgoing, 'sp', split_axis=0, concat_axis=1, tiled=True)  6.61 us
    and x2, other arithmetic, local(): (q_label[:, None] == k_label[None, :]) & (k_place[None, :] <= q_place[:,...  6.26 us
    all_to_all x1, waiting for transfers between devices, local(): lax.all_to_all(kv_sum.astype(jnp.bfloat16), 'sp', split_axis=0, concat_ax...  5.43 us
    unnamed x34, local copies, waits for them, and re-layouts  5.14 us
    all_to_all x1, starting transfers between devices, local(): lax.all_to_all(kv_send, 'sp', split_axis=0, concat_axis=0, tiled=True)  4.47 us
    all_to_all x1, starting transfers between devices, local(): lax.all_to_all(outgoing, 'sp', split_axis=0, concat_axis=1, tiled=True)  4.46 us
  transfers between devices with their start and end apart: 11, of which 6 were waited for; matrix products, arithmetic and copies ran while one was open for 20% of the time, Pallas kernels for 0%

profile of v7, /device:TPU:100, one launch (start us, length us, event | category | flops | bytes accessed | tf_op | source)
XLA Modules:
  0.0 131.2 jit_solution(5241439997611934603)
XLA Ops:
  3.5 4.5 %all-to-all-start = ((bf16[8,64,256]{2,1,0:T(8,128)(2,1)}), bf16[8,64,256]{2,1,0:T(8,128)(2,1)S(1)}, u32[]{:S(2)}, u32[]{:S(2)}) async-start(bf16[8,64,256]{2,1,0:T(8,128)(2,1)} %bitcast.1), calls=%async_computation | async-start | bytes 524288 | tf_op jit(solution)/shard_map/all_to_all | solution.py:86
  9.0 1.9 %convert_reduce_fusion = s32[3072]{0:T(1024)S(1)} fusion(s32[128]{0:T(128)S(1)} %multiply_reduce_fusion.4, s32[3072]{0:T(1024)S(1)} %iota_add_fusion), kind=kLoop, calls=%fused_computation.70 | loop fusion | flops 1176576 | bytes 25088 | tf_op jit(solution)/shard_map/reduce_sum | solution.py:30
  12.6 2.9 %all-to-all-done = bf16[8,64,256]{2,1,0:T(8,128)(2,1)S(1)} async-done(((bf16[8,64,256]{2,1,0:T(8,128)(2,1)}), bf16[8,64,256]{2,1,0:T(8,128)(2,1)S(1)}, u32[]{:S(2)}, u32[]{:S(2)}) %all-to-all-start) | async-done | bytes 262176 | tf_op jit(solution)/shard_map/all_to_all | solution.py:86
  15.5 3.6 %all-to-all-start.1 = ((bf16[128,8,512]{0,2,1:T(8,128)(2,1)}), bf16[128,8,512]{0,2,1:T(8,128)(2,1)S(1)}, u32[]{:S(2)}, u32[]{:S(2)}) async-start(bf16[128,8,512]{0,2,1:T(8,128)(2,1)} %pad_maximum_fusion.2), calls=%async_computation.1 | async-start | bytes 2097152 | tf_op jit(solution)/shard_map/all_to_all | solution.py:101
  19.1 3.1 %collective-permute-start.1 = (bf16[8,64,256]{2,1,0:T(8,128)(2,1)S(1)}, bf16[8,64,256]{2,1,0:T(8,128)(2,1)S(1)}, u32[]{:S(2)}, u32[]{:S(2)}) collective-permute-start(bf16[8,64,256]{2,1,0:T(8,128)(2,1)S(1)} %all-to-all-done), channel_id=1, source_target_pairs={{0,8},{8,16},{16,24},{24,32},{32,40},{40,48},{48,56},{56,64},{64,7... | collective-permute-start | bytes 786440 | tf_op jit(solution)/shard_map/ppermute | solution.py:20
  22.2 5.3 %collective-permute-start = (bf16[8,64,256]{2,1,0:T(8,128)(2,1)S(1)}, bf16[8,64,256]{2,1,0:T(8,128)(2,1)S(1)}, u32[]{:S(2)}, u32[]{:S(2)}) collective-permute-start(bf16[8,64,256]{2,1,0:T(8,128)(2,1)S(1)} %all-to-all-done), channel_id=1, source_target_pairs={{0,16},{8,24},{16,32},{24,40},{32,48},{40,56},{48,64},{56,72},{64,... | collective-permute-start | bytes 786440 | tf_op jit(solution)/shard_map/ppermute | solution.py:20
  27.5 2.2 %compare_and_fusion.2 = (pred[256,2304]{0,1:T(8,128)(4,1)S(1)}, pred[256,2304]{0,1:T(8,128)(4,1)S(1)}) fusion(s32[256]{0:T(256)S(1)} %get-tuple-element.140, s32[256]{0:T(256)S(1)} %get-tuple-element.137, s32[2304]{0:T(1024)S(1)} %get-tuple-element.133, s32[2304]{0:T(1024)S(1)} %get-tuple-element.129, s32[256]{0:T(256)S(1)} %get-tuple-element.138, ...), kind=kLoop, calls=%fused_computation.63 | loop fusion | flops 3538944 | bytes 1220608 | tf_op jit(solution)/shard_map/and | solution.py:131
  29.7 1.9 %collective-permute-start.3 = (bf16[8,64,256]{2,1,0:T(8,128)(2,1)S(1)}, bf16[8,64,256]{2,1,0:T(8,128)(2,1)S(1)}, u32[]{:S(2)}, u32[]{:S(2)}) collective-permute-start(bf16[8,64,256]{2,1,0:T(8,128)(2,1)S(1)} %all-to-all-done), channel_id=1, source_target_pairs={{0,1},{1,0},{2,3},{3,2},{4,5},{5,4},{6,7},{7,6},{8,9},{9,8},{10,11... | collective-permute-start | bytes 786440 | tf_op jit(solution)/shard_map/ppermute | solution.py:109
  31.7 3.7 %collective-permute-done = bf16[8,64,256]{2,1,0:T(8,128)(2,1)S(1)} collective-permute-done((bf16[8,64,256]{2,1,0:T(8,128)(2,1)S(1)}, bf16[8,64,256]{2,1,0:T(8,128)(2,1)S(1)}, u32[]{:S(2)}, u32[]{:S(2)}) %collective-permute-start) | collective-permute-done | bytes 262176 | tf_op jit(solution)/shard_map/ppermute | solution.py:20
  36.2 1.9 %collective-permute-start.2 = (bf16[2,8,64,256]{3,2,1,0:T(8,128)(2,1)}, bf16[2,8,64,256]{3,2,1,0:T(8,128)(2,1)}, u32[]{:S(2)}, u32[]{:S(2)}) collective-permute-start(bf16[2,8,64,256]{3,2,1,0:T(8,128)(2,1)} %pad_maximum_fusion.3), channel_id=1, source_target_pairs={{0,1},{1,0},{2,3},{3,2},{4,5},{5,4},{6,7},{7,6},{8,9},{9,8},{10,11... | collective-permute-start | bytes 1572872 | tf_op jit(solution)/shard_map/ppermute | solution.py:110
  38.1 4.0 %compare_and_fusion = (pred[256,2304]{0,1:T(8,128)(4,1)}, pred[256,2304]{0,1:T(8,128)(4,1)}) fusion(s32[256]{0:T(256)S(1)} %get-tuple-element.141, s32[256]{0:T(256)S(1)} %get-tuple-element.135, s32[2304]{0:T(1024)S(1)} %get-tuple-element.131, s32[2304]{0:T(1024)S(1)} %get-tuple-element.127, s32[256]{0:T(256)S(1)} %get-tuple-element.139, ...), kind=kLoop, calls=%fused_computation.61 | loop fusion | flops 3538944 | bytes 1220608 | tf_op jit(solution)/shard_map/and | solution.py:131
  70.0 1.9 %pad_maximum_fusion = f32[3072,256]{0,1:T(8,128)} fusion(f32[3072,128]{0,1:T(8,128)S(1)} %fusion.35, f32[3072,128]{0,1:T(8,128)S(1)} %fusion.29), kind=kLoop, calls=%fused_computation.60 | loop fusion | flops 786432 | bytes 6291456 | tf_op jit(solution)/shard_map/concatenate | solution.py:146
  71.9 3.5 %copy.243 = f32[3072,256]{1,0:T(8,128)} copy(f32[3072,256]{0,1:T(8,128)} %pad_maximum_fusion) | data formatting | bytes 6291456 | tf_op jit(solution)/shard_map/concatenate | solution.py:146
  75.5 3.5 %select_bitcast_fusion = f32[3,8,64,256]{3,2,1,0:T(8,128)} fusion(f32[3,8,2,64,256]{4,3,2,1,0:T(8,128)} %bitcast.276, pred[]{:T(512)S(6)} %eq.77), kind=kLoop, calls=%fused_computation.69 | loop fusion | flops 393216 | bytes 4718593 | tf_op jit(solution)/shard_map/jit(_where)/select_n | solution.py:151
  79.0 2.5 %collective-permute-start.4 = (f32[3,8,64,256]{3,2,1,0:T(8,128)}, f32[3,8,64,256]{3,2,1,0:T(8,128)}, u32[]{:S(2)}, u32[]{:S(2)}) collective-permute-start(f32[3,8,64,256]{3,2,1,0:T(8,128)} %select_bitcast_fusion), channel_id=1, source_target_pairs={{0,1},{1,0},{2,3},{3,2},{4,5},{5,4},{6,7},{7,6},{8,9},{9,8},{10,11... | collective-permute-start | bytes 4718600 | tf_op jit(solution)/shard_map/ppermute | solution.py:152
  85.3 2.4 %copy.233 = bf16[1024,512]{1,0:T(8,128)(2,1)} copy(bf16[1024,512]{0,1:T(8,128)(2,1)} %maximum_maximum_fusion) | data formatting | bytes 2097152 | tf_op jit(solution)/shard_map/concatenate | solution.py:159
  87.8 4.5 %all-to-all-start.2 = ((bf16[8,128,512]{2,1,0:T(8,128)(2,1)}), bf16[8,128,512]{2,1,0:T(8,128)(2,1)}, u32[]{:S(2)}, u32[]{:S(2)}) async-start(bf16[8,128,512]{2,1,0:T(8,128)(2,1)} %bitcast.279), calls=%async_computation.2 | async-start | bytes 2097152 | tf_op jit(solution)/shard_map/all_to_all | solution.py:160
  92.3 2.9 %fusion.53 = (bf16[3,8,64,256]{3,2,1,0:T(8,128)(2,1)S(1)}, f32[3,8,64,256]{3,2,1,0:T(8,128)}) fusion(f32[3,8,64,256]{3,2,1,0:T(8,128)} %collective-permute-done.4, f32[3,8,2,64,256]{4,3,2,1,0:T(8,128)S(1)} %bitcast.277, pred[]{:T(512)S(6)} %eq.77), kind=kLoop, calls=%fused_computation.125 | loop fusion | flops 1179648 | bytes 7077889 | tf_op jit(solution)/shard_map/convert.4
  95.2 4.2 %collective-permute-start.5 = (bf16[8,64,256]{2,1,0:T(8,128)(2,1)S(1)}, bf16[8,64,256]{2,1,0:T(8,128)(2,1)S(1)}, u32[]{:S(2)}, u32[]{:S(2)}) collective-permute-start(bf16[8,64,256]{2,1,0:T(8,128)(2,1)S(1)} %get-tuple-element.120), channel_id=1, source_target_pairs={{8,0},{16,8},{24,16},{32,24},{40,32},{48,40},{56,48},{64,56},{72,6... | collective-permute-start | bytes 786440 | tf_op jit(solution)/shard_map/ppermute | solution.py:20
  99.4 2.3 %collective-permute-start.6 = (bf16[8,64,256]{2,1,0:T(8,128)(2,1)S(1)}, bf16[8,64,256]{2,1,0:T(8,128)(2,1)S(1)}, u32[]{:S(2)}, u32[]{:S(2)}) collective-permute-start(bf16[8,64,256]{2,1,0:T(8,128)(2,1)S(1)} %get-tuple-element.121), channel_id=1, source_target_pairs={{16,0},{24,8},{32,16},{40,24},{48,32},{56,40},{64,48},{72,56},{80,... | collective-permute-start | bytes 786440 | tf_op jit(solution)/shard_map/ppermute | solution.py:20
  101.7 6.6 %all-to-all-done.2 = bf16[8,128,512]{2,1,0:T(8,128)(2,1)} async-done(((bf16[8,128,512]{2,1,0:T(8,128)(2,1)}), bf16[8,128,512]{2,1,0:T(8,128)(2,1)}, u32[]{:S(2)}, u32[]{:S(2)}) %all-to-all-start.2) | async-done | bytes 1048608 | tf_op jit(solution)/shard_map/all_to_all | solution.py:160
  111.2 4.8 %collective-permute-done.6 = bf16[8,64,256]{2,1,0:T(8,128)(2,1)S(1)} collective-permute-done((bf16[8,64,256]{2,1,0:T(8,128)(2,1)S(1)}, bf16[8,64,256]{2,1,0:T(8,128)(2,1)S(1)}, u32[]{:S(2)}, u32[]{:S(2)}) %collective-permute-start.6) | collective-permute-done | bytes 262176 | tf_op jit(solution)/shard_map/ppermute | solution.py:20
  118.0 4.3 %all-to-all-start.3 = ((bf16[8,64,256]{2,1,0:T(8,128)(2,1)}), bf16[8,64,256]{2,1,0:T(8,128)(2,1)S(1)}, u32[]{:S(2)}, u32[]{:S(2)}) async-start(bf16[8,64,256]{2,1,0:T(8,128)(2,1)} %pad_maximum_fusion.4), calls=%async_computation.3 | async-start | bytes 524288 | tf_op jit(solution)/shard_map/all_to_all | solution.py:168
  124.4 5.4 %all-to-all-done.3 = bf16[8,64,256]{2,1,0:T(8,128)(2,1)S(1)} async-done(((bf16[8,64,256]{2,1,0:T(8,128)(2,1)}), bf16[8,64,256]{2,1,0:T(8,128)(2,1)S(1)}, u32[]{:S(2)}, u32[]{:S(2)}) %all-to-all-start.3) | async-done | bytes 262176 | tf_op jit(solution)/shard_map/all_to_all | solution.py:168
  (111 shorter events, 46.0 us)
Async XLA Ops:
  0.6 10.3 %copy-start.11 = (bf16[128,2048]{1,0:T(8,128)(2,1)S(1)}, bf16[128,2048]{1,0:T(8,128)(2,1)}, u32[]{:S(2)}) copy-start(bf16[128,2048]{1,0:T(8,128)(2,1)} %param.21) | copy-start | bytes 1572868
  0.6 10.6 %copy-start.12 = (bf16[128,2048]{1,0:T(8,128)(2,1)S(1)}, bf16[128,2048]{1,0:T(8,128)(2,1)}, u32[]{:S(2)}) copy-start(bf16[128,2048]{1,0:T(8,128)(2,1)} %param.24) | copy-start | bytes 1572868
  3.5 12.0 %all-to-all-start = ((bf16[8,64,256]{2,1,0:T(8,128)(2,1)}), bf16[8,64,256]{2,1,0:T(8,128)(2,1)S(1)}, u32[]{:S(2)}, u32[]{:S(2)}) async-start(bf16[8,64,256]{2,1,0:T(8,128)(2,1)} %bitcast.1), calls=%async_computation | async-start | bytes 524288 | tf_op jit(solution)/shard_map/all_to_all | solution.py:86
  15.5 28.5 %all-to-all-start.1 = ((bf16[128,8,512]{0,2,1:T(8,128)(2,1)}), bf16[128,8,512]{0,2,1:T(8,128)(2,1)S(1)}, u32[]{:S(2)}, u32[]{:S(2)}) async-start(bf16[128,8,512]{0,2,1:T(8,128)(2,1)} %pad_maximum_fusion.2), calls=%async_computation.1 | async-start | bytes 2097152 | tf_op jit(solution)/shard_map/all_to_all | solution.py:101
  19.1 12.6 %collective-permute-start.1 = (bf16[8,64,256]{2,1,0:T(8,128)(2,1)S(1)}, bf16[8,64,256]{2,1,0:T(8,128)(2,1)S(1)}, u32[]{:S(2)}, u32[]{:S(2)}) collective-permute-start(bf16[8,64,256]{2,1,0:T(8,128)(2,1)S(1)} %all-to-all-done), channel_id=1, source_target_pairs={{0,8},{8,16},{16,24},{24,32},{32,40},{40,48},{48,56},{56,64},{64,7... | collective-permute-start | bytes 786440 | tf_op jit(solution)/shard_map/ppermute | solution.py:20
  22.2 13.2 %collective-permute-start = (bf16[8,64,256]{2,1,0:T(8,128)(2,1)S(1)}, bf16[8,64,256]{2,1,0:T(8,128)(2,1)S(1)}, u32[]{:S(2)}, u32[]{:S(2)}) collective-permute-start(bf16[8,64,256]{2,1,0:T(8,128)(2,1)S(1)} %all-to-all-done), channel_id=1, source_target_pairs={{0,16},{8,24},{16,32},{24,40},{32,48},{40,56},{48,64},{56,72},{64,... | collective-permute-start | bytes 786440 | tf_op jit(solution)/shard_map/ppermute | solution.py:20
  29.7 12.4 %collective-permute-start.3 = (bf16[8,64,256]{2,1,0:T(8,128)(2,1)S(1)}, bf16[8,64,256]{2,1,0:T(8,128)(2,1)S(1)}, u32[]{:S(2)}, u32[]{:S(2)}) collective-permute-start(bf16[8,64,256]{2,1,0:T(8,128)(2,1)S(1)} %all-to-all-done), channel_id=1, source_target_pairs={{0,1},{1,0},{2,3},{3,2},{4,5},{5,4},{6,7},{7,6},{8,9},{9,8},{10,11... | collective-permute-start | bytes 786440 | tf_op jit(solution)/shard_map/ppermute | solution.py:109
  36.2 8.8 %collective-permute-start.2 = (bf16[2,8,64,256]{3,2,1,0:T(8,128)(2,1)}, bf16[2,8,64,256]{3,2,1,0:T(8,128)(2,1)}, u32[]{:S(2)}, u32[]{:S(2)}) collective-permute-start(bf16[2,8,64,256]{3,2,1,0:T(8,128)(2,1)} %pad_maximum_fusion.3), channel_id=1, source_target_pairs={{0,1},{1,0},{2,3},{3,2},{4,5},{5,4},{6,7},{7,6},{8,9},{9,8},{10,11... | collective-permute-start | bytes 1572872 | tf_op jit(solution)/shard_map/ppermute | solution.py:110
  48.9 1.1 copy-start.10
  52.5 1.1 copy-start.9
  53.5 15.6 %copy-start.3 = (bf16[2,256,2304]{1,2,0:T(8,128)(2,1)}, bf16[2,256,2304]{1,2,0:T(8,128)(2,1)S(1)}, u32[]{:S(2)}) copy-start(bf16[2,256,2304]{1,2,0:T(8,128)(2,1)S(1)} %fusion.19) | copy-start | bytes 7077892
  57.0 10.6 %copy-start.5 = (bf16[2,256,2304]{1,2,0:T(8,128)(2,1)}, bf16[2,256,2304]{1,2,0:T(8,128)(2,1)S(1)}, u32[]{:S(2)}) copy-start(bf16[2,256,2304]{1,2,0:T(8,128)(2,1)S(1)} %fusion.18) | copy-start | bytes 7077892
  58.1 1.4 %copy-start = (bf16[2,256,2304]{1,2,0:T(8,128)(2,1)}, bf16[2,256,2304]{1,2,0:T(8,128)(2,1)S(1)}, u32[]{:S(2)}) copy-start(bf16[2,256,2304]{1,2,0:T(8,128)(2,1)S(1)} %fusion.16) | copy-start | bytes 7077892
  66.7 1.5 %copy-start.7 = (bf16[2,256,2304]{1,2,0:T(8,128)(2,1)}, bf16[2,256,2304]{1,2,0:T(8,128)(2,1)S(1)}, u32[]{:S(2)}) copy-start(bf16[2,256,2304]{1,2,0:T(8,128)(2,1)S(1)} %fusion.17) | copy-start | bytes 7077892
  75.5 6.0 %copy-start.4 = (bf16[2,256,2304]{1,2,0:T(8,128)(2,1)S(1)}, bf16[2,256,2304]{1,2,0:T(8,128)(2,1)}, u32[]{:S(2)}) copy-start(bf16[2,256,2304]{1,2,0:T(8,128)(2,1)} %copy-done.3) | copy-start | bytes 7077892
  75.5 6.5 %copy-start.6 = (bf16[2,256,2304]{1,2,0:T(8,128)(2,1)S(1)}, bf16[2,256,2304]{1,2,0:T(8,128)(2,1)}, u32[]{:S(2)}) copy-start(bf16[2,256,2304]{1,2,0:T(8,128)(2,1)} %copy-done.5) | copy-start | bytes 7077892
  78.9 3.6 %copy-start.1 = (bf16[2,256,2304]{1,2,0:T(8,128)(2,1)S(1)}, bf16[2,256,2304]{1,2,0:T(8,128)(2,1)}, u32[]{:S(2)}) copy-start(bf16[2,256,2304]{1,2,0:T(8,128)(2,1)} %copy-done) | copy-start | bytes 7077892
  79.0 13.3 %collective-permute-start.4 = (f32[3,8,64,256]{3,2,1,0:T(8,128)}, f32[3,8,64,256]{3,2,1,0:T(8,128)}, u32[]{:S(2)}, u32[]{:S(2)}) collective-permute-start(f32[3,8,64,256]{3,2,1,0:T(8,128)} %select_bitcast_fusion), channel_id=1, source_target_pairs={{0,1},{1,0},{2,3},{3,2},{4,5},{5,4},{6,7},{7,6},{8,9},{9,8},{10,11... | collective-permute-start | bytes 4718600 | tf_op jit(solution)/shard_map/ppermute | solution.py:152
  82.0 1.7 %copy-start.8 = (bf16[2,256,2304]{1,2,0:T(8,128)(2,1)S(1)}, bf16[2,256,2304]{1,2,0:T(8,128)(2,1)}, u32[]{:S(2)}) copy-start(bf16[2,256,2304]{1,2,0:T(8,128)(2,1)} %copy-done.7) | copy-start | bytes 7077892
  85.3 6.9 %copy-start.2 = (f32[3072,256]{1,0:T(8,128)S(1)}, f32[3072,256]{1,0:T(8,128)}, u32[]{:S(2)}) copy-start(f32[3072,256]{1,0:T(8,128)} %copy.243) | copy-start | bytes 9437188
  87.8 20.5 %all-to-all-start.2 = ((bf16[8,128,512]{2,1,0:T(8,128)(2,1)}), bf16[8,128,512]{2,1,0:T(8,128)(2,1)}, u32[]{:S(2)}, u32[]{:S(2)}) async-start(bf16[8,128,512]{2,1,0:T(8,128)(2,1)} %bitcast.279), calls=%async_computation.2 | async-start | bytes 2097152 | tf_op jit(solution)/shard_map/all_to_all | solution.py:160
  95.2 16.0 %collective-permute-start.5 = (bf16[8,64,256]{2,1,0:T(8,128)(2,1)S(1)}, bf16[8,64,256]{2,1,0:T(8,128)(2,1)S(1)}, u32[]{:S(2)}, u32[]{:S(2)}) collective-permute-start(bf16[8,64,256]{2,1,0:T(8,128)(2,1)S(1)} %get-tuple-element.120), channel_id=1, source_target_pairs={{8,0},{16,8},{24,16},{32,24},{40,32},{48,40},{56,48},{64,56},{72,6... | collective-permute-start | bytes 786440 | tf_op jit(solution)/shard_map/ppermute | solution.py:20
  99.4 16.6 %collective-permute-start.6 = (bf16[8,64,256]{2,1,0:T(8,128)(2,1)S(1)}, bf16[8,64,256]{2,1,0:T(8,128)(2,1)S(1)}, u32[]{:S(2)}, u32[]{:S(2)}) collective-permute-start(bf16[8,64,256]{2,1,0:T(8,128)(2,1)S(1)} %get-tuple-element.121), channel_id=1, source_target_pairs={{16,0},{24,8},{32,16},{40,24},{48,32},{56,40},{64,48},{72,56},{80,... | collective-permute-start | bytes 786440 | tf_op jit(solution)/shard_map/ppermute | solution.py:20
  118.0 11.9 %all-to-all-start.3 = ((bf16[8,64,256]{2,1,0:T(8,128)(2,1)}), bf16[8,64,256]{2,1,0:T(8,128)(2,1)S(1)}, u32[]{:S(2)}, u32[]{:S(2)}) async-start(bf16[8,64,256]{2,1,0:T(8,128)(2,1)} %pad_maximum_fusion.4), calls=%async_computation.3 | async-start | bytes 524288 | tf_op jit(solution)/shard_map/all_to_all | solution.py:168
  (1 other events, 0.7 us)

commit v8 on v7

--- a/solution.py
+++ b/solution.py
@@ -144,9 +144,13 @@
         grad_k_all = grad_k_all.at[k_lo : k_lo + window].add(grad_k)
         grad_v_all = grad_v_all.at[k_lo : k_lo + window].add(grad_v)
     grad_kv_all = jnp.concatenate([grad_k_all, grad_v_all], axis=1)
-    grad_parts = grad_kv_all.reshape(reach_groups + 1, seq_width, 2, part_rows, 2 * HD)
-    low_rows = grad_parts[:, :, 0]
-    high_rows = grad_parts[:, :, 1]
+    half = span_rows // 2
+    low_rows = jnp.stack(
+        [grad_kv_all[g * span_rows : g * span_rows + half] for g in range(reach_groups)]
+    )
+    high_rows = jnp.stack(
+        [grad_kv_all[g * span_rows + half : (g + 1) * span_rows] for g in range(reach_groups)]
+    )
     mine_part = jnp.where(core == 0, low_rows, high_rows)
     their_part = jnp.where(core == 0, high_rows, low_rows)
     pair_sum = mine_part + lax.ppermute(their_part, "sp", sibling)
@@ -156,21 +160,21 @@
     ]
     attn_seq = jnp.concatenate(attn_parts, axis=0)
     dq_seq = jnp.concatenate(dq_parts, axis=0)
-    outgoing = jnp.concatenate([attn_seq, dq_seq], axis=1)
+    back_half = backs[0].astype(jnp.float32)
+    for back in backs[1:]:
+        back_half = back_half + back
+    kv_sum = grad_kv_all[own_start:]
+    kv_sum = lax.dynamic_update_slice_in_dim(
+        kv_sum, lax.dynamic_slice_in_dim(kv_sum, core * half, half, 0) + back_half, core * half, 0
+    )
+    kv_sum = jnp.concatenate([kv_sum[:, :HD] * score_scale, kv_sum[:, HD:]], axis=1)
+    outgoing = jnp.concatenate([attn_seq, dq_seq, kv_sum.astype(jnp.bfloat16)], axis=1)
     back_all = lax.all_to_all(outgoing, "sp", split_axis=0, concat_axis=1, tiled=True)
     back_all = back_all.reshape(tok_dev, seq_width, outgoing.shape[1])
     attn_out = back_all[:, :, :q_width].reshape(tok_dev, heads_q * HD)
-    grad_queries = back_all[:, :, q_width:].reshape(tok_dev, heads_q * HD)
-    kv_sum = pair_sum[reach_groups]
-    for back in backs:
-        kv_sum = kv_sum + back
-    kv_sum = jnp.concatenate([kv_sum[..., :HD] * score_scale, kv_sum[..., HD:]], axis=-1)
-    kv_back = lax.all_to_all(
-        kv_sum.astype(jnp.bfloat16), "sp", split_axis=0, concat_axis=0, tiled=True
-    )
-    kv_back = jnp.transpose(
-        kv_back.reshape(heads_k, 2, part_rows, 2 * HD), (1, 2, 0, 3)
-    ).reshape(tok_dev, heads_k, 2 * HD)
+    grad_queries = back_all[:, :, q_width : 2 * q_width].reshape(tok_dev, heads_q * HD)
+    kv_back = back_all[:, :, 2 * q_width :].astype(jnp.float32)
+    kv_back = jnp.sum(kv_back.reshape(tok_dev, heads_k, seq_width // heads_k, 2 * HD), axis=2)
     grad_keys = kv_back[:, :, :HD].reshape(tok_dev, heads_k * HD)
     grad_values = kv_back[:, :, HD:].reshape(tok_dev, heads_k * HD)
     return (

time: 132 us -> 135 us (1.023)
  the two profiles are of different devices: /device:TPU:100 before, /device:TPU:228 now
where the time goes in v8:
time: 135 us; the launch traced here: 134 us
  starting transfers between devices  29.4 us (22%)
  blocking collectives  26.1 us (19%)
  other arithmetic  23 us (17%)
  matrix products  21.2 us (16%)
  local copies, waits for them, and re-layouts  18.9 us (14%)
  waiting for transfers between devices  14.4 us (11%)
  between operations  1.36 us (1%)
    all_to_all x1, blocking collectives, local(): lax.all_to_all(outgoing, 'sp', split_axis=0, concat_axis=1, tiled=True)  26.1 us
    ppermute x4, starting transfers between devices, passed_along(): lax.ppermute(value, axis, [(source, source + steps) for source in range(f...  15 us
    ppermute x4, waiting for transfers between devices, passed_along(): lax.ppermute(value, axis, [(source, source + steps) for source in range(f...  13.2 us
    and x2, other arithmetic, local(): (q_label[:, None] == k_label[None, :]) & (k_place[None, :] <= q_place[:,...  7.67 us
    unnamed x41, local copies, waits for them, and re-layouts  5.25 us
    all_to_all x1, starting transfers between devices, local(): lax.all_to_all(kv_send, 'sp', split_axis=0, concat_axis=0, tiled=True)  4.47 us
    dot_general x4, matrix products, block_pass(): jnp.einsum('hqk,qhd->kd', probs_bf, g_block, preferred_element_type=jnp.f...  4.3 us
    dot_general x4, matrix products, block_pass(): jnp.einsum('qhd,kd->hqk', g_block, v_win, preferred_element_type=jnp.floa...  4.04 us
  transfers between devices with their start and end apart: 9, of which 4 were waited for; matrix products, arithmetic and copies ran while one was open for 18% of the time, Pallas kernels for 0%

profile of v8, /device:TPU:228, one launch (start us, length us, event | category | flops | bytes accessed | tf_op | source)
XLA Modules:
  0.0 134.3 jit_solution(6683929404839015706)
XLA Ops:
  3.5 4.5 %all-to-all-start = ((bf16[8,64,256]{2,1,0:T(8,128)(2,1)}), bf16[8,64,256]{2,1,0:T(8,128)(2,1)S(1)}, u32[]{:S(2)}, u32[]{:S(2)}) async-start(bf16[8,64,256]{2,1,0:T(8,128)(2,1)} %bitcast.1), calls=%async_computation | async-start | bytes 524288 | tf_op jit(solution)/shard_map/all_to_all | solution.py:86
  10.2 1.9 %convert_reduce_fusion = s32[3072]{0:T(1024)S(1)} fusion(s32[128]{0:T(128)S(1)} %multiply_reduce_fusion.4, s32[3072]{0:T(1024)S(1)} %iota_add_fusion), kind=kLoop, calls=%fused_computation.74 | loop fusion | flops 1176576 | bytes 25088 | tf_op jit(solution)/shard_map/reduce_sum | solution.py:30
  14.3 1.2 all-to-all-done
  15.5 3.8 %all-to-all-start.1 = ((bf16[128,8,512]{0,2,1:T(8,128)(2,1)}), bf16[128,8,512]{0,2,1:T(8,128)(2,1)S(1)}, u32[]{:S(2)}, u32[]{:S(2)}) async-start(bf16[128,8,512]{0,2,1:T(8,128)(2,1)} %pad_maximum_fusion.2), calls=%async_computation.1 | async-start | bytes 2097152 | tf_op jit(solution)/shard_map/all_to_all | solution.py:101
  19.3 3.1 %collective-permute-start.1 = (bf16[8,64,256]{2,1,0:T(8,128)(2,1)S(1)}, bf16[8,64,256]{2,1,0:T(8,128)(2,1)S(1)}, u32[]{:S(2)}, u32[]{:S(2)}) collective-permute-start(bf16[8,64,256]{2,1,0:T(8,128)(2,1)S(1)} %all-to-all-done), channel_id=1, source_target_pairs={{0,8},{8,16},{16,24},{24,32},{32,40},{40,48},{48,56},{56,64},{64,7... | collective-permute-start | bytes 786440 | tf_op jit(solution)/shard_map/ppermute | solution.py:20
  22.4 5.3 %collective-permute-start = (bf16[8,64,256]{2,1,0:T(8,128)(2,1)S(1)}, bf16[8,64,256]{2,1,0:T(8,128)(2,1)S(1)}, u32[]{:S(2)}, u32[]{:S(2)}) collective-permute-start(bf16[8,64,256]{2,1,0:T(8,128)(2,1)S(1)} %all-to-all-done), channel_id=1, source_target_pairs={{0,16},{8,24},{16,32},{24,40},{32,48},{40,56},{48,64},{56,72},{64,... | collective-permute-start | bytes 786440 | tf_op jit(solution)/shard_map/ppermute | solution.py:20
  27.7 3.8 %compare_and_fusion = (pred[256,2304]{0,1:T(8,128)(4,1)}, pred[256,2304]{0,1:T(8,128)(4,1)S(1)}) fusion(s32[256]{0:T(256)S(1)} %get-tuple-element.144, s32[256]{0:T(256)S(1)} %get-tuple-element.140, s32[2304]{0:T(1024)S(1)} %get-tuple-element.136, s32[2304]{0:T(1024)S(1)} %get-tuple-element.132, s32[256]{0:T(256)S(1)} %get-tuple-element.145, ...), kind=kLoop, calls=%fused_computation.68 | loop fusion | flops 3538944 | bytes 1220608 | tf_op jit(solution)/shard_map/and | solution.py:131
  31.5 1.9 %collective-permute-start.3 = (bf16[8,64,256]{2,1,0:T(8,128)(2,1)S(1)}, bf16[8,64,256]{2,1,0:T(8,128)(2,1)S(1)}, u32[]{:S(2)}, u32[]{:S(2)}) collective-permute-start(bf16[8,64,256]{2,1,0:T(8,128)(2,1)S(1)} %all-to-all-done), channel_id=1, source_target_pairs={{0,1},{1,0},{2,3},{3,2},{4,5},{5,4},{6,7},{7,6},{8,9},{9,8},{10,11... | collective-permute-start | bytes 786440 | tf_op jit(solution)/shard_map/ppermute | solution.py:109
  33.4 2.3 %collective-permute-done = bf16[8,64,256]{2,1,0:T(8,128)(2,1)S(1)} collective-permute-done((bf16[8,64,256]{2,1,0:T(8,128)(2,1)S(1)}, bf16[8,64,256]{2,1,0:T(8,128)(2,1)S(1)}, u32[]{:S(2)}, u32[]{:S(2)}) %collective-permute-start) | collective-permute-done | bytes 262176 | tf_op jit(solution)/shard_map/ppermute | solution.py:20
  36.5 1.9 %collective-permute-start.2 = (bf16[2,8,64,256]{3,2,1,0:T(8,128)(2,1)}, bf16[2,8,64,256]{3,2,1,0:T(8,128)(2,1)}, u32[]{:S(2)}, u32[]{:S(2)}) collective-permute-start(bf16[2,8,64,256]{3,2,1,0:T(8,128)(2,1)} %pad_maximum_fusion.6), channel_id=1, source_target_pairs={{0,1},{1,0},{2,3},{3,2},{4,5},{5,4},{6,7},{7,6},{8,9},{9,8},{10,11... | collective-permute-start | bytes 1572872 | tf_op jit(solution)/shard_map/ppermute | solution.py:110
  38.5 3.8 %compare_and_fusion.2 = (pred[256,2304]{0,1:T(8,128)(4,1)}, pred[256,2304]{0,1:T(8,128)(4,1)S(1)}) fusion(s32[256]{0:T(256)S(1)} %get-tuple-element.146, s32[256]{0:T(256)S(1)} %copy-done.15, s32[2304]{0:T(1024)S(1)} %get-tuple-element.138, s32[2304]{0:T(1024)S(1)} %get-tuple-element.134, s32[256]{0:T(256)S(1)} %copy-done.14, s32[2304]{0:T(1024)S(1)} %copy-done.13, ...), kind=kLoop, calls=%fused_computation.70 | loop fusion | flops 3538944 | bytes 1220608 | tf_op jit(solution)/shard_map/and | solution.py:131
  60.7 1.1 fusion.33
  64.2 1.1 fusion.35
  69.5 1.4 %fusion.41 = f32[2,512,256]{1,2,0:T(8,128)} fusion(f32[1,512,256]{1,2,0:T(8,128)S(1)} %get-tuple-element.114, f32[1,512,256]{1,2,0:T(8,128)S(1)} %get-tuple-element.115, f32[1,512,256]{1,2,0:T(8,128)S(1)} %get-tuple-element.113, f32[1,512,256]{1,2,0:T(8,128)S(1)} %get-tuple-element.112, pred[]{:T(512)S(6)} %eq.77), kind=kLoop, calls=%fused_computation.93 | loop fusion | flops 786432 | bytes 3145729 | tf_op jit(solution)/shard_map/jit(_where)/select_n | solution.py:155
  70.9 2.4 %collective-permute-start.4 = (f32[2,512,256]{1,2,0:T(8,128)}, f32[2,512,256]{1,2,0:T(8,128)}, u32[]{:S(2)}, u32[]{:S(2)}) collective-permute-start(f32[2,512,256]{1,2,0:T(8,128)} %fusion.41), channel_id=1, source_target_pairs={{0,1},{1,0},{2,3},{3,2},{4,5},{5,4},{6,7},{7,6},{8,9},{9,8},{10,11... | collective-permute-start | bytes 3145736 | tf_op jit(solution)/shard_map/ppermute | solution.py:156
  76.3 2.0 %copy.267 = bf16[1024,256]{1,0:T(8,128)(2,1)} copy(bf16[1024,256]{0,1:T(8,128)(2,1)} %pad_maximum_fusion.8) | data formatting | bytes 1048576 | tf_op jit(solution)/shard_map/concatenate | solution.py:162
  78.3 2.1 %add_convert_fusion = bf16[2,512,256]{1,2,0:T(8,128)(2,1)S(1)} fusion(f32[2,512,256]{1,2,0:T(8,128)} %collective-permute-done.4, f32[1,512,256]{1,2,0:T(8,128)} %copy-done.2, f32[1,512,256]{1,2,0:T(8,128)} %copy-done.3, f32[1,512,256]{1,2,0:T(8,128)} %copy-done.1, f32[1,512,256]{1,2,0:T(8,128)} %copy-done, pred[]{:T(512)S(6)} %eq.77), kind=kLoop, calls=%fused_computation.92 | loop fusion | flops 1310720 | bytes 3670017 | tf_op jit(solution)/shard_map/convert.9
  81.3 4.5 %collective-permute-start.5 = (bf16[512,256]{0,1:T(8,128)(2,1)}, bf16[512,256]{0,1:T(8,128)(2,1)}, u32[]{:S(2)}, u32[]{:S(2)}) collective-permute-start(bf16[512,256]{0,1:T(8,128)(2,1)} %get-tuple-element.126), channel_id=1, source_target_pairs={{8,0},{16,8},{24,16},{32,24},{40,32},{48,40},{56,48},{64,56},{72,6... | collective-permute-start | bytes 786440 | tf_op jit(solution)/shard_map/ppermute | solution.py:20
  85.8 2.1 %collective-permute-start.6 = (bf16[512,256]{0,1:T(8,128)(2,1)}, bf16[512,256]{0,1:T(8,128)(2,1)}, u32[]{:S(2)}, u32[]{:S(2)}) collective-permute-start(bf16[512,256]{0,1:T(8,128)(2,1)} %get-tuple-element.127), channel_id=1, source_target_pairs={{16,0},{24,8},{32,16},{40,24},{48,32},{56,40},{64,48},{72,56},{80,... | collective-permute-start | bytes 786440 | tf_op jit(solution)/shard_map/ppermute | solution.py:20
  88.8 2.0 %copy.254 = bf16[1024,256]{1,0:T(8,128)(2,1)} copy(bf16[1024,256]{0,1:T(8,128)(2,1)} %pad_maximum_fusion.7) | data formatting | bytes 1048576 | tf_op jit(solution)/shard_map/concatenate | solution.py:161
  91.0 6.6 %collective-permute-done.5 = bf16[512,256]{0,1:T(8,128)(2,1)} collective-permute-done((bf16[512,256]{0,1:T(8,128)(2,1)}, bf16[512,256]{0,1:T(8,128)(2,1)}, u32[]{:S(2)}, u32[]{:S(2)}) %collective-permute-start.5) | collective-permute-done | bytes 262176 | tf_op jit(solution)/shard_map/ppermute | solution.py:20
  97.5 4.3 %collective-permute-done.6 = bf16[512,256]{0,1:T(8,128)(2,1)} collective-permute-done((bf16[512,256]{0,1:T(8,128)(2,1)}, bf16[512,256]{0,1:T(8,128)(2,1)}, u32[]{:S(2)}, u32[]{:S(2)}) %collective-permute-start.6) | collective-permute-done | bytes 262176 | tf_op jit(solution)/shard_map/ppermute | solution.py:20
  101.9 1.2 add_dynamic-update-slice_fusion
  103.6 26.1 %all_to_all.33 = bf16[8,128,768]{2,1,0:T(8,128)(2,1)S(1)} all-to-all(bf16[8,128,768]{2,1,0:T(8,128)(2,1)S(1)} %pad_maximum_fusion.1), channel_id=1, replica_groups=mesh['fsdp'=64,'sp'=8] {'sp'}, dimensions={0} | all-to-all | bytes 3145728 | tf_op jit(solution)/shard_map/all_to_all | solution.py:172
  (119 shorter events, 42.6 us)
Async XLA Ops:
  0.6 12.0 %copy-start.10 = (bf16[128,2048]{1,0:T(8,128)(2,1)S(1)}, bf16[128,2048]{1,0:T(8,128)(2,1)}, u32[]{:S(2)}) copy-start(bf16[128,2048]{1,0:T(8,128)(2,1)} %param.21) | copy-start | bytes 1572868
  0.6 12.3 %copy-start.11 = (bf16[128,2048]{1,0:T(8,128)(2,1)S(1)}, bf16[128,2048]{1,0:T(8,128)(2,1)}, u32[]{:S(2)}) copy-start(bf16[128,2048]{1,0:T(8,128)(2,1)} %param.24) | copy-start | bytes 1572868
  3.5 12.0 %all-to-all-start = ((bf16[8,64,256]{2,1,0:T(8,128)(2,1)}), bf16[8,64,256]{2,1,0:T(8,128)(2,1)S(1)}, u32[]{:S(2)}, u32[]{:S(2)}) async-start(bf16[8,64,256]{2,1,0:T(8,128)(2,1)} %bitcast.1), calls=%async_computation | async-start | bytes 524288 | tf_op jit(solution)/shard_map/all_to_all | solution.py:86
  14.3 24.1 %copy-start.13 = (s32[2304]{0:T(1024)S(1)}, s32[2304]{0:T(1024)}, u32[]{:S(2)}) copy-start(s32[2304]{0:T(1024)} %get-tuple-element.139) | copy-start | bytes 27652
  14.3 24.1 %copy-start.14 = (s32[256]{0:T(256)S(1)}, s32[256]{0:T(256)}, u32[]{:S(2)}) copy-start(s32[256]{0:T(256)} %get-tuple-element.147) | copy-start | bytes 3076
  14.3 24.2 %copy-start.15 = (s32[256]{0:T(256)S(1)}, s32[256]{0:T(256)}, u32[]{:S(2)}) copy-start(s32[256]{0:T(256)} %get-tuple-element.142) | copy-start | bytes 3076
  14.3 24.2 %copy-start.16 = (s32[256]{0:T(256)S(1)}, s32[256]{0:T(256)}, u32[]{:S(2)}) copy-start(s32[256]{0:T(256)} %get-tuple-element.143) | copy-start | bytes 3076
  15.5 28.6 %all-to-all-start.1 = ((bf16[128,8,512]{0,2,1:T(8,128)(2,1)}), bf16[128,8,512]{0,2,1:T(8,128)(2,1)S(1)}, u32[]{:S(2)}, u32[]{:S(2)}) async-start(bf16[128,8,512]{0,2,1:T(8,128)(2,1)} %pad_maximum_fusion.2), calls=%async_computation.1 | async-start | bytes 2097152 | tf_op jit(solution)/shard_map/all_to_all | solution.py:101
  19.3 14.1 %collective-permute-start.1 = (bf16[8,64,256]{2,1,0:T(8,128)(2,1)S(1)}, bf16[8,64,256]{2,1,0:T(8,128)(2,1)S(1)}, u32[]{:S(2)}, u32[]{:S(2)}) collective-permute-start(bf16[8,64,256]{2,1,0:T(8,128)(2,1)S(1)} %all-to-all-done), channel_id=1, source_target_pairs={{0,8},{8,16},{16,24},{24,32},{32,40},{40,48},{48,56},{56,64},{64,7... | collective-permute-start | bytes 786440 | tf_op jit(solution)/shard_map/ppermute | solution.py:20
  22.4 13.3 %collective-permute-start = (bf16[8,64,256]{2,1,0:T(8,128)(2,1)S(1)}, bf16[8,64,256]{2,1,0:T(8,128)(2,1)S(1)}, u32[]{:S(2)}, u32[]{:S(2)}) collective-permute-start(bf16[8,64,256]{2,1,0:T(8,128)(2,1)S(1)} %all-to-all-done), channel_id=1, source_target_pairs={{0,16},{8,24},{16,32},{24,40},{32,48},{40,56},{48,64},{56,72},{64,... | collective-permute-start | bytes 786440 | tf_op jit(solution)/shard_map/ppermute | solution.py:20
  31.5 10.8 %collective-permute-start.3 = (bf16[8,64,256]{2,1,0:T(8,128)(2,1)S(1)}, bf16[8,64,256]{2,1,0:T(8,128)(2,1)S(1)}, u32[]{:S(2)}, u32[]{:S(2)}) collective-permute-start(bf16[8,64,256]{2,1,0:T(8,128)(2,1)S(1)} %all-to-all-done), channel_id=1, source_target_pairs={{0,1},{1,0},{2,3},{3,2},{4,5},{5,4},{6,7},{7,6},{8,9},{9,8},{10,11... | collective-permute-start | bytes 786440 | tf_op jit(solution)/shard_map/ppermute | solution.py:109
  36.5 8.7 %collective-permute-start.2 = (bf16[2,8,64,256]{3,2,1,0:T(8,128)(2,1)}, bf16[2,8,64,256]{3,2,1,0:T(8,128)(2,1)}, u32[]{:S(2)}, u32[]{:S(2)}) collective-permute-start(bf16[2,8,64,256]{3,2,1,0:T(8,128)(2,1)} %pad_maximum_fusion.6), channel_id=1, source_target_pairs={{0,1},{1,0},{2,3},{3,2},{4,5},{5,4},{6,7},{7,6},{8,9},{9,8},{10,11... | collective-permute-start | bytes 1572872 | tf_op jit(solution)/shard_map/ppermute | solution.py:110
  60.7 1.1 copy-start.8
  64.2 1.1 copy-start.6
  69.5 5.9 %copy-start = (f32[1,512,256]{1,2,0:T(8,128)}, f32[1,512,256]{1,2,0:T(8,128)S(1)}, u32[]{:S(2)}) copy-start(f32[1,512,256]{1,2,0:T(8,128)S(1)} %get-tuple-element.112) | copy-start | bytes 1572868
  69.5 5.9 %copy-start.1 = (f32[1,512,256]{1,2,0:T(8,128)}, f32[1,512,256]{1,2,0:T(8,128)S(1)}, u32[]{:S(2)}) copy-start(f32[1,512,256]{1,2,0:T(8,128)S(1)} %get-tuple-element.113) | copy-start | bytes 1572868
  69.5 5.9 %copy-start.2 = (f32[1,512,256]{1,2,0:T(8,128)}, f32[1,512,256]{1,2,0:T(8,128)S(1)}, u32[]{:S(2)}) copy-start(f32[1,512,256]{1,2,0:T(8,128)S(1)} %get-tuple-element.114) | copy-start | bytes 1572868
  69.5 5.9 %copy-start.3 = (f32[1,512,256]{1,2,0:T(8,128)}, f32[1,512,256]{1,2,0:T(8,128)S(1)}, u32[]{:S(2)}) copy-start(f32[1,512,256]{1,2,0:T(8,128)S(1)} %get-tuple-element.115) | copy-start | bytes 1572868
  70.9 7.4 %collective-permute-start.4 = (f32[2,512,256]{1,2,0:T(8,128)}, f32[2,512,256]{1,2,0:T(8,128)}, u32[]{:S(2)}, u32[]{:S(2)}) collective-permute-start(f32[2,512,256]{1,2,0:T(8,128)} %fusion.41), channel_id=1, source_target_pairs={{0,1},{1,0},{2,3},{3,2},{4,5},{5,4},{6,7},{7,6},{8,9},{9,8},{10,11... | collective-permute-start | bytes 3145736 | tf_op jit(solution)/shard_map/ppermute | solution.py:156
  78.3 9.6 %copy-start.7 = (bf16[128,2,256]{2,0,1:T(8,128)(2,1)S(1)}, bf16[128,2,256]{2,0,1:T(8,128)(2,1)}, u32[]{:S(2)}) copy-start(bf16[128,2,256]{2,0,1:T(8,128)(2,1)} %copy-done.6) | copy-start | bytes 393220
  81.3 16.2 %collective-permute-start.5 = (bf16[512,256]{0,1:T(8,128)(2,1)}, bf16[512,256]{0,1:T(8,128)(2,1)}, u32[]{:S(2)}, u32[]{:S(2)}) collective-permute-start(bf16[512,256]{0,1:T(8,128)(2,1)} %get-tuple-element.126), channel_id=1, source_target_pairs={{8,0},{16,8},{24,16},{32,24},{40,32},{48,40},{56,48},{64,56},{72,6... | collective-permute-start | bytes 786440 | tf_op jit(solution)/shard_map/ppermute | solution.py:20
  85.8 16.0 %collective-permute-start.6 = (bf16[512,256]{0,1:T(8,128)(2,1)}, bf16[512,256]{0,1:T(8,128)(2,1)}, u32[]{:S(2)}, u32[]{:S(2)}) collective-permute-start(bf16[512,256]{0,1:T(8,128)(2,1)} %get-tuple-element.127), channel_id=1, source_target_pairs={{16,0},{24,8},{32,16},{40,24},{48,32},{56,40},{64,48},{72,56},{80,... | collective-permute-start | bytes 786440 | tf_op jit(solution)/shard_map/ppermute | solution.py:20
  90.9 12.5 %copy-start.4 = (bf16[1024,256]{1,0:T(8,128)(2,1)S(1)}, bf16[1024,256]{1,0:T(8,128)(2,1)}, u32[]{:S(2)}) copy-start(bf16[1024,256]{1,0:T(8,128)(2,1)} %copy.267) | copy-start | bytes 1572868
  90.9 12.5 %copy-start.5 = (bf16[1024,256]{1,0:T(8,128)(2,1)S(1)}, bf16[1024,256]{1,0:T(8,128)(2,1)}, u32[]{:S(2)}) copy-start(bf16[1024,256]{1,0:T(8,128)(2,1)} %copy.254) | copy-start | bytes 1572868
  (2 other events, 1.8 us)

commit v9 on v8

--- a/solution.py
+++ b/solution.py
@@ -160,6 +160,11 @@
     ]
     attn_seq = jnp.concatenate(attn_parts, axis=0)
     dq_seq = jnp.concatenate(dq_parts, axis=0)
+    outgoing = jnp.concatenate([attn_seq, dq_seq], axis=1)
+    back_all = lax.all_to_all(outgoing, "sp", split_axis=0, concat_axis=1, tiled=True)
+    back_all = back_all.reshape(tok_dev, seq_width, outgoing.shape[1])
+    attn_out = back_all[:, :, :q_width].reshape(tok_dev, heads_q * HD)
+    grad_queries = back_all[:, :, q_width:].reshape(tok_dev, heads_q * HD)
     back_half = backs[0].astype(jnp.float32)
     for back in backs[1:]:
         back_half = back_half + back
@@ -168,12 +173,10 @@
         kv_sum, lax.dynamic_slice_in_dim(kv_sum, core * half, half, 0) + back_half, core * half, 0
     )
     kv_sum = jnp.concatenate([kv_sum[:, :HD] * score_scale, kv_sum[:, HD:]], axis=1)
-    outgoing = jnp.concatenate([attn_seq, dq_seq, kv_sum.astype(jnp.bfloat16)], axis=1)
-    back_all = lax.all_to_all(outgoing, "sp", split_axis=0, concat_axis=1, tiled=True)
-    back_all = back_all.reshape(tok_dev, seq_width, outgoing.shape[1])
-    attn_out = back_all[:, :, :q_width].reshape(tok_dev, heads_q * HD)
-    grad_queries = back_all[:, :, q_width : 2 * q_width].reshape(tok_dev, heads_q * HD)
-    kv_back = back_all[:, :, 2 * q_width :].astype(jnp.float32)
+    kv_back = lax.all_to_all(
+        kv_sum.astype(jnp.bfloat16), "sp", split_axis=0, concat_axis=1, tiled=True
+    )
+    kv_back = kv_back.reshape(tok_dev, seq_width, 2 * HD).astype(jnp.float32)
     kv_back = jnp.sum(kv_back.reshape(tok_dev, heads_k, seq_width // heads_k, 2 * HD), axis=2)
     grad_keys = kv_back[:, :, :HD].reshape(tok_dev, heads_k * HD)
     grad_values = kv_back[:, :, HD:].reshape(tok_dev, heads_k * HD)

time: 135 us -> 125 us (0.926)
  the two profiles are of different devices: /device:TPU:228 before, /device:TPU:384 now
where the time goes in v9:
time: 125 us
  starting transfers between devices  36.2 us (29%)
  waiting for transfers between devices  30.6 us (24%)
  matrix products  21.2 us (17%)
  other arithmetic  18.7 us (15%)
  local copies, waits for them, and re-layouts  16.8 us (13%)
  between operations  1.34 us (1%)
    ppermute x4, starting transfers between devices, passed_along(): lax.ppermute(value, axis, [(source, source + steps) for source in range(f...  13.8 us
    all_to_all x1, waiting for transfers between devices, local(): lax.all_to_all(outgoing, 'sp', split_axis=0, concat_axis=1, tiled=True)  12 us
    ppermute x4, waiting for transfers between devices, passed_along(): lax.ppermute(value, axis, [(source, source + steps) for source in range(f...  10.7 us
    all_to_all x1, waiting for transfers between devices, local(): lax.all_to_all(kv_sum.astype(jnp.bfloat16), 'sp', split_axis=0, concat_ax...  6.53 us
    and x2, other arithmetic, local(): (q_label[:, None] == k_label[None, :]) & (k_place[None, :] <= q_place[:,...  6.27 us
    all_to_all x1, starting transfers between devices, local(): lax.all_to_all(kv_send, 'sp', split_axis=0, concat_axis=0, tiled=True)  4.47 us
    all_to_all x1, starting transfers between devices, local(): lax.all_to_all(outgoing, 'sp', split_axis=0, concat_axis=1, tiled=True)  4.45 us
    unnamed x35, local copies, waits for them, and re-layouts  4.42 us
  transfers between devices with their start and end apart: 11, of which 7 were waited for; matrix products, arithmetic and copies ran while one was open for 22% of the time, Pallas kernels for 0%

profile of v9, /device:TPU:384, one launch (start us, length us, event | category | flops | bytes accessed | tf_op | source)
XLA Modules:
  0.0 124.7 jit_solution(9655448425182240245)
XLA Ops:
  3.5 4.5 %all-to-all-start = ((bf16[8,64,256]{2,1,0:T(8,128)(2,1)}), bf16[8,64,256]{2,1,0:T(8,128)(2,1)S(1)}, u32[]{:S(2)}, u32[]{:S(2)}) async-start(bf16[8,64,256]{2,1,0:T(8,128)(2,1)} %bitcast.1), calls=%async_computation | async-start | bytes 524288 | tf_op jit(solution)/shard_map/all_to_all | solution.py:86
  9.0 1.9 %convert_reduce_fusion = s32[3072]{0:T(1024)S(1)} fusion(s32[128]{0:T(128)S(1)} %multiply_reduce_fusion.4, s32[3072]{0:T(1024)S(1)} %iota_add_fusion), kind=kLoop, calls=%fused_computation.73 | loop fusion | flops 1176576 | bytes 25088 | tf_op jit(solution)/shard_map/reduce_sum | solution.py:30
  15.5 3.7 %all-to-all-start.1 = ((bf16[128,8,512]{0,2,1:T(8,128)(2,1)}), bf16[128,8,512]{0,2,1:T(8,128)(2,1)S(1)}, u32[]{:S(2)}, u32[]{:S(2)}) async-start(bf16[128,8,512]{0,2,1:T(8,128)(2,1)} %pad_maximum_fusion.1), calls=%async_computation.1 | async-start | bytes 2097152 | tf_op jit(solution)/shard_map/all_to_all | solution.py:101
  19.3 4.9 %collective-permute-start = (bf16[8,64,256]{2,1,0:T(8,128)(2,1)S(1)}, bf16[8,64,256]{2,1,0:T(8,128)(2,1)S(1)}, u32[]{:S(2)}, u32[]{:S(2)}) collective-permute-start(bf16[8,64,256]{2,1,0:T(8,128)(2,1)S(1)} %all-to-all-done), channel_id=1, source_target_pairs={{0,16},{8,24},{16,32},{24,40},{32,48},{40,56},{48,64},{56,72},{64,... | collective-permute-start | bytes 786440 | tf_op jit(solution)/shard_map/ppermute | solution.py:20
  24.2 2.5 %collective-permute-start.1 = (bf16[8,64,256]{2,1,0:T(8,128)(2,1)S(1)}, bf16[8,64,256]{2,1,0:T(8,128)(2,1)S(1)}, u32[]{:S(2)}, u32[]{:S(2)}) collective-permute-start(bf16[8,64,256]{2,1,0:T(8,128)(2,1)S(1)} %all-to-all-done), channel_id=1, source_target_pairs={{0,8},{8,16},{16,24},{24,32},{32,40},{40,48},{48,56},{56,64},{64,7... | collective-permute-start | bytes 786440 | tf_op jit(solution)/shard_map/ppermute | solution.py:20
  26.7 2.2 %compare_and_fusion.2 = (pred[256,2304]{0,1:T(8,128)(4,1)S(1)}, pred[256,2304]{0,1:T(8,128)(4,1)S(1)}) fusion(s32[256]{0:T(256)S(1)} %copy-done.13, s32[256]{0:T(256)S(1)} %copy-done.11, s32[2304]{0:T(1024)S(1)} %get-tuple-element.135, s32[2304]{0:T(1024)S(1)} %copy-done.6, s32[256]{0:T(256)S(1)} %copy-done.12, s32[2304]{0:T(1024)S(1)} %get-tuple-element.132, ...), kind=kLoop, calls=%fused_computation.70 | loop fusion | flops 3538944 | bytes 1220608 | tf_op jit(solution)/shard_map/and | solution.py:131
  29.0 1.9 %collective-permute-start.3 = (bf16[8,64,256]{2,1,0:T(8,128)(2,1)S(1)}, bf16[8,64,256]{2,1,0:T(8,128)(2,1)}, u32[]{:S(2)}, u32[]{:S(2)}) collective-permute-start(bf16[8,64,256]{2,1,0:T(8,128)(2,1)S(1)} %all-to-all-done), channel_id=1, source_target_pairs={{0,1},{1,0},{2,3},{3,2},{4,5},{5,4},{6,7},{7,6},{8,9},{9,8},{10,11... | collective-permute-start | bytes 786440 | tf_op jit(solution)/shard_map/ppermute | solution.py:109
  30.9 2.6 %collective-permute-done = bf16[8,64,256]{2,1,0:T(8,128)(2,1)S(1)} collective-permute-done((bf16[8,64,256]{2,1,0:T(8,128)(2,1)S(1)}, bf16[8,64,256]{2,1,0:T(8,128)(2,1)S(1)}, u32[]{:S(2)}, u32[]{:S(2)}) %collective-permute-start) | collective-permute-done | bytes 262176 | tf_op jit(solution)/shard_map/ppermute | solution.py:20
  33.6 6.1 %collective-permute-done.1 = bf16[8,64,256]{2,1,0:T(8,128)(2,1)S(1)} collective-permute-done((bf16[8,64,256]{2,1,0:T(8,128)(2,1)S(1)}, bf16[8,64,256]{2,1,0:T(8,128)(2,1)S(1)}, u32[]{:S(2)}, u32[]{:S(2)}) %collective-permute-start.1) | collective-permute-done | bytes 262176 | tf_op jit(solution)/shard_map/ppermute | solution.py:20
  40.6 1.9 %collective-permute-start.2 = (bf16[2,8,64,256]{3,2,1,0:T(8,128)(2,1)}, bf16[2,8,64,256]{3,2,1,0:T(8,128)(2,1)}, u32[]{:S(2)}, u32[]{:S(2)}) collective-permute-start(bf16[2,8,64,256]{3,2,1,0:T(8,128)(2,1)} %pad_maximum_fusion.5), channel_id=1, source_target_pairs={{0,1},{1,0},{2,3},{3,2},{4,5},{5,4},{6,7},{7,6},{8,9},{9,8},{10,11... | collective-permute-start | bytes 1572872 | tf_op jit(solution)/shard_map/ppermute | solution.py:110
  42.5 4.0 %compare_and_fusion = (pred[256,2304]{0,1:T(8,128)(4,1)}, pred[256,2304]{0,1:T(8,128)(4,1)}) fusion(s32[256]{0:T(256)S(1)} %copy-done.9, s32[256]{0:T(256)S(1)} %get-tuple-element.137, s32[2304]{0:T(1024)S(1)} %get-tuple-element.133, s32[2304]{0:T(1024)S(1)} %get-tuple-element.129, s32[256]{0:T(256)S(1)} %copy-done.8, s32[2304]{0:T(1024)S(1)} %get-tuple-element.134, ...), kind=kLoop, calls=%fused_computation.68 | loop fusion | flops 3538944 | bytes 1220608 | tf_op jit(solution)/shard_map/and | solution.py:131
  56.1 1.1 fusion.31
  62.2 1.2 convolution_convert_fusion
  73.1 2.4 %collective-permute-start.4 = (f32[2,512,256]{1,2,0:T(8,128)S(1)}, f32[2,512,256]{1,2,0:T(8,128)S(1)}, u32[]{:S(2)}, u32[]{:S(2)}) collective-permute-start(f32[2,512,256]{1,2,0:T(8,128)S(1)} %fusion.41), channel_id=1, source_target_pairs={{0,1},{1,0},{2,3},{3,2},{4,5},{5,4},{6,7},{7,6},{8,9},{9,8},{10,11... | collective-permute-start | bytes 3145736 | tf_op jit(solution)/shard_map/ppermute | solution.py:156
  79.0 2.3 %collective-permute-start.5 = (bf16[512,256]{0,1:T(8,128)(2,1)}, bf16[512,256]{0,1:T(8,128)(2,1)S(1)}, u32[]{:S(2)}, u32[]{:S(2)}) collective-permute-start(bf16[512,256]{0,1:T(8,128)(2,1)} %get-tuple-element.122), channel_id=1, source_target_pairs={{8,0},{16,8},{24,16},{32,24},{40,32},{48,40},{56,48},{64,56},{72,6... | collective-permute-start | bytes 786440 | tf_op jit(solution)/shard_map/ppermute | solution.py:20
  81.3 4.1 %collective-permute-start.6 = (bf16[512,256]{0,1:T(8,128)(2,1)}, bf16[512,256]{0,1:T(8,128)(2,1)}, u32[]{:S(2)}, u32[]{:S(2)}) collective-permute-start(bf16[512,256]{0,1:T(8,128)(2,1)} %get-tuple-element.123), channel_id=1, source_target_pairs={{16,0},{24,8},{32,16},{40,24},{48,32},{56,40},{64,48},{72,56},{80,... | collective-permute-start | bytes 786440 | tf_op jit(solution)/shard_map/ppermute | solution.py:20
  85.3 1.2 maximum_maximum_fusion
  86.5 2.3 %copy.215 = bf16[1024,512]{1,0:T(8,128)(2,1)} copy(bf16[1024,512]{0,1:T(8,128)(2,1)} %maximum_maximum_fusion) | data formatting | bytes 2097152 | tf_op jit(solution)/shard_map/concatenate | solution.py:163
  88.8 4.4 %all-to-all-start.2 = ((bf16[8,128,512]{2,1,0:T(8,128)(2,1)}), bf16[8,128,512]{2,1,0:T(8,128)(2,1)}, u32[]{:S(2)}, u32[]{:S(2)}) async-start(bf16[8,128,512]{2,1,0:T(8,128)(2,1)} %bitcast.258), calls=%async_computation.2 | async-start | bytes 2097152 | tf_op jit(solution)/shard_map/all_to_all | solution.py:164
  93.4 1.9 %collective-permute-done.5 = bf16[512,256]{0,1:T(8,128)(2,1)S(1)} collective-permute-done((bf16[512,256]{0,1:T(8,128)(2,1)}, bf16[512,256]{0,1:T(8,128)(2,1)S(1)}, u32[]{:S(2)}, u32[]{:S(2)}) %collective-permute-start.5) | collective-permute-done | bytes 262176 | tf_op jit(solution)/shard_map/ppermute | solution.py:20
  97.3 12.0 %all-to-all-done.2 = bf16[8,128,512]{2,1,0:T(8,128)(2,1)} async-done(((bf16[8,128,512]{2,1,0:T(8,128)(2,1)}), bf16[8,128,512]{2,1,0:T(8,128)(2,1)}, u32[]{:S(2)}, u32[]{:S(2)}) %all-to-all-start.2) | async-done | bytes 1048608 | tf_op jit(solution)/shard_map/all_to_all | solution.py:164
  109.3 3.5 %all-to-all-start.3 = ((bf16[8,128,256]{1,2,0:T(8,128)(2,1)}), bf16[8,128,256]{1,2,0:T(8,128)(2,1)S(1)}, u32[]{:S(2)}, u32[]{:S(2)}) async-start(bf16[8,128,256]{1,2,0:T(8,128)(2,1)} %pad_maximum_fusion.6), calls=%async_computation.3 | async-start | bytes 1048576 | tf_op jit(solution)/shard_map/all_to_all | solution.py:176
  112.8 1.6 %copy.216 = bf16[8,128,512]{1,2,0:T(8,128)(2,1)S(1)} copy(bf16[8,128,512]{2,1,0:T(8,128)(2,1)} %all-to-all-done.2) | data formatting | bytes 2097152 | tf_op jit(solution)/shard_map/all_to_all | solution.py:164
  116.6 6.5 %all-to-all-done.3 = bf16[8,128,256]{1,2,0:T(8,128)(2,1)S(1)} async-done(((bf16[8,128,256]{1,2,0:T(8,128)(2,1)}), bf16[8,128,256]{1,2,0:T(8,128)(2,1)S(1)}, u32[]{:S(2)}, u32[]{:S(2)}) %all-to-all-start.3) | async-done | bytes 524320 | tf_op jit(solution)/shard_map/all_to_all | solution.py:176
  (112 shorter events, 42.5 us)
Async XLA Ops:
  0.6 12.1 %copy-start.2 = (bf16[128,2048]{1,0:T(8,128)(2,1)S(1)}, bf16[128,2048]{1,0:T(8,128)(2,1)}, u32[]{:S(2)}) copy-start(bf16[128,2048]{1,0:T(8,128)(2,1)} %param.21) | copy-start | bytes 1572868
  0.6 12.4 %copy-start.3 = (bf16[128,2048]{1,0:T(8,128)(2,1)S(1)}, bf16[128,2048]{1,0:T(8,128)(2,1)}, u32[]{:S(2)}) copy-start(bf16[128,2048]{1,0:T(8,128)(2,1)} %param.24) | copy-start | bytes 1572868
  3.5 12.0 %all-to-all-start = ((bf16[8,64,256]{2,1,0:T(8,128)(2,1)}), bf16[8,64,256]{2,1,0:T(8,128)(2,1)S(1)}, u32[]{:S(2)}, u32[]{:S(2)}) async-start(bf16[8,64,256]{2,1,0:T(8,128)(2,1)} %bitcast.1), calls=%async_computation | async-start | bytes 524288 | tf_op jit(solution)/shard_map/all_to_all | solution.py:86
  13.3 13.4 %copy-start.5 = (s32[2304]{0:T(1024)S(1)}, s32[2304]{0:T(1024)}, u32[]{:S(2)}) copy-start(s32[2304]{0:T(1024)} %get-tuple-element.128) | copy-start | bytes 27652
  13.3 13.4 %copy-start.6 = (s32[2304]{0:T(1024)S(1)}, s32[2304]{0:T(1024)}, u32[]{:S(2)}) copy-start(s32[2304]{0:T(1024)} %get-tuple-element.131) | copy-start | bytes 27652
  13.3 13.4 %copy-start.10 = (s32[256]{0:T(256)S(1)}, s32[256]{0:T(256)}, u32[]{:S(2)}) copy-start(s32[256]{0:T(256)} %get-tuple-element.136) | copy-start | bytes 3076
  13.3 13.4 %copy-start.11 = (s32[256]{0:T(256)S(1)}, s32[256]{0:T(256)}, u32[]{:S(2)}) copy-start(s32[256]{0:T(256)} %get-tuple-element.139) | copy-start | bytes 3076
  13.3 13.4 %copy-start.12 = (s32[256]{0:T(256)S(1)}, s32[256]{0:T(256)}, u32[]{:S(2)}) copy-start(s32[256]{0:T(256)} %get-tuple-element.140) | copy-start | bytes 3076
  13.3 13.4 %copy-start.13 = (s32[256]{0:T(256)S(1)}, s32[256]{0:T(256)}, u32[]{:S(2)}) copy-start(s32[256]{0:T(256)} %get-tuple-element.142) | copy-start | bytes 3076
  14.4 28.1 %copy-start.4 = (s32[2304]{0:T(1024)S(1)}, s32[2304]{0:T(1024)}, u32[]{:S(2)}) copy-start(s32[2304]{0:T(1024)} %get-tuple-element.130) | copy-start | bytes 27652
  14.4 28.1 %copy-start.7 = (s32[256]{0:T(256)S(1)}, s32[256]{0:T(256)}, u32[]{:S(2)}) copy-start(s32[256]{0:T(256)} %get-tuple-element.138) | copy-start | bytes 3076
  14.4 28.1 %copy-start.8 = (s32[256]{0:T(256)S(1)}, s32[256]{0:T(256)}, u32[]{:S(2)}) copy-start(s32[256]{0:T(256)} %get-tuple-element.141) | copy-start | bytes 3076
  14.4 28.1 %copy-start.9 = (s32[256]{0:T(256)S(1)}, s32[256]{0:T(256)}, u32[]{:S(2)}) copy-start(s32[256]{0:T(256)} %get-tuple-element.143) | copy-start | bytes 3076
  15.5 32.1 %all-to-all-start.1 = ((bf16[128,8,512]{0,2,1:T(8,128)(2,1)}), bf16[128,8,512]{0,2,1:T(8,128)(2,1)S(1)}, u32[]{:S(2)}, u32[]{:S(2)}) async-start(bf16[128,8,512]{0,2,1:T(8,128)(2,1)} %pad_maximum_fusion.1), calls=%async_computation.1 | async-start | bytes 2097152 | tf_op jit(solution)/shard_map/all_to_all | solution.py:101
  19.3 14.3 %collective-permute-start = (bf16[8,64,256]{2,1,0:T(8,128)(2,1)S(1)}, bf16[8,64,256]{2,1,0:T(8,128)(2,1)S(1)}, u32[]{:S(2)}, u32[]{:S(2)}) collective-permute-start(bf16[8,64,256]{2,1,0:T(8,128)(2,1)S(1)} %all-to-all-done), channel_id=1, source_target_pairs={{0,16},{8,24},{16,32},{24,40},{32,48},{40,56},{48,64},{56,72},{64,... | collective-permute-start | bytes 786440 | tf_op jit(solution)/shard_map/ppermute | solution.py:20
  24.2 15.5 %collective-permute-start.1 = (bf16[8,64,256]{2,1,0:T(8,128)(2,1)S(1)}, bf16[8,64,256]{2,1,0:T(8,128)(2,1)S(1)}, u32[]{:S(2)}, u32[]{:S(2)}) collective-permute-start(bf16[8,64,256]{2,1,0:T(8,128)(2,1)S(1)} %all-to-all-done), channel_id=1, source_target_pairs={{0,8},{8,16},{16,24},{24,32},{32,40},{40,48},{48,56},{56,64},{64,7... | collective-permute-start | bytes 786440 | tf_op jit(solution)/shard_map/ppermute | solution.py:20
  29.0 17.6 %collective-permute-start.3 = (bf16[8,64,256]{2,1,0:T(8,128)(2,1)S(1)}, bf16[8,64,256]{2,1,0:T(8,128)(2,1)}, u32[]{:S(2)}, u32[]{:S(2)}) collective-permute-start(bf16[8,64,256]{2,1,0:T(8,128)(2,1)S(1)} %all-to-all-done), channel_id=1, source_target_pairs={{0,1},{1,0},{2,3},{3,2},{4,5},{5,4},{6,7},{7,6},{8,9},{9,8},{10,11... | collective-permute-start | bytes 786440 | tf_op jit(solution)/shard_map/ppermute | solution.py:109
  40.6 8.2 %collective-permute-start.2 = (bf16[2,8,64,256]{3,2,1,0:T(8,128)(2,1)}, bf16[2,8,64,256]{3,2,1,0:T(8,128)(2,1)}, u32[]{:S(2)}, u32[]{:S(2)}) collective-permute-start(bf16[2,8,64,256]{3,2,1,0:T(8,128)(2,1)} %pad_maximum_fusion.5), channel_id=1, source_target_pairs={{0,1},{1,0},{2,3},{3,2},{4,5},{5,4},{6,7},{7,6},{8,9},{9,8},{10,11... | collective-permute-start | bytes 1572872 | tf_op jit(solution)/shard_map/ppermute | solution.py:110
  56.1 1.1 copy-start.1
  73.1 4.7 %collective-permute-start.4 = (f32[2,512,256]{1,2,0:T(8,128)S(1)}, f32[2,512,256]{1,2,0:T(8,128)S(1)}, u32[]{:S(2)}, u32[]{:S(2)}) collective-permute-start(f32[2,512,256]{1,2,0:T(8,128)S(1)} %fusion.41), channel_id=1, source_target_pairs={{0,1},{1,0},{2,3},{3,2},{4,5},{5,4},{6,7},{7,6},{8,9},{9,8},{10,11... | collective-permute-start | bytes 3145736 | tf_op jit(solution)/shard_map/ppermute | solution.py:156
  79.0 16.3 %collective-permute-start.5 = (bf16[512,256]{0,1:T(8,128)(2,1)}, bf16[512,256]{0,1:T(8,128)(2,1)S(1)}, u32[]{:S(2)}, u32[]{:S(2)}) collective-permute-start(bf16[512,256]{0,1:T(8,128)(2,1)} %get-tuple-element.122), channel_id=1, source_target_pairs={{8,0},{16,8},{24,16},{32,24},{40,32},{48,40},{56,48},{64,56},{72,6... | collective-permute-start | bytes 786440 | tf_op jit(solution)/shard_map/ppermute | solution.py:20
  81.3 14.0 %collective-permute-start.6 = (bf16[512,256]{0,1:T(8,128)(2,1)}, bf16[512,256]{0,1:T(8,128)(2,1)}, u32[]{:S(2)}, u32[]{:S(2)}) collective-permute-start(bf16[512,256]{0,1:T(8,128)(2,1)} %get-tuple-element.123), channel_id=1, source_target_pairs={{16,0},{24,8},{32,16},{40,24},{48,32},{56,40},{64,48},{72,56},{80,... | collective-permute-start | bytes 786440 | tf_op jit(solution)/shard_map/ppermute | solution.py:20
  88.8 20.5 %all-to-all-start.2 = ((bf16[8,128,512]{2,1,0:T(8,128)(2,1)}), bf16[8,128,512]{2,1,0:T(8,128)(2,1)}, u32[]{:S(2)}, u32[]{:S(2)}) async-start(bf16[8,128,512]{2,1,0:T(8,128)(2,1)} %bitcast.258), calls=%async_computation.2 | async-start | bytes 2097152 | tf_op jit(solution)/shard_map/all_to_all | solution.py:164
  109.3 13.8 %all-to-all-start.3 = ((bf16[8,128,256]{1,2,0:T(8,128)(2,1)}), bf16[8,128,256]{1,2,0:T(8,128)(2,1)S(1)}, u32[]{:S(2)}, u32[]{:S(2)}) async-start(bf16[8,128,256]{1,2,0:T(8,128)(2,1)} %pad_maximum_fusion.6), calls=%async_computation.3 | async-start | bytes 1048576 | tf_op jit(solution)/shard_map/all_to_all | solution.py:176
  (1 other events, 1.1 us)

commit v10 on v9

--- a/solution.py
+++ b/solution.py
@@ -160,23 +160,23 @@
     ]
     attn_seq = jnp.concatenate(attn_parts, axis=0)
     dq_seq = jnp.concatenate(dq_parts, axis=0)
-    outgoing = jnp.concatenate([attn_seq, dq_seq], axis=1)
+    own_sum = grad_kv_all[own_start:]
+    own_sum = jnp.concatenate([own_sum[:, :HD] * score_scale, own_sum[:, HD:]], axis=1)
+    outgoing = jnp.concatenate([attn_seq, dq_seq, own_sum.astype(jnp.bfloat16)], axis=1)
     back_all = lax.all_to_all(outgoing, "sp", split_axis=0, concat_axis=1, tiled=True)
     back_all = back_all.reshape(tok_dev, seq_width, outgoing.shape[1])
     attn_out = back_all[:, :, :q_width].reshape(tok_dev, heads_q * HD)
-    grad_queries = back_all[:, :, q_width:].reshape(tok_dev, heads_q * HD)
+    grad_queries = back_all[:, :, q_width : 2 * q_width].reshape(tok_dev, heads_q * HD)
     back_half = backs[0].astype(jnp.float32)
     for back in backs[1:]:
         back_half = back_half + back
-    kv_sum = grad_kv_all[own_start:]
-    kv_sum = lax.dynamic_update_slice_in_dim(
-        kv_sum, lax.dynamic_slice_in_dim(kv_sum, core * half, half, 0) + back_half, core * half, 0
-    )
-    kv_sum = jnp.concatenate([kv_sum[:, :HD] * score_scale, kv_sum[:, HD:]], axis=1)
-    kv_back = lax.all_to_all(
-        kv_sum.astype(jnp.bfloat16), "sp", split_axis=0, concat_axis=1, tiled=True
-    )
+    back_half = jnp.concatenate([back_half[:, :HD] * score_scale, back_half[:, HD:]], axis=1)
+    back_full = lax.dynamic_update_slice_in_dim(
+        jnp.zeros((span_rows, 2 * HD), jnp.bfloat16), back_half.astype(jnp.bfloat16), core * half, 0
+    )
+    kv_back = lax.all_to_all(back_full, "sp", split_axis=0, concat_axis=1, tiled=True)
     kv_back = kv_back.reshape(tok_dev, seq_width, 2 * HD).astype(jnp.float32)
+    kv_back = kv_back + back_all[:, :, 2 * q_width :].astype(jnp.float32)
     kv_back = jnp.sum(kv_back.reshape(tok_dev, heads_k, seq_width // heads_k, 2 * HD), axis=2)
     grad_keys = kv_back[:, :, :HD].reshape(tok_dev, heads_k * HD)
     grad_values = kv_back[:, :, HD:].reshape(tok_dev, heads_k * HD)

time: 125 us -> 141 us (1.13)
  the two profiles are of different devices: /device:TPU:384 before, /device:TPU:228 now
where the time goes in v10:
time: 141 us; the launch traced here: 140 us
  starting transfers between devices  38.1 us (27%)
  local copies, waits for them, and re-layouts  28.8 us (20%)
  matrix products  24.5 us (17%)
  waiting for transfers between devices  23.6 us (17%)
  other arithmetic  23.4 us (17%)
    ppermute x4, waiting for transfers between devices, passed_along(): lax.ppermute(value, axis, [(source, source + steps) for source in range(f...  16.6 us
    ppermute x4, starting transfers between devices, passed_along(): lax.ppermute(value, axis, [(source, source + steps) for source in range(f...  14.8 us
    and x2, other arithmetic, local(): (q_label[:, None] == k_label[None, :]) & (k_place[None, :] <= q_place[:,...  7.67 us
    dot_general x4, matrix products, block_pass(): jnp.einsum('hqk,kd->qhd', dscores, k_win, preferred_element_type=jnp.floa...  6.44 us
    unnamed x43, local copies, waits for them, and re-layouts  6.04 us
    reshape x4, local copies, waits for them, and re-layouts, local(): dq_parts.append(dq_block.reshape(Q_ROWS, local_q * HD))  6 us
    all_to_all x1, waiting for transfers between devices, local(): lax.all_to_all(back_full, 'sp', split_axis=0, concat_axis=1, tiled=True)  5.82 us
    reshape x4, local copies, waits for them, and re-layouts, local(): attn_parts.append(attn_block.reshape(Q_ROWS, local_q * HD))  4.91 us
  transfers between devices with their start and end apart: 11, of which 5 were waited for; matrix products, arithmetic and copies ran while one was open for 31% of the time, Pallas kernels for 0%

profile of v10, /device:TPU:228, one launch (start us, length us, event | category | flops | bytes accessed | tf_op | source)
XLA Modules:
  0.0 139.9 jit_solution(11435715145288613778)
XLA Ops:
  3.5 4.5 %all-to-all-start = ((bf16[8,64,256]{2,1,0:T(8,128)(2,1)}), bf16[8,64,256]{2,1,0:T(8,128)(2,1)S(1)}, u32[]{:S(2)}, u32[]{:S(2)}) async-start(bf16[8,64,256]{2,1,0:T(8,128)(2,1)} %bitcast.1), calls=%async_computation | async-start | bytes 524288 | tf_op jit(solution)/shard_map/all_to_all | solution.py:86
  10.2 1.9 %convert_reduce_fusion = s32[3072]{0:T(1024)S(1)} fusion(s32[128]{0:T(128)S(1)} %multiply_reduce_fusion.4, s32[3072]{0:T(1024)S(1)} %iota_add_fusion), kind=kLoop, calls=%fused_computation.64 | loop fusion | flops 1176576 | bytes 25088 | tf_op jit(solution)/shard_map/reduce_sum | solution.py:30
  15.5 3.7 %all-to-all-start.1 = ((bf16[128,8,512]{0,2,1:T(8,128)(2,1)}), bf16[128,8,512]{0,2,1:T(8,128)(2,1)S(1)}, u32[]{:S(2)}, u32[]{:S(2)}) async-start(bf16[128,8,512]{0,2,1:T(8,128)(2,1)} %pad_maximum_fusion.2), calls=%async_computation.1 | async-start | bytes 2097152 | tf_op jit(solution)/shard_map/all_to_all | solution.py:101
  19.2 3.1 %collective-permute-start.1 = (bf16[8,64,256]{2,1,0:T(8,128)(2,1)S(1)}, bf16[8,64,256]{2,1,0:T(8,128)(2,1)S(1)}, u32[]{:S(2)}, u32[]{:S(2)}) collective-permute-start(bf16[8,64,256]{2,1,0:T(8,128)(2,1)S(1)} %all-to-all-done), channel_id=1, source_target_pairs={{0,8},{8,16},{16,24},{24,32},{32,40},{40,48},{48,56},{56,64},{64,7... | collective-permute-start | bytes 786440 | tf_op jit(solution)/shard_map/ppermute | solution.py:20
  22.3 5.3 %collective-permute-start = (bf16[8,64,256]{2,1,0:T(8,128)(2,1)S(1)}, bf16[8,64,256]{2,1,0:T(8,128)(2,1)S(1)}, u32[]{:S(2)}, u32[]{:S(2)}) collective-permute-start(bf16[8,64,256]{2,1,0:T(8,128)(2,1)S(1)} %all-to-all-done), channel_id=1, source_target_pairs={{0,16},{8,24},{16,32},{24,40},{32,48},{40,56},{48,64},{56,72},{64,... | collective-permute-start | bytes 786440 | tf_op jit(solution)/shard_map/ppermute | solution.py:20
  27.6 3.8 %compare_and_fusion = (pred[256,2304]{0,1:T(8,128)(4,1)S(1)}, pred[256,2304]{0,1:T(8,128)(4,1)}) fusion(s32[256]{0:T(256)S(1)} %get-tuple-element.152, s32[256]{0:T(256)S(1)} %get-tuple-element.148, s32[2304]{0:T(1024)S(1)} %get-tuple-element.144, s32[2304]{0:T(1024)S(1)} %get-tuple-element.140, s32[256]{0:T(256)S(1)} %get-tuple-element.153, ...), kind=kLoop, calls=%fused_computation.58 | loop fusion | flops 3538944 | bytes 1220608 | tf_op jit(solution)/shard_map/and | solution.py:131
  31.5 1.9 %collective-permute-start.3 = (bf16[8,64,256]{2,1,0:T(8,128)(2,1)S(1)}, bf16[8,64,256]{2,1,0:T(8,128)(2,1)S(1)}, u32[]{:S(2)}, u32[]{:S(2)}) collective-permute-start(bf16[8,64,256]{2,1,0:T(8,128)(2,1)S(1)} %all-to-all-done), channel_id=1, source_target_pairs={{0,1},{1,0},{2,3},{3,2},{4,5},{5,4},{6,7},{7,6},{8,9},{9,8},{10,11... | collective-permute-start | bytes 786440 | tf_op jit(solution)/shard_map/ppermute | solution.py:109
  33.4 2.2 %collective-permute-done = bf16[8,64,256]{2,1,0:T(8,128)(2,1)S(1)} collective-permute-done((bf16[8,64,256]{2,1,0:T(8,128)(2,1)S(1)}, bf16[8,64,256]{2,1,0:T(8,128)(2,1)S(1)}, u32[]{:S(2)}, u32[]{:S(2)}) %collective-permute-start) | collective-permute-done | bytes 262176 | tf_op jit(solution)/shard_map/ppermute | solution.py:20
  36.5 1.9 %collective-permute-start.2 = (bf16[2,8,64,256]{3,2,1,0:T(8,128)(2,1)}, bf16[2,8,64,256]{3,2,1,0:T(8,128)(2,1)}, u32[]{:S(2)}, u32[]{:S(2)}) collective-permute-start(bf16[2,8,64,256]{3,2,1,0:T(8,128)(2,1)} %pad_maximum_fusion.6), channel_id=1, source_target_pairs={{0,1},{1,0},{2,3},{3,2},{4,5},{5,4},{6,7},{7,6},{8,9},{9,8},{10,11... | collective-permute-start | bytes 1572872 | tf_op jit(solution)/shard_map/ppermute | solution.py:110
  38.4 3.8 %compare_and_fusion.2 = (pred[256,2304]{0,1:T(8,128)(4,1)}, pred[256,2304]{0,1:T(8,128)(4,1)S(1)}) fusion(s32[256]{0:T(256)S(1)} %get-tuple-element.154, s32[256]{0:T(256)S(1)} %copy-done.16, s32[2304]{0:T(1024)S(1)} %get-tuple-element.146, s32[2304]{0:T(1024)S(1)} %get-tuple-element.142, s32[256]{0:T(256)S(1)} %copy-done.15, s32[2304]{0:T(1024)S(1)} %copy-done.14, ...), kind=kLoop, calls=%fused_computation.60 | loop fusion | flops 3538944 | bytes 1220608 | tf_op jit(solution)/shard_map/and | solution.py:131
  72.8 2.4 %collective-permute-start.4 = (f32[2,512,256]{2,1,0:T(8,128)}, f32[2,512,256]{2,1,0:T(8,128)}, u32[]{:S(2)}, u32[]{:S(2)}) collective-permute-start(f32[2,512,256]{2,1,0:T(8,128)} %fusion.38), channel_id=1, source_target_pairs={{0,1},{1,0},{2,3},{3,2},{4,5},{5,4},{6,7},{7,6},{8,9},{9,8},{10,11... | collective-permute-start | bytes 3145736 | tf_op jit(solution)/shard_map/ppermute | solution.py:156
  77.9 1.7 %copy.324 = bf16[256,256]{1,0:T(8,128)(2,1)} copy(bf16[256,256]{0,1:T(8,128)(2,1)} %bitcast.298) | data formatting | bytes 262144 | tf_op jit(solution)/shard_map/reshape | solution.py:143
  79.6 1.7 %copy.309 = bf16[256,256]{1,0:T(8,128)(2,1)} copy(bf16[256,256]{0,1:T(8,128)(2,1)} %bitcast.280) | data formatting | bytes 262144 | tf_op jit(solution)/shard_map/reshape | solution.py:142
  81.2 1.7 %copy.325 = bf16[256,256]{1,0:T(8,128)(2,1)} copy(bf16[256,256]{0,1:T(8,128)(2,1)} %bitcast.299) | data formatting | bytes 262144 | tf_op jit(solution)/shard_map/reshape | solution.py:143
  83.7 1.7 %copy.323 = bf16[256,256]{1,0:T(8,128)(2,1)} copy(bf16[256,256]{0,1:T(8,128)(2,1)} %bitcast.300) | data formatting | bytes 262144 | tf_op jit(solution)/shard_map/reshape | solution.py:143
  85.4 1.7 %copy.310 = bf16[256,256]{1,0:T(8,128)(2,1)} copy(bf16[256,256]{0,1:T(8,128)(2,1)} %bitcast.282) | data formatting | bytes 262144 | tf_op jit(solution)/shard_map/reshape | solution.py:142
  87.0 2.9 %fusion.37 = bf16[128,2,256]{2,0,1:T(8,128)(2,1)} fusion(bf16[2,256,2304]{1,2,0:T(8,128)(2,1)} %copy-done, bf16[3072,256]{1,0:T(8,128)(2,1)S(1)} %pad_maximum_fusion), kind=kOutput, calls=%fused_computation.76 | convolution fusion | flops 302120960 | bytes 3080192 | tf_op jit(solution)/shard_map/hqk,kd->qhd/dot_general | solution.py:60
  94.5 4.6 %all-to-all-start.2 = ((bf16[8,128,768]{2,1,0:T(8,128)(2,1)}), bf16[8,128,768]{2,1,0:T(8,128)(2,1)S(1)}, u32[]{:S(2)}, u32[]{:S(2)}) async-start(bf16[8,128,768]{2,1,0:T(8,128)(2,1)} %pad_maximum_fusion.1), calls=%async_computation.2 | async-start | bytes 3145728 | tf_op jit(solution)/shard_map/all_to_all | solution.py:166
  100.7 4.1 %collective-permute-start.5 = (bf16[512,256]{1,0:T(8,128)(2,1)S(1)}, bf16[512,256]{1,0:T(8,128)(2,1)S(1)}, u32[]{:S(2)}, u32[]{:S(2)}) collective-permute-start(bf16[512,256]{1,0:T(8,128)(2,1)S(1)} %get-tuple-element.134), channel_id=1, source_target_pairs={{8,0},{16,8},{24,16},{32,24},{40,32},{48,40},{56,48},{64,56},{72,6... | collective-permute-start | bytes 786440 | tf_op jit(solution)/shard_map/ppermute | solution.py:20
  104.8 2.3 %collective-permute-start.6 = (bf16[512,256]{1,0:T(8,128)(2,1)S(1)}, bf16[512,256]{1,0:T(8,128)(2,1)S(1)}, u32[]{:S(2)}, u32[]{:S(2)}) collective-permute-start(bf16[512,256]{1,0:T(8,128)(2,1)S(1)} %get-tuple-element.135), channel_id=1, source_target_pairs={{16,0},{24,8},{32,16},{40,24},{48,32},{56,40},{64,48},{72,56},{80,... | collective-permute-start | bytes 786440 | tf_op jit(solution)/shard_map/ppermute | solution.py:20
  107.1 9.5 %collective-permute-done.5 = bf16[512,256]{1,0:T(8,128)(2,1)S(1)} collective-permute-done((bf16[512,256]{1,0:T(8,128)(2,1)S(1)}, bf16[512,256]{1,0:T(8,128)(2,1)S(1)}, u32[]{:S(2)}, u32[]{:S(2)}) %collective-permute-start.5) | collective-permute-done | bytes 262176 | tf_op jit(solution)/shard_map/ppermute | solution.py:20
  116.7 4.8 %collective-permute-done.6 = bf16[512,256]{1,0:T(8,128)(2,1)S(1)} collective-permute-done((bf16[512,256]{1,0:T(8,128)(2,1)S(1)}, bf16[512,256]{1,0:T(8,128)(2,1)S(1)}, u32[]{:S(2)}, u32[]{:S(2)}) %collective-permute-start.6) | collective-permute-done | bytes 262176 | tf_op jit(solution)/shard_map/ppermute | solution.py:20
  123.2 4.3 %all-to-all-start.3 = ((bf16[8,128,256]{2,1,0:T(8,128)(2,1)}), bf16[8,128,256]{2,1,0:T(8,128)(2,1)S(1)}, u32[]{:S(2)}, u32[]{:S(2)}) async-start(bf16[8,128,256]{2,1,0:T(8,128)(2,1)} %bitcast.91), calls=%async_computation.3 | async-start | bytes 1048576 | tf_op jit(solution)/shard_map/all_to_all | solution.py:177
  132.0 5.8 %all-to-all-done.3 = bf16[8,128,256]{2,1,0:T(8,128)(2,1)S(1)} async-done(((bf16[8,128,256]{2,1,0:T(8,128)(2,1)}), bf16[8,128,256]{2,1,0:T(8,128)(2,1)S(1)}, u32[]{:S(2)}, u32[]{:S(2)}) %all-to-all-start.3) | async-done | bytes 524320 | tf_op jit(solution)/shard_map/all_to_all | solution.py:177
  (136 shorter events, 57.3 us)
Async XLA Ops:
  0.6 12.0 %copy-start.11 = (bf16[128,2048]{1,0:T(8,128)(2,1)S(1)}, bf16[128,2048]{1,0:T(8,128)(2,1)}, u32[]{:S(2)}) copy-start(bf16[128,2048]{1,0:T(8,128)(2,1)} %param.21) | copy-start | bytes 1572868
  0.6 12.3 %copy-start.12 = (bf16[128,2048]{1,0:T(8,128)(2,1)S(1)}, bf16[128,2048]{1,0:T(8,128)(2,1)}, u32[]{:S(2)}) copy-start(bf16[128,2048]{1,0:T(8,128)(2,1)} %param.24) | copy-start | bytes 1572868
  3.5 12.0 %all-to-all-start = ((bf16[8,64,256]{2,1,0:T(8,128)(2,1)}), bf16[8,64,256]{2,1,0:T(8,128)(2,1)S(1)}, u32[]{:S(2)}, u32[]{:S(2)}) async-start(bf16[8,64,256]{2,1,0:T(8,128)(2,1)} %bitcast.1), calls=%async_computation | async-start | bytes 524288 | tf_op jit(solution)/shard_map/all_to_all | solution.py:86
  14.3 24.1 %copy-start.14 = (s32[2304]{0:T(1024)S(1)}, s32[2304]{0:T(1024)}, u32[]{:S(2)}) copy-start(s32[2304]{0:T(1024)} %get-tuple-element.147) | copy-start | bytes 27652
  14.3 24.1 %copy-start.15 = (s32[256]{0:T(256)S(1)}, s32[256]{0:T(256)}, u32[]{:S(2)}) copy-start(s32[256]{0:T(256)} %get-tuple-element.155) | copy-start | bytes 3076
  14.3 24.2 %copy-start.16 = (s32[256]{0:T(256)S(1)}, s32[256]{0:T(256)}, u32[]{:S(2)}) copy-start(s32[256]{0:T(256)} %get-tuple-element.150) | copy-start | bytes 3076
  14.3 24.2 %copy-start.17 = (s32[256]{0:T(256)S(1)}, s32[256]{0:T(256)}, u32[]{:S(2)}) copy-start(s32[256]{0:T(256)} %get-tuple-element.151) | copy-start | bytes 3076
  15.5 28.6 %all-to-all-start.1 = ((bf16[128,8,512]{0,2,1:T(8,128)(2,1)}), bf16[128,8,512]{0,2,1:T(8,128)(2,1)S(1)}, u32[]{:S(2)}, u32[]{:S(2)}) async-start(bf16[128,8,512]{0,2,1:T(8,128)(2,1)} %pad_maximum_fusion.2), calls=%async_computation.1 | async-start | bytes 2097152 | tf_op jit(solution)/shard_map/all_to_all | solution.py:101
  19.2 14.1 %collective-permute-start.1 = (bf16[8,64,256]{2,1,0:T(8,128)(2,1)S(1)}, bf16[8,64,256]{2,1,0:T(8,128)(2,1)S(1)}, u32[]{:S(2)}, u32[]{:S(2)}) collective-permute-start(bf16[8,64,256]{2,1,0:T(8,128)(2,1)S(1)} %all-to-all-done), channel_id=1, source_target_pairs={{0,8},{8,16},{16,24},{24,32},{32,40},{40,48},{48,56},{56,64},{64,7... | collective-permute-start | bytes 786440 | tf_op jit(solution)/shard_map/ppermute | solution.py:20
  22.3 13.3 %collective-permute-start = (bf16[8,64,256]{2,1,0:T(8,128)(2,1)S(1)}, bf16[8,64,256]{2,1,0:T(8,128)(2,1)S(1)}, u32[]{:S(2)}, u32[]{:S(2)}) collective-permute-start(bf16[8,64,256]{2,1,0:T(8,128)(2,1)S(1)} %all-to-all-done), channel_id=1, source_target_pairs={{0,16},{8,24},{16,32},{24,40},{32,48},{40,56},{48,64},{56,72},{64,... | collective-permute-start | bytes 786440 | tf_op jit(solution)/shard_map/ppermute | solution.py:20
  31.5 10.8 %collective-permute-start.3 = (bf16[8,64,256]{2,1,0:T(8,128)(2,1)S(1)}, bf16[8,64,256]{2,1,0:T(8,128)(2,1)S(1)}, u32[]{:S(2)}, u32[]{:S(2)}) collective-permute-start(bf16[8,64,256]{2,1,0:T(8,128)(2,1)S(1)} %all-to-all-done), channel_id=1, source_target_pairs={{0,1},{1,0},{2,3},{3,2},{4,5},{5,4},{6,7},{7,6},{8,9},{9,8},{10,11... | collective-permute-start | bytes 786440 | tf_op jit(solution)/shard_map/ppermute | solution.py:109
  36.5 8.6 %collective-permute-start.2 = (bf16[2,8,64,256]{3,2,1,0:T(8,128)(2,1)}, bf16[2,8,64,256]{3,2,1,0:T(8,128)(2,1)}, u32[]{:S(2)}, u32[]{:S(2)}) collective-permute-start(bf16[2,8,64,256]{3,2,1,0:T(8,128)(2,1)} %pad_maximum_fusion.6), channel_id=1, source_target_pairs={{0,1},{1,0},{2,3},{3,2},{4,5},{5,4},{6,7},{7,6},{8,9},{9,8},{10,11... | collective-permute-start | bytes 1572872 | tf_op jit(solution)/shard_map/ppermute | solution.py:110
  57.2 2.3 %copy-start.6 = (bf16[128,2,256]{2,0,1:T(8,128)(2,1)}, bf16[128,2,256]{2,0,1:T(8,128)(2,1)S(1)}, u32[]{:S(2)}) copy-start(bf16[128,2,256]{2,0,1:T(8,128)(2,1)S(1)} %convolution_convert_fusion.1) | copy-start | bytes 393220
  71.5 4.9 %copy-start.1 = (f32[1,512,256]{2,1,0:T(8,128)}, f32[1,512,256]{2,1,0:T(8,128)S(1)}, u32[]{:S(2)}) copy-start(f32[1,512,256]{2,1,0:T(8,128)S(1)} %get-tuple-element.121) | copy-start | bytes 1572868
  71.5 4.9 %copy-start.3 = (f32[1,512,256]{2,1,0:T(8,128)}, f32[1,512,256]{2,1,0:T(8,128)S(1)}, u32[]{:S(2)}) copy-start(f32[1,512,256]{2,1,0:T(8,128)S(1)} %get-tuple-element.122) | copy-start | bytes 1572868
  71.5 4.9 %copy-start.5 = (f32[1,512,256]{2,1,0:T(8,128)}, f32[1,512,256]{2,1,0:T(8,128)S(1)}, u32[]{:S(2)}) copy-start(f32[1,512,256]{2,1,0:T(8,128)S(1)} %get-tuple-element.123) | copy-start | bytes 1572868
  72.8 26.3 %collective-permute-start.4 = (f32[2,512,256]{2,1,0:T(8,128)}, f32[2,512,256]{2,1,0:T(8,128)}, u32[]{:S(2)}, u32[]{:S(2)}) collective-permute-start(f32[2,512,256]{2,1,0:T(8,128)} %fusion.38), channel_id=1, source_target_pairs={{0,1},{1,0},{2,3},{3,2},{4,5},{5,4},{6,7},{7,6},{8,9},{9,8},{10,11... | collective-permute-start | bytes 3145736 | tf_op jit(solution)/shard_map/ppermute | solution.py:156
  87.0 6.1 %copy-start.8 = (bf16[1024,128]{1,0:T(8,128)(2,1)S(1)}, bf16[1024,128]{1,0:T(8,128)(2,1)}, u32[]{:S(2)}) copy-start(bf16[1024,128]{1,0:T(8,128)(2,1)} %slice.473) | copy-start | bytes 786436
  94.5 4.6 %copy-start.2 = (f32[1,512,256]{2,1,0:T(8,128)S(1)}, f32[1,512,256]{2,1,0:T(8,128)}, u32[]{:S(2)}) copy-start(f32[1,512,256]{2,1,0:T(8,128)} %copy-done.1) | copy-start | bytes 1572868
  94.5 4.6 %copy-start.4 = (f32[1,512,256]{2,1,0:T(8,128)S(1)}, f32[1,512,256]{2,1,0:T(8,128)}, u32[]{:S(2)}) copy-start(f32[1,512,256]{2,1,0:T(8,128)} %copy-done.3) | copy-start | bytes 1572868
  94.5 28.7 %all-to-all-start.2 = ((bf16[8,128,768]{2,1,0:T(8,128)(2,1)}), bf16[8,128,768]{2,1,0:T(8,128)(2,1)S(1)}, u32[]{:S(2)}, u32[]{:S(2)}) async-start(bf16[8,128,768]{2,1,0:T(8,128)(2,1)} %pad_maximum_fusion.1), calls=%async_computation.2 | async-start | bytes 3145728 | tf_op jit(solution)/shard_map/all_to_all | solution.py:166
  100.7 16.0 %collective-permute-start.5 = (bf16[512,256]{1,0:T(8,128)(2,1)S(1)}, bf16[512,256]{1,0:T(8,128)(2,1)S(1)}, u32[]{:S(2)}, u32[]{:S(2)}) collective-permute-start(bf16[512,256]{1,0:T(8,128)(2,1)S(1)} %get-tuple-element.134), channel_id=1, source_target_pairs={{8,0},{16,8},{24,16},{32,24},{40,32},{48,40},{56,48},{64,56},{72,6... | collective-permute-start | bytes 786440 | tf_op jit(solution)/shard_map/ppermute | solution.py:20
  104.8 16.7 %collective-permute-start.6 = (bf16[512,256]{1,0:T(8,128)(2,1)S(1)}, bf16[512,256]{1,0:T(8,128)(2,1)S(1)}, u32[]{:S(2)}, u32[]{:S(2)}) collective-permute-start(bf16[512,256]{1,0:T(8,128)(2,1)S(1)} %get-tuple-element.135), channel_id=1, source_target_pairs={{16,0},{24,8},{32,16},{40,24},{48,32},{56,40},{64,48},{72,56},{80,... | collective-permute-start | bytes 786440 | tf_op jit(solution)/shard_map/ppermute | solution.py:20
  123.2 14.7 %all-to-all-start.3 = ((bf16[8,128,256]{2,1,0:T(8,128)(2,1)}), bf16[8,128,256]{2,1,0:T(8,128)(2,1)S(1)}, u32[]{:S(2)}, u32[]{:S(2)}) async-start(bf16[8,128,256]{2,1,0:T(8,128)(2,1)} %bitcast.91), calls=%async_computation.3 | async-start | bytes 1048576 | tf_op jit(solution)/shard_map/all_to_all | solution.py:177
  (5 other events, 5.2 us)

commit v11 on v9

--- a/solution.py
+++ b/solution.py
@@ -8,7 +8,7 @@
 HD = 128
 BLK = 128
 MOST_BLK = 16
-Q_ROWS = 256
+Q_ROWS = 128
 
 
 MASK_FILL = -1e30

time: 125 us -> 137 us (1.096)
  other arithmetic: 18.7 us -> 26.5 us
  matrix products: 21.2 us -> 25.1 us
  waiting for transfers between devices: 30.6 us -> 29 us
    and x2 -> x4, other arithmetic: 6.27 us -> 14.6 us  [local(): (q_label[:, None] == k_label[None, :]) & (k_place[None, :] <= q_place[:,...]
    unnamed x35 -> x43, local copies, waits for them, and re-layouts: 4.42 us -> 7.22 us
    dot_general x4 -> x8, matrix products: 3.19 us -> 4.24 us  [block_pass(): jnp.einsum('qhd,kd->hqk', q_block, k_win, preferred_element_type=jnp.floa...]
    dot_general x4 -> x8, matrix products: 2.02 us -> 2.96 us  [block_pass(): jnp.einsum('hqk,kd->qhd', dscores, k_win, preferred_element_type=jnp.floa...]
    dot_general x4 -> x8, matrix products: 4.3 us -> 5.15 us  [block_pass(): jnp.einsum('hqk,qhd->kd', probs_bf, g_block, preferred_element_type=jnp.f...]
    dot_general x4 -> x8, matrix products: 3.68 us -> 4.45 us  [block_pass(): jnp.einsum('hqk,qhd->kd', dscores, q_block, preferred_element_type=jnp.fl...]
    dot_general x4 -> x8, matrix products: 4.02 us -> 4.61 us  [block_pass(): jnp.einsum('qhd,kd->hqk', g_block, v_win, preferred_element_type=jnp.floa...]
    dot_general x4 -> x8, matrix products: 3.97 us -> 3.74 us  [block_pass(): jnp.einsum('hqk,kd->qhd', probs_bf, v_win, preferred_element_type=jnp.flo...]
  transfers between devices with their start and end apart: 11 -> 11, of which waited for: 7 -> 6; matrix products, arithmetic and copies ran while one was open for 22% -> 23% of each run, Pallas kernels for 0% -> 0%
where the time goes in v11:
time: 137 us; the launch traced here: 136 us
  starting transfers between devices  37.2 us (27%)
  waiting for transfers between devices  29 us (21%)
  other arithmetic  26.5 us (19%)
  matrix products  25.1 us (18%)
  local copies, waits for them, and re-layouts  16.2 us (12%)
  between operations  1.59 us (1%)
    and x4, other arithmetic, local(): (q_label[:, None] == k_label[None, :]) & (k_place[None, :] <= q_place[:,...  14.6 us
    ppermute x4, starting transfers between devices, passed_along(): lax.ppermute(value, axis, [(source, source + steps) for source in range(f...  13.8 us
    all_to_all x1, waiting for transfers between devices, local(): lax.all_to_all(outgoing, 'sp', split_axis=0, concat_axis=1, tiled=True)  12 us
    ppermute x4, waiting for transfers between devices, passed_along(): lax.ppermute(value, axis, [(source, source + steps) for source in range(f...  9.43 us
    unnamed x43, local copies, waits for them, and re-layouts  7.22 us
    all_to_all x1, waiting for transfers between devices, local(): lax.all_to_all(kv_sum.astype(jnp.bfloat16), 'sp', split_axis=0, concat_ax...  6.53 us
    dot_general x8, matrix products, block_pass(): jnp.einsum('hqk,qhd->kd', probs_bf, g_block, preferred_element_type=jnp.f...  5.15 us
    all_to_all x1, starting transfers between devices, local(): lax.all_to_all(qg_pack, 'sp', split_axis=1, concat_axis=0, tiled=True)  4.79 us
  transfers between devices with their start and end apart: 11, of which 6 were waited for; matrix products, arithmetic and copies ran while one was open for 23% of the time, Pallas kernels for 0%

profile of v11, /device:TPU:384, one launch (start us, length us, event | category | flops | bytes accessed | tf_op | source)
XLA Modules:
  0.0 135.7 jit_solution(5773288686720738876)
XLA Ops:
  3.4 4.5 %all-to-all-start = ((bf16[8,64,256]{2,1,0:T(8,128)(2,1)}), bf16[8,64,256]{2,1,0:T(8,128)(2,1)S(1)}, u32[]{:S(2)}, u32[]{:S(2)}) async-start(bf16[8,64,256]{2,1,0:T(8,128)(2,1)} %bitcast.1), calls=%async_computation | async-start | bytes 524288 | tf_op jit(solution)/shard_map/all_to_all | solution.py:86
  8.3 1.9 %convert_reduce_fusion = s32[3072]{0:T(1024)S(1)} fusion(s32[128]{0:T(128)S(1)} %multiply_reduce_fusion.8, s32[3072]{0:T(1024)S(1)} %iota_add_fusion), kind=kLoop, calls=%fused_computation.133 | loop fusion | flops 1176576 | bytes 25088 | tf_op jit(solution)/shard_map/reduce_sum | solution.py:30
  10.3 3.6 %compare_and_fusion.6 = (pred[128,2176]{0,1:T(8,128)(4,1)}, pred[128,2176]{0,1:T(8,128)(4,1)}) fusion(s32[128]{0:T(128)S(1)} %get-tuple-element.262, s32[128]{0:T(128)S(1)} %get-tuple-element.254, s32[2176]{0:T(1024)S(1)} %get-tuple-element.246, s32[2176]{0:T(1024)S(1)} %get-tuple-element.238, s32[128]{0:T(128)S(1)} %get-tuple-element.263, ...), kind=kLoop, calls=%fused_computation.164 | loop fusion | flops 1671168 | bytes 593920 | tf_op jit(solution)/shard_map/and | solution.py:131
  13.9 3.6 %compare_and_fusion.4 = (pred[128,2176]{0,1:T(8,128)(4,1)}, pred[128,2176]{0,1:T(8,128)(4,1)}) fusion(s32[128]{0:T(128)S(1)} %get-tuple-element.260, s32[128]{0:T(128)S(1)} %get-tuple-element.252, s32[2176]{0:T(1024)S(1)} %get-tuple-element.244, s32[2176]{0:T(1024)S(1)} %get-tuple-element.236, s32[128]{0:T(128)S(1)} %get-tuple-element.261, ...), kind=kLoop, calls=%fused_computation.162 | loop fusion | flops 1671168 | bytes 593920 | tf_op jit(solution)/shard_map/and | solution.py:131
  19.1 4.8 %all-to-all-start.1 = ((bf16[128,8,512]{0,2,1:T(8,128)(2,1)}), bf16[128,8,512]{0,2,1:T(8,128)(2,1)S(1)}, u32[]{:S(2)}, u32[]{:S(2)}) async-start(bf16[128,8,512]{0,2,1:T(8,128)(2,1)} %pad_maximum_fusion.1), calls=%async_computation.1 | async-start | bytes 2097152 | tf_op jit(solution)/shard_map/all_to_all | solution.py:101
  23.9 4.9 %collective-permute-start = (bf16[8,64,256]{2,1,0:T(8,128)(2,1)S(1)}, bf16[8,64,256]{2,1,0:T(8,128)(2,1)S(1)}, u32[]{:S(2)}, u32[]{:S(2)}) collective-permute-start(bf16[8,64,256]{2,1,0:T(8,128)(2,1)S(1)} %all-to-all-done), channel_id=1, source_target_pairs={{0,16},{8,24},{16,32},{24,40},{32,48},{40,56},{48,64},{56,72},{64,... | collective-permute-start | bytes 786440 | tf_op jit(solution)/shard_map/ppermute | solution.py:20
  28.9 2.5 %collective-permute-start.1 = (bf16[8,64,256]{2,1,0:T(8,128)(2,1)S(1)}, bf16[8,64,256]{2,1,0:T(8,128)(2,1)S(1)}, u32[]{:S(2)}, u32[]{:S(2)}) collective-permute-start(bf16[8,64,256]{2,1,0:T(8,128)(2,1)S(1)} %all-to-all-done), channel_id=1, source_target_pairs={{0,8},{8,16},{16,24},{24,32},{32,40},{40,48},{48,56},{56,64},{64,7... | collective-permute-start | bytes 786440 | tf_op jit(solution)/shard_map/ppermute | solution.py:20
  31.4 3.7 %compare_and_fusion.2 = (pred[128,2176]{0,1:T(8,128)(4,1)}, pred[128,2176]{0,1:T(8,128)(4,1)}) fusion(s32[128]{0:T(128)S(1)} %get-tuple-element.258, s32[128]{0:T(128)S(1)} %get-tuple-element.250, s32[2176]{0:T(1024)S(1)} %get-tuple-element.242, s32[2176]{0:T(1024)S(1)} %get-tuple-element.234, s32[128]{0:T(128)S(1)} %get-tuple-element.259, ...), kind=kLoop, calls=%fused_computation.160 | loop fusion | flops 1671168 | bytes 593920 | tf_op jit(solution)/shard_map/and | solution.py:131
  35.0 1.9 %collective-permute-start.3 = (bf16[8,64,256]{2,1,0:T(8,128)(2,1)S(1)}, bf16[8,64,256]{2,1,0:T(8,128)(2,1)}, u32[]{:S(2)}, u32[]{:S(2)}) collective-permute-start(bf16[8,64,256]{2,1,0:T(8,128)(2,1)S(1)} %all-to-all-done), channel_id=1, source_target_pairs={{0,1},{1,0},{2,3},{3,2},{4,5},{5,4},{6,7},{7,6},{8,9},{9,8},{10,11... | collective-permute-start | bytes 786440 | tf_op jit(solution)/shard_map/ppermute | solution.py:109
  36.9 1.3 collective-permute-done
  38.2 6.1 %collective-permute-done.1 = bf16[8,64,256]{2,1,0:T(8,128)(2,1)S(1)} collective-permute-done((bf16[8,64,256]{2,1,0:T(8,128)(2,1)S(1)}, bf16[8,64,256]{2,1,0:T(8,128)(2,1)S(1)}, u32[]{:S(2)}, u32[]{:S(2)}) %collective-permute-start.1) | collective-permute-done | bytes 262176 | tf_op jit(solution)/shard_map/ppermute | solution.py:20
  44.4 1.9 %collective-permute-start.2 = (bf16[2,8,64,256]{3,2,1,0:T(8,128)(2,1)S(1)}, bf16[2,8,64,256]{3,2,1,0:T(8,128)(2,1)S(1)}, u32[]{:S(2)}, u32[]{:S(2)}) collective-permute-start(bf16[2,8,64,256]{3,2,1,0:T(8,128)(2,1)S(1)} %pad_maximum_fusion.6), channel_id=1, source_target_pairs={{0,1},{1,0},{2,3},{3,2},{4,5},{5,4},{6,7},{7,6},{8,9},{9,8},{10,11... | collective-permute-start | bytes 1572872 | tf_op jit(solution)/shard_map/ppermute | solution.py:110
  46.4 3.7 %compare_and_fusion = (pred[128,2176]{0,1:T(8,128)(4,1)}, pred[128,2176]{0,1:T(8,128)(4,1)}) fusion(s32[128]{0:T(128)S(1)} %get-tuple-element.256, s32[128]{0:T(128)S(1)} %get-tuple-element.248, s32[2176]{0:T(1024)S(1)} %get-tuple-element.240, s32[2176]{0:T(1024)S(1)} %get-tuple-element.232, s32[128]{0:T(128)S(1)} %get-tuple-element.257, ...), kind=kLoop, calls=%fused_computation.158 | loop fusion | flops 1671168 | bytes 593920 | tf_op jit(solution)/shard_map/and | solution.py:131
  84.1 2.4 %collective-permute-start.4 = (f32[2,512,256]{1,2,0:T(8,128)S(1)}, f32[2,512,256]{1,2,0:T(8,128)S(1)}, u32[]{:S(2)}, u32[]{:S(2)}) collective-permute-start(f32[2,512,256]{1,2,0:T(8,128)S(1)} %fusion.85), channel_id=1, source_target_pairs={{0,1},{1,0},{2,3},{3,2},{4,5},{5,4},{6,7},{7,6},{8,9},{9,8},{10,11... | collective-permute-start | bytes 3145736 | tf_op jit(solution)/shard_map/ppermute | solution.py:156
  87.7 1.1 collective-permute-done.4
  90.0 2.3 %collective-permute-start.5 = (bf16[512,256]{0,1:T(8,128)(2,1)}, bf16[512,256]{0,1:T(8,128)(2,1)S(1)}, u32[]{:S(2)}, u32[]{:S(2)}) collective-permute-start(bf16[512,256]{0,1:T(8,128)(2,1)} %get-tuple-element.226), channel_id=1, source_target_pairs={{8,0},{16,8},{24,16},{32,24},{40,32},{48,40},{56,48},{64,56},{72,6... | collective-permute-start | bytes 786440 | tf_op jit(solution)/shard_map/ppermute | solution.py:20
  92.3 4.1 %collective-permute-start.6 = (bf16[512,256]{0,1:T(8,128)(2,1)}, bf16[512,256]{0,1:T(8,128)(2,1)}, u32[]{:S(2)}, u32[]{:S(2)}) collective-permute-start(bf16[512,256]{0,1:T(8,128)(2,1)} %get-tuple-element.227), channel_id=1, source_target_pairs={{16,0},{24,8},{32,16},{40,24},{48,32},{56,40},{64,48},{72,56},{80,... | collective-permute-start | bytes 786440 | tf_op jit(solution)/shard_map/ppermute | solution.py:20
  97.5 2.3 %copy.367 = bf16[1024,512]{1,0:T(8,128)(2,1)} copy(bf16[1024,512]{0,1:T(8,128)(2,1)} %pad_maximum_fusion.2) | data formatting | bytes 2097152 | tf_op jit(solution)/shard_map/concatenate | solution.py:163
  99.8 4.4 %all-to-all-start.2 = ((bf16[8,128,512]{2,1,0:T(8,128)(2,1)}), bf16[8,128,512]{2,1,0:T(8,128)(2,1)}, u32[]{:S(2)}, u32[]{:S(2)}) async-start(bf16[8,128,512]{2,1,0:T(8,128)(2,1)} %bitcast.462), calls=%async_computation.2 | async-start | bytes 2097152 | tf_op jit(solution)/shard_map/all_to_all | solution.py:164
  104.3 2.0 %collective-permute-done.5 = bf16[512,256]{0,1:T(8,128)(2,1)S(1)} collective-permute-done((bf16[512,256]{0,1:T(8,128)(2,1)}, bf16[512,256]{0,1:T(8,128)(2,1)S(1)}, u32[]{:S(2)}, u32[]{:S(2)}) %collective-permute-start.5) | collective-permute-done | bytes 262176 | tf_op jit(solution)/shard_map/ppermute | solution.py:20
  108.3 12.0 %all-to-all-done.2 = bf16[8,128,512]{2,1,0:T(8,128)(2,1)} async-done(((bf16[8,128,512]{2,1,0:T(8,128)(2,1)}), bf16[8,128,512]{2,1,0:T(8,128)(2,1)}, u32[]{:S(2)}, u32[]{:S(2)}) %all-to-all-start.2) | async-done | bytes 1048608 | tf_op jit(solution)/shard_map/all_to_all | solution.py:164
  120.3 3.5 %all-to-all-start.3 = ((bf16[8,128,256]{1,2,0:T(8,128)(2,1)}), bf16[8,128,256]{1,2,0:T(8,128)(2,1)S(1)}, u32[]{:S(2)}, u32[]{:S(2)}) async-start(bf16[8,128,256]{1,2,0:T(8,128)(2,1)} %pad_maximum_fusion.7), calls=%async_computation.3 | async-start | bytes 1048576 | tf_op jit(solution)/shard_map/all_to_all | solution.py:176
  123.8 1.6 %copy.368 = bf16[8,128,512]{1,2,0:T(8,128)(2,1)S(1)} copy(bf16[8,128,512]{2,1,0:T(8,128)(2,1)} %all-to-all-done.2) | data formatting | bytes 2097152 | tf_op jit(solution)/shard_map/all_to_all | solution.py:164
  127.5 6.5 %all-to-all-done.3 = bf16[8,128,256]{1,2,0:T(8,128)(2,1)S(1)} async-done(((bf16[8,128,256]{1,2,0:T(8,128)(2,1)}), bf16[8,128,256]{1,2,0:T(8,128)(2,1)S(1)}, u32[]{:S(2)}, u32[]{:S(2)}) %all-to-all-start.3) | async-done | bytes 524320 | tf_op jit(solution)/shard_map/all_to_all | solution.py:176
  (160 shorter events, 47.5 us)
Async XLA Ops:
  0.6 7.3 %copy-start.10 = (s32[128]{0:T(128)S(1)}, s32[128]{0:T(128)}, u32[]{:S(2)}) copy-start(s32[128]{0:T(128)} %param.41) | copy-start | bytes 1540
  2.7 14.8 %copy-start = (bf16[128,2048]{1,0:T(8,128)(2,1)S(1)}, bf16[128,2048]{1,0:T(8,128)(2,1)}, u32[]{:S(2)}) copy-start(bf16[128,2048]{1,0:T(8,128)(2,1)} %param.37) | copy-start | bytes 1572868
  3.4 15.7 %all-to-all-start = ((bf16[8,64,256]{2,1,0:T(8,128)(2,1)}), bf16[8,64,256]{2,1,0:T(8,128)(2,1)S(1)}, u32[]{:S(2)}, u32[]{:S(2)}) async-start(bf16[8,64,256]{2,1,0:T(8,128)(2,1)} %bitcast.1), calls=%async_computation | async-start | bytes 524288 | tf_op jit(solution)/shard_map/all_to_all | solution.py:86
  7.9 9.9 %copy-start.1 = (bf16[128,2048]{1,0:T(8,128)(2,1)S(1)}, bf16[128,2048]{1,0:T(8,128)(2,1)}, u32[]{:S(2)}) copy-start(bf16[128,2048]{1,0:T(8,128)(2,1)} %param.40) | copy-start | bytes 1572868
  19.1 32.0 %all-to-all-start.1 = ((bf16[128,8,512]{0,2,1:T(8,128)(2,1)}), bf16[128,8,512]{0,2,1:T(8,128)(2,1)S(1)}, u32[]{:S(2)}, u32[]{:S(2)}) async-start(bf16[128,8,512]{0,2,1:T(8,128)(2,1)} %pad_maximum_fusion.1), calls=%async_computation.1 | async-start | bytes 2097152 | tf_op jit(solution)/shard_map/all_to_all | solution.py:101
  23.9 14.3 %collective-permute-start = (bf16[8,64,256]{2,1,0:T(8,128)(2,1)S(1)}, bf16[8,64,256]{2,1,0:T(8,128)(2,1)S(1)}, u32[]{:S(2)}, u32[]{:S(2)}) collective-permute-start(bf16[8,64,256]{2,1,0:T(8,128)(2,1)S(1)} %all-to-all-done), channel_id=1, source_target_pairs={{0,16},{8,24},{16,32},{24,40},{32,48},{40,56},{48,64},{56,72},{64,... | collective-permute-start | bytes 786440 | tf_op jit(solution)/shard_map/ppermute | solution.py:20
  28.9 15.5 %collective-permute-start.1 = (bf16[8,64,256]{2,1,0:T(8,128)(2,1)S(1)}, bf16[8,64,256]{2,1,0:T(8,128)(2,1)S(1)}, u32[]{:S(2)}, u32[]{:S(2)}) collective-permute-start(bf16[8,64,256]{2,1,0:T(8,128)(2,1)S(1)} %all-to-all-done), channel_id=1, source_target_pairs={{0,8},{8,16},{16,24},{24,32},{32,40},{40,48},{48,56},{56,64},{64,7... | collective-permute-start | bytes 786440 | tf_op jit(solution)/shard_map/ppermute | solution.py:20
  35.0 15.0 %collective-permute-start.3 = (bf16[8,64,256]{2,1,0:T(8,128)(2,1)S(1)}, bf16[8,64,256]{2,1,0:T(8,128)(2,1)}, u32[]{:S(2)}, u32[]{:S(2)}) collective-permute-start(bf16[8,64,256]{2,1,0:T(8,128)(2,1)S(1)} %all-to-all-done), channel_id=1, source_target_pairs={{0,1},{1,0},{2,3},{3,2},{4,5},{5,4},{6,7},{7,6},{8,9},{9,8},{10,11... | collective-permute-start | bytes 786440 | tf_op jit(solution)/shard_map/ppermute | solution.py:109
  44.4 7.9 %collective-permute-start.2 = (bf16[2,8,64,256]{3,2,1,0:T(8,128)(2,1)S(1)}, bf16[2,8,64,256]{3,2,1,0:T(8,128)(2,1)S(1)}, u32[]{:S(2)}, u32[]{:S(2)}) collective-permute-start(bf16[2,8,64,256]{3,2,1,0:T(8,128)(2,1)S(1)} %pad_maximum_fusion.6), channel_id=1, source_target_pairs={{0,1},{1,0},{2,3},{3,2},{4,5},{5,4},{6,7},{7,6},{8,9},{9,8},{10,11... | collective-permute-start | bytes 1572872 | tf_op jit(solution)/shard_map/ppermute | solution.py:110
  52.7 1.0 copy-start.9
  56.2 1.0 copy-start.6
  58.7 1.0 copy-start.4
  61.0 1.0 copy-start.2
  63.2 1.0 copy-start.7
  65.5 1.0 copy-start.3
  68.0 1.0 copy-start.8
  70.3 1.0 copy-start.5
  84.1 4.7 %collective-permute-start.4 = (f32[2,512,256]{1,2,0:T(8,128)S(1)}, f32[2,512,256]{1,2,0:T(8,128)S(1)}, u32[]{:S(2)}, u32[]{:S(2)}) collective-permute-start(f32[2,512,256]{1,2,0:T(8,128)S(1)} %fusion.85), channel_id=1, source_target_pairs={{0,1},{1,0},{2,3},{3,2},{4,5},{5,4},{6,7},{7,6},{8,9},{9,8},{10,11... | collective-permute-start | bytes 3145736 | tf_op jit(solution)/shard_map/ppermute | solution.py:156
  90.0 16.3 %collective-permute-start.5 = (bf16[512,256]{0,1:T(8,128)(2,1)}, bf16[512,256]{0,1:T(8,128)(2,1)S(1)}, u32[]{:S(2)}, u32[]{:S(2)}) collective-permute-start(bf16[512,256]{0,1:T(8,128)(2,1)} %get-tuple-element.226), channel_id=1, source_target_pairs={{8,0},{16,8},{24,16},{32,24},{40,32},{48,40},{56,48},{64,56},{72,6... | collective-permute-start | bytes 786440 | tf_op jit(solution)/shard_map/ppermute | solution.py:20
  92.3 14.0 %collective-permute-start.6 = (bf16[512,256]{0,1:T(8,128)(2,1)}, bf16[512,256]{0,1:T(8,128)(2,1)}, u32[]{:S(2)}, u32[]{:S(2)}) collective-permute-start(bf16[512,256]{0,1:T(8,128)(2,1)} %get-tuple-element.227), channel_id=1, source_target_pairs={{16,0},{24,8},{32,16},{40,24},{48,32},{56,40},{64,48},{72,56},{80,... | collective-permute-start | bytes 786440 | tf_op jit(solution)/shard_map/ppermute | solution.py:20
  99.8 20.5 %all-to-all-start.2 = ((bf16[8,128,512]{2,1,0:T(8,128)(2,1)}), bf16[8,128,512]{2,1,0:T(8,128)(2,1)}, u32[]{:S(2)}, u32[]{:S(2)}) async-start(bf16[8,128,512]{2,1,0:T(8,128)(2,1)} %bitcast.462), calls=%async_computation.2 | async-start | bytes 2097152 | tf_op jit(solution)/shard_map/all_to_all | solution.py:164
  120.3 13.8 %all-to-all-start.3 = ((bf16[8,128,256]{1,2,0:T(8,128)(2,1)}), bf16[8,128,256]{1,2,0:T(8,128)(2,1)S(1)}, u32[]{:S(2)}, u32[]{:S(2)}) async-start(bf16[8,128,256]{1,2,0:T(8,128)(2,1)} %pad_maximum_fusion.7), calls=%async_computation.3 | async-start | bytes 1048576 | tf_op jit(solution)/shard_map/all_to_all | solution.py:176

commit v12 on v9

--- a/solution.py
+++ b/solution.py
@@ -153,7 +153,7 @@
     )
     mine_part = jnp.where(core == 0, low_rows, high_rows)
     their_part = jnp.where(core == 0, high_rows, low_rows)
-    pair_sum = mine_part + lax.ppermute(their_part, "sp", sibling)
+    pair_sum = mine_part + lax.ppermute(their_part.astype(jnp.bfloat16), "sp", sibling)
     backs = [
         passed_along(pair_sum[reach_groups - d].astype(jnp.bfloat16), "fsdp", -d)
         for d in range(1, reach_groups + 1)

time: 125 us -> 126 us (level)
  transfers between devices with their start and end apart: 11 -> 11, of which waited for: 7 -> 7; matrix products, arithmetic and copies ran while one was open for 22% -> 21% of each run, Pallas kernels for 0% -> 0%
where the time goes in v12:
time: 126 us; the launch traced here: 125 us
  starting transfers between devices  36.2 us (29%)
  waiting for transfers between devices  30.8 us (24%)
  matrix products  21.2 us (17%)
  other arithmetic  18.6 us (15%)
  local copies, waits for them, and re-layouts  16.8 us (13%)
  between operations  1.34 us (1%)
    ppermute x4, starting transfers between devices, passed_along(): lax.ppermute(value, axis, [(source, source + steps) for source in range(f...  13.8 us
    all_to_all x1, waiting for transfers between devices, local(): lax.all_to_all(outgoing, 'sp', split_axis=0, concat_axis=1, tiled=True)  12 us
    ppermute x4, waiting for transfers between devices, passed_along(): lax.ppermute(value, axis, [(source, source + steps) for source in range(f...  10.7 us
    all_to_all x1, waiting for transfers between devices, local(): lax.all_to_all(kv_sum.astype(jnp.bfloat16), 'sp', split_axis=0, concat_ax...  6.53 us
    and x2, other arithmetic, local(): (q_label[:, None] == k_label[None, :]) & (k_place[None, :] <= q_place[:,...  6.27 us
    dot_general x4, matrix products, block_pass(): jnp.einsum('hqk,qhd->kd', probs_bf, g_block, preferred_element_type=jnp.f...  4.51 us
    all_to_all x1, starting transfers between devices, local(): lax.all_to_all(kv_send, 'sp', split_axis=0, concat_axis=0, tiled=True)  4.47 us
    all_to_all x1, starting transfers between devices, local(): lax.all_to_all(outgoing, 'sp', split_axis=0, concat_axis=1, tiled=True)  4.45 us
  transfers between devices with their start and end apart: 11, of which 7 were waited for; matrix products, arithmetic and copies ran while one was open for 21% of the time, Pallas kernels for 0%

profile of v12, /device:TPU:384, one launch (start us, length us, event | category | flops | bytes accessed | tf_op | source)
XLA Modules:
  0.0 124.8 jit_solution(5608771237135902209)
XLA Ops:
  3.5 4.5 %all-to-all-start = ((bf16[8,64,256]{2,1,0:T(8,128)(2,1)}), bf16[8,64,256]{2,1,0:T(8,128)(2,1)S(1)}, u32[]{:S(2)}, u32[]{:S(2)}) async-start(bf16[8,64,256]{2,1,0:T(8,128)(2,1)} %bitcast.1), calls=%async_computation | async-start | bytes 524288 | tf_op jit(solution)/shard_map/all_to_all | solution.py:86
  9.0 1.9 %convert_reduce_fusion = s32[3072]{0:T(1024)S(1)} fusion(s32[128]{0:T(128)S(1)} %multiply_reduce_fusion.4, s32[3072]{0:T(1024)S(1)} %iota_add_fusion), kind=kLoop, calls=%fused_computation.73 | loop fusion | flops 1176576 | bytes 25088 | tf_op jit(solution)/shard_map/reduce_sum | solution.py:30
  15.5 3.7 %all-to-all-start.1 = ((bf16[128,8,512]{0,2,1:T(8,128)(2,1)}), bf16[128,8,512]{0,2,1:T(8,128)(2,1)S(1)}, u32[]{:S(2)}, u32[]{:S(2)}) async-start(bf16[128,8,512]{0,2,1:T(8,128)(2,1)} %pad_maximum_fusion.1), calls=%async_computation.1 | async-start | bytes 2097152 | tf_op jit(solution)/shard_map/all_to_all | solution.py:101
  19.3 4.9 %collective-permute-start = (bf16[8,64,256]{2,1,0:T(8,128)(2,1)S(1)}, bf16[8,64,256]{2,1,0:T(8,128)(2,1)S(1)}, u32[]{:S(2)}, u32[]{:S(2)}) collective-permute-start(bf16[8,64,256]{2,1,0:T(8,128)(2,1)S(1)} %all-to-all-done), channel_id=1, source_target_pairs={{0,16},{8,24},{16,32},{24,40},{32,48},{40,56},{48,64},{56,72},{64,... | collective-permute-start | bytes 786440 | tf_op jit(solution)/shard_map/ppermute | solution.py:20
  24.2 2.5 %collective-permute-start.1 = (bf16[8,64,256]{2,1,0:T(8,128)(2,1)S(1)}, bf16[8,64,256]{2,1,0:T(8,128)(2,1)S(1)}, u32[]{:S(2)}, u32[]{:S(2)}) collective-permute-start(bf16[8,64,256]{2,1,0:T(8,128)(2,1)S(1)} %all-to-all-done), channel_id=1, source_target_pairs={{0,8},{8,16},{16,24},{24,32},{32,40},{40,48},{48,56},{56,64},{64,7... | collective-permute-start | bytes 786440 | tf_op jit(solution)/shard_map/ppermute | solution.py:20
  26.7 2.2 %compare_and_fusion.2 = (pred[256,2304]{0,1:T(8,128)(4,1)S(1)}, pred[256,2304]{0,1:T(8,128)(4,1)S(1)}) fusion(s32[256]{0:T(256)S(1)} %copy-done.13, s32[256]{0:T(256)S(1)} %copy-done.11, s32[2304]{0:T(1024)S(1)} %get-tuple-element.135, s32[2304]{0:T(1024)S(1)} %copy-done.6, s32[256]{0:T(256)S(1)} %copy-done.12, s32[2304]{0:T(1024)S(1)} %get-tuple-element.132, ...), kind=kLoop, calls=%fused_computation.70 | loop fusion | flops 3538944 | bytes 1220608 | tf_op jit(solution)/shard_map/and | solution.py:131
  29.0 1.9 %collective-permute-start.3 = (bf16[8,64,256]{2,1,0:T(8,128)(2,1)S(1)}, bf16[8,64,256]{2,1,0:T(8,128)(2,1)}, u32[]{:S(2)}, u32[]{:S(2)}) collective-permute-start(bf16[8,64,256]{2,1,0:T(8,128)(2,1)S(1)} %all-to-all-done), channel_id=1, source_target_pairs={{0,1},{1,0},{2,3},{3,2},{4,5},{5,4},{6,7},{7,6},{8,9},{9,8},{10,11... | collective-permute-start | bytes 786440 | tf_op jit(solution)/shard_map/ppermute | solution.py:109
  30.9 2.6 %collective-permute-done = bf16[8,64,256]{2,1,0:T(8,128)(2,1)S(1)} collective-permute-done((bf16[8,64,256]{2,1,0:T(8,128)(2,1)S(1)}, bf16[8,64,256]{2,1,0:T(8,128)(2,1)S(1)}, u32[]{:S(2)}, u32[]{:S(2)}) %collective-permute-start) | collective-permute-done | bytes 262176 | tf_op jit(solution)/shard_map/ppermute | solution.py:20
  33.6 6.1 %collective-permute-done.1 = bf16[8,64,256]{2,1,0:T(8,128)(2,1)S(1)} collective-permute-done((bf16[8,64,256]{2,1,0:T(8,128)(2,1)S(1)}, bf16[8,64,256]{2,1,0:T(8,128)(2,1)S(1)}, u32[]{:S(2)}, u32[]{:S(2)}) %collective-permute-start.1) | collective-permute-done | bytes 262176 | tf_op jit(solution)/shard_map/ppermute | solution.py:20
  40.6 1.9 %collective-permute-start.2 = (bf16[2,8,64,256]{3,2,1,0:T(8,128)(2,1)}, bf16[2,8,64,256]{3,2,1,0:T(8,128)(2,1)}, u32[]{:S(2)}, u32[]{:S(2)}) collective-permute-start(bf16[2,8,64,256]{3,2,1,0:T(8,128)(2,1)} %pad_maximum_fusion.5), channel_id=1, source_target_pairs={{0,1},{1,0},{2,3},{3,2},{4,5},{5,4},{6,7},{7,6},{8,9},{9,8},{10,11... | collective-permute-start | bytes 1572872 | tf_op jit(solution)/shard_map/ppermute | solution.py:110
  42.5 4.0 %compare_and_fusion = (pred[256,2304]{0,1:T(8,128)(4,1)}, pred[256,2304]{0,1:T(8,128)(4,1)}) fusion(s32[256]{0:T(256)S(1)} %copy-done.9, s32[256]{0:T(256)S(1)} %get-tuple-element.137, s32[2304]{0:T(1024)S(1)} %get-tuple-element.133, s32[2304]{0:T(1024)S(1)} %get-tuple-element.129, s32[256]{0:T(256)S(1)} %copy-done.8, s32[2304]{0:T(1024)S(1)} %get-tuple-element.134, ...), kind=kLoop, calls=%fused_computation.68 | loop fusion | flops 3538944 | bytes 1220608 | tf_op jit(solution)/shard_map/and | solution.py:131
  58.6 1.1 fusion.31
  62.1 1.3 %fusion.33 = f32[3072,128]{0,1:T(8,128)S(1)} fusion(f32[3072,128]{0,1:T(8,128)S(1)} %fusion.31, bf16[256,2,128]{0,2,1:T(8,128)(2,1)S(1)} %bitcast.265, f32[2,256,2304]{1,2,0:T(8,128)S(1)} %get-tuple-element.147, f32[2,256]{1,0:T(2,128)S(1)} %log_add_fusion.1), kind=kOutput, calls=%fused_computation.65 | convolution fusion | flops 304644096 | bytes 7211008 | tf_op jit(solution)/shard_map/hqk,qhd->kd/dot_general | solution.py:64
  74.0 2.4 %collective-permute-start.4 = (bf16[2,512,256]{1,2,0:T(8,128)(2,1)S(1)}, bf16[2,512,256]{1,2,0:T(8,128)(2,1)S(1)}, u32[]{:S(2)}, u32[]{:S(2)}) collective-permute-start(bf16[2,512,256]{1,2,0:T(8,128)(2,1)S(1)} %select_convert_fusion), channel_id=1, source_target_pairs={{0,1},{1,0},{2,3},{3,2},{4,5},{5,4},{6,7},{7,6},{8,9},{9,8},{10,11... | collective-permute-start | bytes 1572872 | tf_op jit(solution)/shard_map/ppermute | solution.py:156
  79.1 2.3 %collective-permute-start.5 = (bf16[512,256]{0,1:T(8,128)(2,1)}, bf16[512,256]{0,1:T(8,128)(2,1)S(1)}, u32[]{:S(2)}, u32[]{:S(2)}) collective-permute-start(bf16[512,256]{0,1:T(8,128)(2,1)} %get-tuple-element.122), channel_id=1, source_target_pairs={{8,0},{16,8},{24,16},{32,24},{40,32},{48,40},{56,48},{64,56},{72,6... | collective-permute-start | bytes 786440 | tf_op jit(solution)/shard_map/ppermute | solution.py:20
  81.4 4.1 %collective-permute-start.6 = (bf16[512,256]{0,1:T(8,128)(2,1)}, bf16[512,256]{0,1:T(8,128)(2,1)}, u32[]{:S(2)}, u32[]{:S(2)}) collective-permute-start(bf16[512,256]{0,1:T(8,128)(2,1)} %get-tuple-element.123), channel_id=1, source_target_pairs={{16,0},{24,8},{32,16},{40,24},{48,32},{56,40},{64,48},{72,56},{80,... | collective-permute-start | bytes 786440 | tf_op jit(solution)/shard_map/ppermute | solution.py:20
  85.4 1.2 maximum_maximum_fusion
  86.6 2.3 %copy.215 = bf16[1024,512]{1,0:T(8,128)(2,1)} copy(bf16[1024,512]{0,1:T(8,128)(2,1)} %maximum_maximum_fusion) | data formatting | bytes 2097152 | tf_op jit(solution)/shard_map/concatenate | solution.py:163
  88.9 4.4 %all-to-all-start.2 = ((bf16[8,128,512]{2,1,0:T(8,128)(2,1)}), bf16[8,128,512]{2,1,0:T(8,128)(2,1)}, u32[]{:S(2)}, u32[]{:S(2)}) async-start(bf16[8,128,512]{2,1,0:T(8,128)(2,1)} %bitcast.258), calls=%async_computation.2 | async-start | bytes 2097152 | tf_op jit(solution)/shard_map/all_to_all | solution.py:164
  93.5 1.9 %collective-permute-done.5 = bf16[512,256]{0,1:T(8,128)(2,1)S(1)} collective-permute-done((bf16[512,256]{0,1:T(8,128)(2,1)}, bf16[512,256]{0,1:T(8,128)(2,1)S(1)}, u32[]{:S(2)}, u32[]{:S(2)}) %collective-permute-start.5) | collective-permute-done | bytes 262176 | tf_op jit(solution)/shard_map/ppermute | solution.py:20
  97.4 12.0 %all-to-all-done.2 = bf16[8,128,512]{2,1,0:T(8,128)(2,1)} async-done(((bf16[8,128,512]{2,1,0:T(8,128)(2,1)}), bf16[8,128,512]{2,1,0:T(8,128)(2,1)}, u32[]{:S(2)}, u32[]{:S(2)}) %all-to-all-start.2) | async-done | bytes 1048608 | tf_op jit(solution)/shard_map/all_to_all | solution.py:164
  109.4 3.5 %all-to-all-start.3 = ((bf16[8,128,256]{1,2,0:T(8,128)(2,1)}), bf16[8,128,256]{1,2,0:T(8,128)(2,1)S(1)}, u32[]{:S(2)}, u32[]{:S(2)}) async-start(bf16[8,128,256]{1,2,0:T(8,128)(2,1)} %pad_maximum_fusion.6), calls=%async_computation.3 | async-start | bytes 1048576 | tf_op jit(solution)/shard_map/all_to_all | solution.py:176
  112.9 1.6 %copy.216 = bf16[8,128,512]{1,2,0:T(8,128)(2,1)S(1)} copy(bf16[8,128,512]{2,1,0:T(8,128)(2,1)} %all-to-all-done.2) | data formatting | bytes 2097152 | tf_op jit(solution)/shard_map/all_to_all | solution.py:164
  116.7 6.5 %all-to-all-done.3 = bf16[8,128,256]{1,2,0:T(8,128)(2,1)S(1)} async-done(((bf16[8,128,256]{1,2,0:T(8,128)(2,1)}), bf16[8,128,256]{1,2,0:T(8,128)(2,1)S(1)}, u32[]{:S(2)}, u32[]{:S(2)}) %all-to-all-start.3) | async-done | bytes 524320 | tf_op jit(solution)/shard_map/all_to_all | solution.py:176
  (112 shorter events, 42.4 us)
Async XLA Ops:
  0.6 12.1 %copy-start.2 = (bf16[128,2048]{1,0:T(8,128)(2,1)S(1)}, bf16[128,2048]{1,0:T(8,128)(2,1)}, u32[]{:S(2)}) copy-start(bf16[128,2048]{1,0:T(8,128)(2,1)} %param.21) | copy-start | bytes 1572868
  0.6 12.4 %copy-start.3 = (bf16[128,2048]{1,0:T(8,128)(2,1)S(1)}, bf16[128,2048]{1,0:T(8,128)(2,1)}, u32[]{:S(2)}) copy-start(bf16[128,2048]{1,0:T(8,128)(2,1)} %param.24) | copy-start | bytes 1572868
  3.5 12.0 %all-to-all-start = ((bf16[8,64,256]{2,1,0:T(8,128)(2,1)}), bf16[8,64,256]{2,1,0:T(8,128)(2,1)S(1)}, u32[]{:S(2)}, u32[]{:S(2)}) async-start(bf16[8,64,256]{2,1,0:T(8,128)(2,1)} %bitcast.1), calls=%async_computation | async-start | bytes 524288 | tf_op jit(solution)/shard_map/all_to_all | solution.py:86
  13.3 13.4 %copy-start.5 = (s32[2304]{0:T(1024)S(1)}, s32[2304]{0:T(1024)}, u32[]{:S(2)}) copy-start(s32[2304]{0:T(1024)} %get-tuple-element.128) | copy-start | bytes 27652
  13.3 13.4 %copy-start.6 = (s32[2304]{0:T(1024)S(1)}, s32[2304]{0:T(1024)}, u32[]{:S(2)}) copy-start(s32[2304]{0:T(1024)} %get-tuple-element.131) | copy-start | bytes 27652
  13.3 13.4 %copy-start.10 = (s32[256]{0:T(256)S(1)}, s32[256]{0:T(256)}, u32[]{:S(2)}) copy-start(s32[256]{0:T(256)} %get-tuple-element.136) | copy-start | bytes 3076
  13.3 13.4 %copy-start.11 = (s32[256]{0:T(256)S(1)}, s32[256]{0:T(256)}, u32[]{:S(2)}) copy-start(s32[256]{0:T(256)} %get-tuple-element.139) | copy-start | bytes 3076
  13.3 13.4 %copy-start.12 = (s32[256]{0:T(256)S(1)}, s32[256]{0:T(256)}, u32[]{:S(2)}) copy-start(s32[256]{0:T(256)} %get-tuple-element.140) | copy-start | bytes 3076
  13.3 13.4 %copy-start.13 = (s32[256]{0:T(256)S(1)}, s32[256]{0:T(256)}, u32[]{:S(2)}) copy-start(s32[256]{0:T(256)} %get-tuple-element.142) | copy-start | bytes 3076
  14.4 28.1 %copy-start.4 = (s32[2304]{0:T(1024)S(1)}, s32[2304]{0:T(1024)}, u32[]{:S(2)}) copy-start(s32[2304]{0:T(1024)} %get-tuple-element.130) | copy-start | bytes 27652
  14.4 28.1 %copy-start.7 = (s32[256]{0:T(256)S(1)}, s32[256]{0:T(256)}, u32[]{:S(2)}) copy-start(s32[256]{0:T(256)} %get-tuple-element.138) | copy-start | bytes 3076
  14.4 28.1 %copy-start.8 = (s32[256]{0:T(256)S(1)}, s32[256]{0:T(256)}, u32[]{:S(2)}) copy-start(s32[256]{0:T(256)} %get-tuple-element.141) | copy-start | bytes 3076
  14.4 28.1 %copy-start.9 = (s32[256]{0:T(256)S(1)}, s32[256]{0:T(256)}, u32[]{:S(2)}) copy-start(s32[256]{0:T(256)} %get-tuple-element.143) | copy-start | bytes 3076
  15.5 32.1 %all-to-all-start.1 = ((bf16[128,8,512]{0,2,1:T(8,128)(2,1)}), bf16[128,8,512]{0,2,1:T(8,128)(2,1)S(1)}, u32[]{:S(2)}, u32[]{:S(2)}) async-start(bf16[128,8,512]{0,2,1:T(8,128)(2,1)} %pad_maximum_fusion.1), calls=%async_computation.1 | async-start | bytes 2097152 | tf_op jit(solution)/shard_map/all_to_all | solution.py:101
  19.3 14.3 %collective-permute-start = (bf16[8,64,256]{2,1,0:T(8,128)(2,1)S(1)}, bf16[8,64,256]{2,1,0:T(8,128)(2,1)S(1)}, u32[]{:S(2)}, u32[]{:S(2)}) collective-permute-start(bf16[8,64,256]{2,1,0:T(8,128)(2,1)S(1)} %all-to-all-done), channel_id=1, source_target_pairs={{0,16},{8,24},{16,32},{24,40},{32,48},{40,56},{48,64},{56,72},{64,... | collective-permute-start | bytes 786440 | tf_op jit(solution)/shard_map/ppermute | solution.py:20
  24.2 15.5 %collective-permute-start.1 = (bf16[8,64,256]{2,1,0:T(8,128)(2,1)S(1)}, bf16[8,64,256]{2,1,0:T(8,128)(2,1)S(1)}, u32[]{:S(2)}, u32[]{:S(2)}) collective-permute-start(bf16[8,64,256]{2,1,0:T(8,128)(2,1)S(1)} %all-to-all-done), channel_id=1, source_target_pairs={{0,8},{8,16},{16,24},{24,32},{32,40},{40,48},{48,56},{56,64},{64,7... | collective-permute-start | bytes 786440 | tf_op jit(solution)/shard_map/ppermute | solution.py:20
  29.0 17.6 %collective-permute-start.3 = (bf16[8,64,256]{2,1,0:T(8,128)(2,1)S(1)}, bf16[8,64,256]{2,1,0:T(8,128)(2,1)}, u32[]{:S(2)}, u32[]{:S(2)}) collective-permute-start(bf16[8,64,256]{2,1,0:T(8,128)(2,1)S(1)} %all-to-all-done), channel_id=1, source_target_pairs={{0,1},{1,0},{2,3},{3,2},{4,5},{5,4},{6,7},{7,6},{8,9},{9,8},{10,11... | collective-permute-start | bytes 786440 | tf_op jit(solution)/shard_map/ppermute | solution.py:109
  40.6 8.2 %collective-permute-start.2 = (bf16[2,8,64,256]{3,2,1,0:T(8,128)(2,1)}, bf16[2,8,64,256]{3,2,1,0:T(8,128)(2,1)}, u32[]{:S(2)}, u32[]{:S(2)}) collective-permute-start(bf16[2,8,64,256]{3,2,1,0:T(8,128)(2,1)} %pad_maximum_fusion.5), channel_id=1, source_target_pairs={{0,1},{1,0},{2,3},{3,2},{4,5},{5,4},{6,7},{7,6},{8,9},{9,8},{10,11... | collective-permute-start | bytes 1572872 | tf_op jit(solution)/shard_map/ppermute | solution.py:110
  62.1 1.4 %copy-start = (pred[256,2304]{0,1:T(8,128)(4,1)S(1)}, pred[256,2304]{0,1:T(8,128)(4,1)}, u32[]{:S(2)}) copy-start(pred[256,2304]{0,1:T(8,128)(4,1)} %get-tuple-element.154) | copy-start | bytes 1769476
  74.0 3.9 %collective-permute-start.4 = (bf16[2,512,256]{1,2,0:T(8,128)(2,1)S(1)}, bf16[2,512,256]{1,2,0:T(8,128)(2,1)S(1)}, u32[]{:S(2)}, u32[]{:S(2)}) collective-permute-start(bf16[2,512,256]{1,2,0:T(8,128)(2,1)S(1)} %select_convert_fusion), channel_id=1, source_target_pairs={{0,1},{1,0},{2,3},{3,2},{4,5},{5,4},{6,7},{7,6},{8,9},{9,8},{10,11... | collective-permute-start | bytes 1572872 | tf_op jit(solution)/shard_map/ppermute | solution.py:156
  79.1 16.3 %collective-permute-start.5 = (bf16[512,256]{0,1:T(8,128)(2,1)}, bf16[512,256]{0,1:T(8,128)(2,1)S(1)}, u32[]{:S(2)}, u32[]{:S(2)}) collective-permute-start(bf16[512,256]{0,1:T(8,128)(2,1)} %get-tuple-element.122), channel_id=1, source_target_pairs={{8,0},{16,8},{24,16},{32,24},{40,32},{48,40},{56,48},{64,56},{72,6... | collective-permute-start | bytes 786440 | tf_op jit(solution)/shard_map/ppermute | solution.py:20
  81.4 14.0 %collective-permute-start.6 = (bf16[512,256]{0,1:T(8,128)(2,1)}, bf16[512,256]{0,1:T(8,128)(2,1)}, u32[]{:S(2)}, u32[]{:S(2)}) collective-permute-start(bf16[512,256]{0,1:T(8,128)(2,1)} %get-tuple-element.123), channel_id=1, source_target_pairs={{16,0},{24,8},{32,16},{40,24},{48,32},{56,40},{64,48},{72,56},{80,... | collective-permute-start | bytes 786440 | tf_op jit(solution)/shard_map/ppermute | solution.py:20
  88.9 20.5 %all-to-all-start.2 = ((bf16[8,128,512]{2,1,0:T(8,128)(2,1)}), bf16[8,128,512]{2,1,0:T(8,128)(2,1)}, u32[]{:S(2)}, u32[]{:S(2)}) async-start(bf16[8,128,512]{2,1,0:T(8,128)(2,1)} %bitcast.258), calls=%async_computation.2 | async-start | bytes 2097152 | tf_op jit(solution)/shard_map/all_to_all | solution.py:164
  109.4 13.8 %all-to-all-start.3 = ((bf16[8,128,256]{1,2,0:T(8,128)(2,1)}), bf16[8,128,256]{1,2,0:T(8,128)(2,1)S(1)}, u32[]{:S(2)}, u32[]{:S(2)}) async-start(bf16[8,128,256]{1,2,0:T(8,128)(2,1)} %pad_maximum_fusion.6), calls=%async_computation.3 | async-start | bytes 1048576 | tf_op jit(solution)/shard_map/all_to_all | solution.py:176
  (1 other events, 1.1 us)

commit v13 on v9

--- a/solution.py
+++ b/solution.py
@@ -53,7 +53,7 @@
     attn_block = jnp.einsum(
         "hqk,kd->qhd", probs_bf, v_win, preferred_element_type=jnp.float32
     ).astype(jnp.bfloat16)
-    row_delta = jnp.transpose(jnp.sum(lifted(g_block) * lifted(attn_block), axis=-1), (1, 0))
+    row_delta = jnp.transpose(jnp.sum(g_block.astype(jnp.float32) * lifted(attn_block), axis=-1), (1, 0))
     dprobs = jnp.einsum("qhd,kd->hqk", g_block, v_win, preferred_element_type=jnp.float32)
     dscores = (weights * (dprobs - row_delta[..., None])).astype(jnp.bfloat16)
     dq_block = (

time: 125 us -> 127 us (1.016)
  waiting for transfers between devices: 30.6 us -> 32.3 us
    all_to_all x1, waiting for transfers between devices: 1.08 us -> 2.91 us  [local(): lax.all_to_all(kv_send, 'sp', split_axis=0, concat_axis=0, tiled=True)]
    unnamed x35 -> x17, local copies, waits for them, and re-layouts: 4.42 us -> 5.89 us
  transfers between devices with their start and end apart: 11 -> 11, of which waited for: 7 -> 7; matrix products, arithmetic and copies ran while one was open for 22% -> 20% of each run, Pallas kernels for 0% -> 0%
where the time goes in v13:
time: 127 us; the launch traced here: 126 us
  starting transfers between devices  36 us (28%)
  waiting for transfers between devices  32.3 us (25%)
  matrix products  21.2 us (17%)
  other arithmetic  18.7 us (15%)
  local copies, waits for them, and re-layouts  16.5 us (13%)
    ppermute x4, starting transfers between devices, passed_along(): lax.ppermute(value, axis, [(source, source + steps) for source in range(f...  13.8 us
    all_to_all x1, waiting for transfers between devices, local(): lax.all_to_all(outgoing, 'sp', split_axis=0, concat_axis=1, tiled=True)  12.1 us
    ppermute x4, waiting for transfers between devices, passed_along(): lax.ppermute(value, axis, [(source, source + steps) for source in range(f...  10.6 us
    all_to_all x1, waiting for transfers between devices, local(): lax.all_to_all(kv_sum.astype(jnp.bfloat16), 'sp', split_axis=0, concat_ax...  6.53 us
    and x2, other arithmetic, local(): (q_label[:, None] == k_label[None, :]) & (k_place[None, :] <= q_place[:,...  6.27 us
    unnamed x17, local copies, waits for them, and re-layouts  5.89 us
    all_to_all x1, starting transfers between devices, local(): lax.all_to_all(outgoing, 'sp', split_axis=0, concat_axis=1, tiled=True)  4.47 us
    all_to_all x1, starting transfers between devices, local(): lax.all_to_all(kv_send, 'sp', split_axis=0, concat_axis=0, tiled=True)  4.47 us
  transfers between devices with their start and end apart: 11, of which 7 were waited for; matrix products, arithmetic and copies ran while one was open for 20% of the time, Pallas kernels for 0%

profile of v13, /device:TPU:384, one launch (start us, length us, event | category | flops | bytes accessed | tf_op | source)
XLA Modules:
  0.0 125.9 jit_solution(3178982819724135194)
XLA Ops:
  3.5 4.5 %all-to-all-start = ((bf16[8,64,256]{2,1,0:T(8,128)(2,1)}), bf16[8,64,256]{2,1,0:T(8,128)(2,1)S(1)}, u32[]{:S(2)}, u32[]{:S(2)}) async-start(bf16[8,64,256]{2,1,0:T(8,128)(2,1)} %bitcast.1), calls=%async_computation | async-start | bytes 524288 | tf_op jit(solution)/shard_map/all_to_all | solution.py:86
  9.0 1.9 %convert_reduce_fusion = s32[3072]{0:T(1024)S(1)} fusion(s32[128]{0:T(128)S(1)} %multiply_reduce_fusion.4, s32[3072]{0:T(1024)S(1)} %iota_add_fusion), kind=kLoop, calls=%fused_computation.73 | loop fusion | flops 1176576 | bytes 25088 | tf_op jit(solution)/shard_map/reduce_sum | solution.py:30
  12.6 2.9 %all-to-all-done = bf16[8,64,256]{2,1,0:T(8,128)(2,1)S(1)} async-done(((bf16[8,64,256]{2,1,0:T(8,128)(2,1)}), bf16[8,64,256]{2,1,0:T(8,128)(2,1)S(1)}, u32[]{:S(2)}, u32[]{:S(2)}) %all-to-all-start) | async-done | bytes 262176 | tf_op jit(solution)/shard_map/all_to_all | solution.py:86
  15.5 3.6 %all-to-all-start.1 = ((bf16[128,8,512]{0,2,1:T(8,128)(2,1)}), bf16[128,8,512]{0,2,1:T(8,128)(2,1)S(1)}, u32[]{:S(2)}, u32[]{:S(2)}) async-start(bf16[128,8,512]{0,2,1:T(8,128)(2,1)} %pad_maximum_fusion.1), calls=%async_computation.1 | async-start | bytes 2097152 | tf_op jit(solution)/shard_map/all_to_all | solution.py:101
  19.1 5.0 %collective-permute-start = (bf16[8,64,256]{2,1,0:T(8,128)(2,1)S(1)}, bf16[8,64,256]{2,1,0:T(8,128)(2,1)S(1)}, u32[]{:S(2)}, u32[]{:S(2)}) collective-permute-start(bf16[8,64,256]{2,1,0:T(8,128)(2,1)S(1)} %all-to-all-done), channel_id=1, source_target_pairs={{0,16},{8,24},{16,32},{24,40},{32,48},{40,56},{48,64},{56,72},{64,... | collective-permute-start | bytes 786440 | tf_op jit(solution)/shard_map/ppermute | solution.py:20
  24.0 2.5 %collective-permute-start.1 = (bf16[8,64,256]{2,1,0:T(8,128)(2,1)S(1)}, bf16[8,64,256]{2,1,0:T(8,128)(2,1)S(1)}, u32[]{:S(2)}, u32[]{:S(2)}) collective-permute-start(bf16[8,64,256]{2,1,0:T(8,128)(2,1)S(1)} %all-to-all-done), channel_id=1, source_target_pairs={{0,8},{8,16},{16,24},{24,32},{32,40},{40,48},{48,56},{56,64},{64,7... | collective-permute-start | bytes 786440 | tf_op jit(solution)/shard_map/ppermute | solution.py:20
  26.6 2.2 %compare_and_fusion.2 = (pred[256,2304]{0,1:T(8,128)(4,1)S(1)}, pred[256,2304]{0,1:T(8,128)(4,1)S(1)}) fusion(s32[256]{0:T(256)S(1)} %get-tuple-element.145, s32[256]{0:T(256)S(1)} %get-tuple-element.142, s32[2304]{0:T(1024)S(1)} %get-tuple-element.138, s32[2304]{0:T(1024)S(1)} %get-tuple-element.134, s32[256]{0:T(256)S(1)} %get-tuple-element.146, ...), kind=kLoop, calls=%fused_computation.70 | loop fusion | flops 3538944 | bytes 1220608 | tf_op jit(solution)/shard_map/and | solution.py:131
  28.8 1.9 %collective-permute-start.3 = (bf16[8,64,256]{2,1,0:T(8,128)(2,1)S(1)}, bf16[8,64,256]{2,1,0:T(8,128)(2,1)S(1)}, u32[]{:S(2)}, u32[]{:S(2)}) collective-permute-start(bf16[8,64,256]{2,1,0:T(8,128)(2,1)S(1)} %all-to-all-done), channel_id=1, source_target_pairs={{0,1},{1,0},{2,3},{3,2},{4,5},{5,4},{6,7},{7,6},{8,9},{9,8},{10,11... | collective-permute-start | bytes 786440 | tf_op jit(solution)/shard_map/ppermute | solution.py:109
  30.7 2.6 %collective-permute-done = bf16[8,64,256]{2,1,0:T(8,128)(2,1)S(1)} collective-permute-done((bf16[8,64,256]{2,1,0:T(8,128)(2,1)S(1)}, bf16[8,64,256]{2,1,0:T(8,128)(2,1)S(1)}, u32[]{:S(2)}, u32[]{:S(2)}) %collective-permute-start) | collective-permute-done | bytes 262176 | tf_op jit(solution)/shard_map/ppermute | solution.py:20
  33.3 6.1 %collective-permute-done.1 = bf16[8,64,256]{2,1,0:T(8,128)(2,1)S(1)} collective-permute-done((bf16[8,64,256]{2,1,0:T(8,128)(2,1)S(1)}, bf16[8,64,256]{2,1,0:T(8,128)(2,1)S(1)}, u32[]{:S(2)}, u32[]{:S(2)}) %collective-permute-start.1) | collective-permute-done | bytes 262176 | tf_op jit(solution)/shard_map/ppermute | solution.py:20
  40.3 1.9 %collective-permute-start.2 = (bf16[2,8,64,256]{3,2,1,0:T(8,128)(2,1)}, bf16[2,8,64,256]{3,2,1,0:T(8,128)(2,1)}, u32[]{:S(2)}, u32[]{:S(2)}) collective-permute-start(bf16[2,8,64,256]{3,2,1,0:T(8,128)(2,1)} %pad_maximum_fusion.5), channel_id=1, source_target_pairs={{0,1},{1,0},{2,3},{3,2},{4,5},{5,4},{6,7},{7,6},{8,9},{9,8},{10,11... | collective-permute-start | bytes 1572872 | tf_op jit(solution)/shard_map/ppermute | solution.py:110
  42.2 4.0 %compare_and_fusion = (pred[256,2304]{0,1:T(8,128)(4,1)}, pred[256,2304]{0,1:T(8,128)(4,1)}) fusion(s32[256]{0:T(256)S(1)} %get-tuple-element.147, s32[256]{0:T(256)S(1)} %get-tuple-element.141, s32[2304]{0:T(1024)S(1)} %get-tuple-element.137, s32[2304]{0:T(1024)S(1)} %get-tuple-element.133, s32[256]{0:T(256)S(1)} %get-tuple-element.144, ...), kind=kLoop, calls=%fused_computation.68 | loop fusion | flops 3538944 | bytes 1220608 | tf_op jit(solution)/shard_map/and | solution.py:131
  64.5 1.1 fusion.31
  74.2 2.4 %collective-permute-start.4 = (f32[2,512,256]{1,2,0:T(8,128)S(1)}, f32[2,512,256]{1,2,0:T(8,128)S(1)}, u32[]{:S(2)}, u32[]{:S(2)}) collective-permute-start(f32[2,512,256]{1,2,0:T(8,128)S(1)} %fusion.41), channel_id=1, source_target_pairs={{0,1},{1,0},{2,3},{3,2},{4,5},{5,4},{6,7},{7,6},{8,9},{9,8},{10,11... | collective-permute-start | bytes 3145736 | tf_op jit(solution)/shard_map/ppermute | solution.py:156
  80.1 2.3 %collective-permute-start.5 = (bf16[512,256]{0,1:T(8,128)(2,1)}, bf16[512,256]{0,1:T(8,128)(2,1)S(1)}, u32[]{:S(2)}, u32[]{:S(2)}) collective-permute-start(bf16[512,256]{0,1:T(8,128)(2,1)} %get-tuple-element.126), channel_id=1, source_target_pairs={{8,0},{16,8},{24,16},{32,24},{40,32},{48,40},{56,48},{64,56},{72,6... | collective-permute-start | bytes 786440 | tf_op jit(solution)/shard_map/ppermute | solution.py:20
  82.4 4.1 %collective-permute-start.6 = (bf16[512,256]{0,1:T(8,128)(2,1)}, bf16[512,256]{0,1:T(8,128)(2,1)}, u32[]{:S(2)}, u32[]{:S(2)}) collective-permute-start(bf16[512,256]{0,1:T(8,128)(2,1)} %get-tuple-element.127), channel_id=1, source_target_pairs={{16,0},{24,8},{32,16},{40,24},{48,32},{56,40},{64,48},{72,56},{80,... | collective-permute-start | bytes 786440 | tf_op jit(solution)/shard_map/ppermute | solution.py:20
  86.5 1.2 maximum_maximum_fusion
  87.7 2.3 %copy.215 = bf16[1024,512]{1,0:T(8,128)(2,1)} copy(bf16[1024,512]{0,1:T(8,128)(2,1)} %maximum_maximum_fusion) | data formatting | bytes 2097152 | tf_op jit(solution)/shard_map/concatenate | solution.py:163
  90.0 4.5 %all-to-all-start.2 = ((bf16[8,128,512]{2,1,0:T(8,128)(2,1)}), bf16[8,128,512]{2,1,0:T(8,128)(2,1)}, u32[]{:S(2)}, u32[]{:S(2)}) async-start(bf16[8,128,512]{2,1,0:T(8,128)(2,1)} %bitcast.264), calls=%async_computation.2 | async-start | bytes 2097152 | tf_op jit(solution)/shard_map/all_to_all | solution.py:164
  94.6 1.9 %collective-permute-done.5 = bf16[512,256]{0,1:T(8,128)(2,1)S(1)} collective-permute-done((bf16[512,256]{0,1:T(8,128)(2,1)}, bf16[512,256]{0,1:T(8,128)(2,1)S(1)}, u32[]{:S(2)}, u32[]{:S(2)}) %collective-permute-start.5) | collective-permute-done | bytes 262176 | tf_op jit(solution)/shard_map/ppermute | solution.py:20
  98.5 12.1 %all-to-all-done.2 = bf16[8,128,512]{2,1,0:T(8,128)(2,1)} async-done(((bf16[8,128,512]{2,1,0:T(8,128)(2,1)}), bf16[8,128,512]{2,1,0:T(8,128)(2,1)}, u32[]{:S(2)}, u32[]{:S(2)}) %all-to-all-start.2) | async-done | bytes 1048608 | tf_op jit(solution)/shard_map/all_to_all | solution.py:164
  110.5 3.5 %all-to-all-start.3 = ((bf16[8,128,256]{1,2,0:T(8,128)(2,1)}), bf16[8,128,256]{1,2,0:T(8,128)(2,1)S(1)}, u32[]{:S(2)}, u32[]{:S(2)}) async-start(bf16[8,128,256]{1,2,0:T(8,128)(2,1)} %pad_maximum_fusion.6), calls=%async_computation.3 | async-start | bytes 1048576 | tf_op jit(solution)/shard_map/all_to_all | solution.py:176
  114.0 1.6 %copy.216 = bf16[8,128,512]{1,2,0:T(8,128)(2,1)S(1)} copy(bf16[8,128,512]{2,1,0:T(8,128)(2,1)} %all-to-all-done.2) | data formatting | bytes 2097152 | tf_op jit(solution)/shard_map/all_to_all | solution.py:164
  117.8 6.5 %all-to-all-done.3 = bf16[8,128,256]{1,2,0:T(8,128)(2,1)S(1)} async-done(((bf16[8,128,256]{1,2,0:T(8,128)(2,1)}), bf16[8,128,256]{1,2,0:T(8,128)(2,1)S(1)}, u32[]{:S(2)}, u32[]{:S(2)}) %all-to-all-start.3) | async-done | bytes 524320 | tf_op jit(solution)/shard_map/all_to_all | solution.py:176
  (91 shorter events, 42.2 us)
Async XLA Ops:
  0.6 10.3 %copy-start.2 = (bf16[128,2048]{1,0:T(8,128)(2,1)S(1)}, bf16[128,2048]{1,0:T(8,128)(2,1)}, u32[]{:S(2)}) copy-start(bf16[128,2048]{1,0:T(8,128)(2,1)} %param.21) | copy-start | bytes 1572868
  0.6 10.6 %copy-start.3 = (bf16[128,2048]{1,0:T(8,128)(2,1)S(1)}, bf16[128,2048]{1,0:T(8,128)(2,1)}, u32[]{:S(2)}) copy-start(bf16[128,2048]{1,0:T(8,128)(2,1)} %param.24) | copy-start | bytes 1572868
  3.5 12.0 %all-to-all-start = ((bf16[8,64,256]{2,1,0:T(8,128)(2,1)}), bf16[8,64,256]{2,1,0:T(8,128)(2,1)S(1)}, u32[]{:S(2)}, u32[]{:S(2)}) async-start(bf16[8,64,256]{2,1,0:T(8,128)(2,1)} %bitcast.1), calls=%async_computation | async-start | bytes 524288 | tf_op jit(solution)/shard_map/all_to_all | solution.py:86
  15.5 32.6 %all-to-all-start.1 = ((bf16[128,8,512]{0,2,1:T(8,128)(2,1)}), bf16[128,8,512]{0,2,1:T(8,128)(2,1)S(1)}, u32[]{:S(2)}, u32[]{:S(2)}) async-start(bf16[128,8,512]{0,2,1:T(8,128)(2,1)} %pad_maximum_fusion.1), calls=%async_computation.1 | async-start | bytes 2097152 | tf_op jit(solution)/shard_map/all_to_all | solution.py:101
  19.1 14.2 %collective-permute-start = (bf16[8,64,256]{2,1,0:T(8,128)(2,1)S(1)}, bf16[8,64,256]{2,1,0:T(8,128)(2,1)S(1)}, u32[]{:S(2)}, u32[]{:S(2)}) collective-permute-start(bf16[8,64,256]{2,1,0:T(8,128)(2,1)S(1)} %all-to-all-done), channel_id=1, source_target_pairs={{0,16},{8,24},{16,32},{24,40},{32,48},{40,56},{48,64},{56,72},{64,... | collective-permute-start | bytes 786440 | tf_op jit(solution)/shard_map/ppermute | solution.py:20
  24.0 15.4 %collective-permute-start.1 = (bf16[8,64,256]{2,1,0:T(8,128)(2,1)S(1)}, bf16[8,64,256]{2,1,0:T(8,128)(2,1)S(1)}, u32[]{:S(2)}, u32[]{:S(2)}) collective-permute-start(bf16[8,64,256]{2,1,0:T(8,128)(2,1)S(1)} %all-to-all-done), channel_id=1, source_target_pairs={{0,8},{8,16},{16,24},{24,32},{32,40},{40,48},{48,56},{56,64},{64,7... | collective-permute-start | bytes 786440 | tf_op jit(solution)/shard_map/ppermute | solution.py:20
  28.8 17.4 %collective-permute-start.3 = (bf16[8,64,256]{2,1,0:T(8,128)(2,1)S(1)}, bf16[8,64,256]{2,1,0:T(8,128)(2,1)S(1)}, u32[]{:S(2)}, u32[]{:S(2)}) collective-permute-start(bf16[8,64,256]{2,1,0:T(8,128)(2,1)S(1)} %all-to-all-done), channel_id=1, source_target_pairs={{0,1},{1,0},{2,3},{3,2},{4,5},{5,4},{6,7},{7,6},{8,9},{9,8},{10,11... | collective-permute-start | bytes 786440 | tf_op jit(solution)/shard_map/ppermute | solution.py:109
  40.3 8.8 %collective-permute-start.2 = (bf16[2,8,64,256]{3,2,1,0:T(8,128)(2,1)}, bf16[2,8,64,256]{3,2,1,0:T(8,128)(2,1)}, u32[]{:S(2)}, u32[]{:S(2)}) collective-permute-start(bf16[2,8,64,256]{3,2,1,0:T(8,128)(2,1)} %pad_maximum_fusion.5), channel_id=1, source_target_pairs={{0,1},{1,0},{2,3},{3,2},{4,5},{5,4},{6,7},{7,6},{8,9},{9,8},{10,11... | collective-permute-start | bytes 1572872 | tf_op jit(solution)/shard_map/ppermute | solution.py:110
  46.2 0.7 copy-start.4
  54.7 1.1 copy-start.1
  56.6 1.1 copy-start
  74.2 4.7 %collective-permute-start.4 = (f32[2,512,256]{1,2,0:T(8,128)S(1)}, f32[2,512,256]{1,2,0:T(8,128)S(1)}, u32[]{:S(2)}, u32[]{:S(2)}) collective-permute-start(f32[2,512,256]{1,2,0:T(8,128)S(1)} %fusion.41), channel_id=1, source_target_pairs={{0,1},{1,0},{2,3},{3,2},{4,5},{5,4},{6,7},{7,6},{8,9},{9,8},{10,11... | collective-permute-start | bytes 3145736 | tf_op jit(solution)/shard_map/ppermute | solution.py:156
  80.1 16.3 %collective-permute-start.5 = (bf16[512,256]{0,1:T(8,128)(2,1)}, bf16[512,256]{0,1:T(8,128)(2,1)S(1)}, u32[]{:S(2)}, u32[]{:S(2)}) collective-permute-start(bf16[512,256]{0,1:T(8,128)(2,1)} %get-tuple-element.126), channel_id=1, source_target_pairs={{8,0},{16,8},{24,16},{32,24},{40,32},{48,40},{56,48},{64,56},{72,6... | collective-permute-start | bytes 786440 | tf_op jit(solution)/shard_map/ppermute | solution.py:20
  82.4 14.0 %collective-permute-start.6 = (bf16[512,256]{0,1:T(8,128)(2,1)}, bf16[512,256]{0,1:T(8,128)(2,1)}, u32[]{:S(2)}, u32[]{:S(2)}) collective-permute-start(bf16[512,256]{0,1:T(8,128)(2,1)} %get-tuple-element.127), channel_id=1, source_target_pairs={{16,0},{24,8},{32,16},{40,24},{48,32},{56,40},{64,48},{72,56},{80,... | collective-permute-start | bytes 786440 | tf_op jit(solution)/shard_map/ppermute | solution.py:20
  90.0 20.5 %all-to-all-start.2 = ((bf16[8,128,512]{2,1,0:T(8,128)(2,1)}), bf16[8,128,512]{2,1,0:T(8,128)(2,1)}, u32[]{:S(2)}, u32[]{:S(2)}) async-start(bf16[8,128,512]{2,1,0:T(8,128)(2,1)} %bitcast.264), calls=%async_computation.2 | async-start | bytes 2097152 | tf_op jit(solution)/shard_map/all_to_all | solution.py:164
  110.5 13.8 %all-to-all-start.3 = ((bf16[8,128,256]{1,2,0:T(8,128)(2,1)}), bf16[8,128,256]{1,2,0:T(8,128)(2,1)S(1)}, u32[]{:S(2)}, u32[]{:S(2)}) async-start(bf16[8,128,256]{1,2,0:T(8,128)(2,1)} %pad_maximum_fusion.6), calls=%async_computation.3 | async-start | bytes 1048576 | tf_op jit(solution)/shard_map/all_to_all | solution.py:176
